TPU v7x, 128 devices: a whole 4x4x4 slice. The times are simulated.
128 devices in a mesh: sec: 2 (over core), tile: 64 (over y, x, z).
Axes of the slice: x: 4, y: 4, z: 4, core: 2. Of those that a mesh axis runs over, the one named last changes fastest.
Arguments:
- land_wind: float32 [16384, 128], P(('sec', 'tile')), may hold values from 0.15 to 0.9
- land_moist: float32 [16384, 128], P(('sec', 'tile')), may hold values from 0 to 0.3
- texture: int32 [16384, 128], P(('sec', 'tile')), may hold values from 0 to 3
- land_index: int32 [16384, 128], P(('sec', 'tile')), may hold values from 0 to 32767
- erod_map: float32 [4194304], P(('sec', 'tile')), may hold values from 0.2 to 1
- mass_frac: float32 [4, 12], replicated, may hold values from 0.02 to 0.3
- blast_table: float32 [4, 8, 12], replicated, may hold values from 0.05 to 1
- dest_tile: int32 [16384, 1], P(('sec', 'tile')), may hold values from 0 to 127; in each aligned block of 128 rows (0 to 127, 128 to 255, ...) at most 2 rows name the same one
- regrid_w: bfloat16 [16384, 128, 256], P(('sec', 'tile')), may hold values from 0 to 0.25, as said below
- atm_state: float32 [3, 16, 32768], P(None, None, ('sec', 'tile')), may hold values from -5 to 5
- dust_mix: float32 [8, 16, 32768], P(None, None, ('sec', 'tile')), may hold values from 0 to 1
- mixing: float32 [15, 32768], P(None, ('sec', 'tile')), may hold values from 0.1 to 10
- settle: float32 [8], replicated, may hold values from 0.05 to 0.5
Outputs:
- land_fields: float32 [2, 16384, 128], P(None, ('sec', 'tile'))
- dust_out: float32 [8, 16, 32768], P(None, None, ('sec', 'tile'))
Inputs may be any that keep to these rules, and one draw needn't show every extreme that they name: `land_index`: each land cell's index points into its own device's 32768 cells of erod_map. `dest_tile`: among the 128 blocks of one device at most 2 name the same tile, a bound that some block reaches. `regrid_w`: each land cell has 1 to 4 positive weights, of 0.05 or more, on adjacent columns of its tile, and 0 elsewhere.
All inputs are finite; a program needn't handle non-finite values.
Results may differ from a plain program's by a relative error of at most 0.0023.
Values may be sent and summed in bfloat16 or wider, within the bound.
No kernel may reach another device: no remote copies, remote signals or barrier semaphores. Data moves between devices by JAX's collectives and lax.ppermute only.
A program may use at most 64 MiB of HBM per device.

v0:
```python
import jax
import jax.numpy as jnp
from jax import lax
from jax.sharding import PartitionSpec as P


def threshold_table(count):
    diameter = 4e-05 * jnp.power(jnp.float32(1.35), jnp.arange(count).astype(jnp.float32))
    return jnp.sqrt(0.0123 * (2160.0 * 9.81 * diameter + 0.0003 / (1.227 * diameter)))


def emit(wind_rows, moist_rows, texture_rows, erodible, mass_frac, blast_table, base_thresh):
    high = lax.Precision.HIGHEST
    thresh = base_thresh[:, None, None] * jnp.sqrt(1.0 + 12.1 * moist_rows)[None]
    classes = jnp.arange(mass_frac.shape[0])
    onehot = (texture_rows[None] == classes[:, None, None]).astype(jnp.float32)
    fraction = jnp.einsum("tb,tnl->bnl", mass_frac, onehot, precision=high)
    speed = wind_rows[None]
    salt = (
        40.0
        * fraction
        * erodible[None]
        * (speed + thresh)
        * jnp.maximum(speed * speed - thresh * thresh, 0.0)
    )
    blasted = jnp.einsum("tkb,bnl->tknl", blast_table, salt, precision=high)
    emission = jnp.sum(blasted * onehot[:, None], axis=0)
    return jnp.transpose(emission, (1, 0, 2)).astype(jnp.bfloat16)


def lookup(table, index):
    rows = table.shape[0] // 128
    flat = index.reshape(-1)
    high_part = flat // 128
    low_part = flat % 128
    pick_row = (lax.broadcasted_iota(jnp.int32, (rows, flat.shape[0]), 0) == high_part[None, :]).astype(jnp.bfloat16)
    grid = table.reshape(rows, 128)
    first_wide = lax.reduce_precision(grid, exponent_bits=8, mantissa_bits=7)
    rest = grid - first_wide
    second_wide = lax.reduce_precision(rest, exponent_bits=8, mantissa_bits=7)
    first = first_wide.astype(jnp.bfloat16)
    second = second_wide.astype(jnp.bfloat16)
    third = (rest - second_wide).astype(jnp.bfloat16)
    dims = (((0,), (0,)), ((), ()))
    parts = [lax.dot_general(p, pick_row, dims, preferred_element_type=jnp.float32) for p in (first, second, third)]
    row_values = (parts[0] + parts[1]) + parts[2]
    pick_lane = lax.broadcasted_iota(jnp.int32, row_values.shape, 0) == low_part[None, :]
    return jnp.sum(jnp.where(pick_lane, row_values, 0.0), axis=0).reshape(index.shape)


def solve(right_side, coupling, sinking):
    levels = right_side.shape[1]
    sink_col = sinking[:, None]
    zero_row = jnp.zeros_like(coupling[0])
    ratios = []
    partial_value = []
    ratio_prev = None
    part_prev = None
    for level in range(levels):
        lower_c = coupling[level - 1] if level > 0 else zero_row
        upper_c = coupling[level] if level < levels - 1 else zero_row
        diagonal = 1.0 + lower_c[None] + upper_c[None] + sink_col
        if level == 0:
            pivot = diagonal
            part_now = right_side[:, level] / pivot
        else:
            pivot = diagonal + lower_c[None] * ratio_prev
            part_now = (right_side[:, level] + lower_c[None] * part_prev) / pivot
        if level < levels - 1:
            ratio_now = -(upper_c[None] + sink_col) / pivot
        else:
            ratio_now = jnp.zeros_like(pivot)
        ratios.append(ratio_now)
        partial_value.append(part_now)
        ratio_prev = ratio_now
        part_prev = part_now
    result = [None] * levels
    result[levels - 1] = partial_value[levels - 1]
    for level in range(levels - 2, -1, -1):
        result[level] = partial_value[level] - ratios[level] * result[level + 1]
    return jnp.stack(result, axis=1)


def on_device(
    land_wind,
    land_moist,
    texture,
    land_index,
    erod_map,
    mass_frac,
    blast_table,
    dest_tile,
    regrid_w,
    atm_state,
    dust_mix,
    mixing,
    settle,
):
    high = lax.Precision.HIGHEST
    nblocks, ncells = land_wind.shape
    columns = atm_state.shape[2]
    nbins = blast_table.shape[1]
    devices = lax.axis_size(("sec", "tile"))
    state = solve(atm_state, mixing, jnp.zeros((3,), jnp.float32))
    speed = jnp.sqrt(state[0, 0] ** 2 + state[1, 0] ** 2 + 0.25)
    surface = jnp.stack([speed, state[2, 0]]).astype(jnp.bfloat16).reshape(1, 2 * columns)
    spread = jnp.broadcast_to(surface, (devices, 2 * columns))
    gathered = lax.all_to_all(spread, ("sec", "tile"), split_axis=0, concat_axis=0, tiled=True)
    base_thresh = threshold_table(mass_frac.shape[1])
    erodible = lookup(erod_map, land_index)
    emission = emit(land_wind, land_moist, texture, erodible, mass_frac, blast_table, base_thresh)
    partial_flux = jnp.einsum(
        "gkl,gla->gka", emission, regrid_w, preferred_element_type=jnp.float32
    )
    flat_flux = partial_flux.reshape(nblocks, nbins * columns)
    targets = dest_tile[:, 0]
    onehot = (targets[:, None] == jnp.arange(devices)[None, :]).astype(jnp.float32)
    dims = (((0,), (0,)), ((), ()))
    outgoing = lax.dot_general(onehot, flat_flux, dims, precision=high)
    incoming = lax.all_to_all(
        outgoing.astype(jnp.bfloat16), ("sec", "tile"), split_axis=0, concat_axis=0, tiled=True
    )
    flux = jnp.sum(incoming.astype(jnp.float32), axis=0).reshape(nbins, columns)
    flux = flux * (float(columns) / float(ncells * nblocks))
    loaded = dust_mix.at[:, 0, :].add(flux)
    dust_out = solve(loaded, mixing, settle)
    picked = jnp.dot(onehot.astype(jnp.bfloat16), gathered, preferred_element_type=jnp.float32)
    picked = picked.astype(jnp.bfloat16).reshape(nblocks, 2, columns)
    picked = jnp.concatenate([picked, jnp.ones((nblocks, 1, columns), jnp.bfloat16)], axis=1)
    numer = jnp.einsum("gla,gka->kgl", regrid_w, picked, preferred_element_type=jnp.float32)
    denom = numer[2]
    land_fields = jnp.stack([numer[0] / denom, 0.5 * land_moist + 0.5 * numer[1] / denom])
    return (land_fields, dust_out)


def solution(mesh):
    in_specs = (
        P(("sec", "tile"), None),
        P(("sec", "tile"), None),
        P(("sec", "tile"), None),
        P(("sec", "tile"), None),
        P(("sec", "tile")),
        P(),
        P(),
        P(("sec", "tile"), None),
        P(("sec", "tile"), None, None),
        P(None, None, ("sec", "tile")),
        P(None, None, ("sec", "tile")),
        P(None, ("sec", "tile")),
        P(),
    )
    out_specs = (P(None, ("sec", "tile"), None), P(None, None, ("sec", "tile")))
    return jax.shard_map(
        on_device, mesh=mesh, in_specs=in_specs, out_specs=out_specs, check_vma=False
    )
```

profile of v0, /device:TPU:1, one launch (start us, length us, event | category | flops | bytes accessed | tf_op | source)
XLA Modules:
  0.0 77.2 jit_solution(8018444946558179971)
XLA Ops:
  0.7 1.0 %fusion.87 = (f32[1,256]{1,0:T(1,128)S(1)}, f32[1,256]{1,0:T(1,128)S(1)}, f32[1,256]{1,0:T(1,128)S(1)}, f32[1,256]{1,0:T(1,128)S(1)}, f32[1,256]{1,0:T(1,128)S(1...) fusion(f32[15,256]{1,0:T(8,128)} %param.26), kind=kLoop, calls=%fused_computation.259 | loop fusion | flops 2816 | bytes 24576 | tf_op jit(solution)/shard_map/slice | solution.py:61
  1.6 1.0 %broadcast_add_fusion.1 = (f32[1,256]{1,0:T(1,128)S(1)}, f32[1,256]{1,0:T(1,128)S(1)}, f32[1,256]{1,0:T(1,128)S(1)}, f32[1,256]{1,0:T(1,128)S(1)}, f32[1,256]{1,...) fusion(f32[15,256]{1,0:T(8,128)} %param.26), kind=kLoop, calls=%fused_computation.253 | loop fusion | flops 4608 | bytes 20480 | tf_op jit(solution)/shard_map/add;add | solution.py:62
  2.6 0.9 %fusion.88 = (f32[1,256]{1,0:T(1,128)S(1)}, f32[1,256]{1,0:T(1,128)S(1)}, f32[1,256]{1,0:T(1,128)S(1)}, f32[1,256]{1,0:T(1,128)S(1)}, f32[1,256]{1,0:T(1,128)S(1...) fusion(f32[15,256]{1,0:T(8,128)} %param.26), kind=kLoop, calls=%fused_computation.260 | loop fusion | bytes 14336 | tf_op jit(solution)/shard_map/slice | solution.py:61
  3.5 1.2 %fusion.86 = (f32[3,1,256]{2,1,0:T(1,128)S(1)}, f32[3,1,256]{2,1,0:T(1,128)S(1)}, f32[3,1,256]{2,1,0:T(1,128)S(1)}, f32[3,1,256]{2,1,0:T(1,128)S(1)}, f32[3,1,25...) fusion(f32[3,16,256]{2,1,0:T(8,128)} %param.24), kind=kLoop, calls=%fused_computation.258 | loop fusion | bytes 98304 | tf_op jit(solution)/shard_map/slice | solution.py:65
  5.3 0.5 broadcast.18982
  5.8 1.4 %reduce.3 = bf16[128,512]{1,0:T(8,128)(2,1)S(1)} reduce(bf16[128,1,512]{2,1,0:T(2,128)(2,1)S(1)} %broadcast_in_dim.5, bf16[]{:T(256)} %broadcast.18982), dimensions={1}, to_apply=%broadcast_in_dim.5.reduce_sub_computation | reduce | bytes 262146 | tf_op jit(solution)/shard_map/broadcast_in_dim | solution.py:107
  7.2 0.7 reshape.27206
  7.9 11.5 %all-to-all-start = ((bf16[128,2,256]{2,1,0:T(2,128)(2,1)}), bf16[128,2,256]{2,1,0:T(2,128)(2,1)S(1)}, u32[]{:S(2)}, u32[]{:S(2)}) async-start(bf16[128,2,256]{2,1,0:T(2,128)(2,1)} %reshape.27206), calls=%async_computation | async-start | bytes 262144 | tf_op jit(solution)/shard_map/all_to_all | solution.py:108
  19.4 0.9 %add_select_fusion.1 = (s32[16384]{0:T(1024)S(1)}, s32[16384]{0:T(1024)S(1)}) fusion(s32[128,128]{1,0:T(8,128)} %param.18), kind=kLoop, calls=%fused_computation.43 | loop fusion | flops 311296 | bytes 196608 | tf_op jit(solution)/shard_map/jit(remainder)/select_n | solution.py:35
  20.3 4.4 %convolution_bitcast_fusion = f32[128,16384]{1,0:T(8,128)S(1)} fusion(s32[16384]{0:T(1024)S(1)} %get-tuple-element.81, f32[32768]{0:T(1024)} %param.19), kind=kOutput, calls=%fused_computation | convolution fusion | flops 1078001664 | bytes 8585216 | tf_op jit(solution)/shard_map/dot_general | solution.py:45
  24.7 4.0 %convolution_add_fusion.1 = f32[128,16384]{1,0:T(8,128)S(1)} fusion(f32[128,16384]{1,0:T(8,128)S(1)} %convolution_bitcast_fusion, s32[16384]{0:T(1024)S(1)} %get-tuple-element.81, f32[32768]{0:T(1024)S(1)} %copy-done.1), kind=kOutput, calls=%fused_computation.3 | convolution fusion | flops 1080164352 | bytes 16973824 | tf_op jit(solution)/shard_map/dot_general | solution.py:45
  28.9 5.2 %fusion.6 = f32[16384]{0:T(1024)S(1)} fusion(f32[128,16384]{1,0:T(8,128)S(1)} %convolution_add_fusion.1, s32[16384]{0:T(1024)S(1)} %get-tuple-element.81, s32[16384]{0:T(1024)S(1)} %get-tuple-element.80, f32[32768]{0:T(1024)S(1)} %copy-done.1), kind=kOutput, calls=%fused_computation.13 | convolution fusion | flops 1086472192 | bytes 8716288 | tf_op jit(solution)/shard_map/dot_general | solution.py:45
  34.6 5.6 %convolution_bitcast_fusion.1 = f32[3,128,128]{2,0,1:T(4,128)S(1)} fusion(bf16[128,128,256]{2,1,0:T(8,128)(2,1)} %param.23, bf16[128,2,256]{2,1,0:T(2,128)(2,1)S(1)} %reshape.27199), kind=kOutput, calls=%fused_computation.21 | convolution fusion | flops 25165824 | bytes 8716288 | tf_op jit(solution)/shard_map/gla,gka->kgl/dot_general | solution.py:130
  40.5 0.8 %fusion.10 = f32[12,128,128,1]{2,0,3,1:T(8,128)S(1)} fusion(f32[128,128]{1,0:T(8,128)S(1)} %mul.1955, f32[128,128]{1,0:T(8,128)S(1)} %get-tuple-element.82, f32[12]{0:T(128)S(1)} %multiply_sqrt_fusion, f32[128,128]{1,0:T(8,128)S(1)} %copy-done.2, f32[128,128]{1,0:T(8,128)S(1)} %multiply_bitcast_fusion, s32[128,128]{1,0:T(8,128)S(1)} %copy-done.4, ...), kind=kOutput, calls=%fused_computation.20 | convolution fusion | flops 11075584 | bytes 1114352 | tf_op jit(solution)/shard_map/tb,tnl->bnl/dot_general | solution.py:17
  41.3 1.8 %fusion.5 = bf16[8,128,128]{2,0,1:T(8,128)(2,1)S(1)} fusion(f32[12,128,128,1]{2,0,3,1:T(8,128)S(1)} %fusion.10, f32[4,128,128]{2,0,1:T(4,128)S(1)} %fusion.16, f32[4,8,12]{2,1,0:T(8,128)S(1)} %copy-done), kind=kOutput, calls=%fused_computation.12 | convolution fusion | flops 76414976 | bytes 1312256 | tf_op jit(solution)/shard_map/tkb,bnl->tknl/dot_general | solution.py:26
  43.1 4.6 %fusion.13 = f32[128,8,256]{2,1,0:T(8,128)S(1)} fusion(bf16[128,128,256]{2,1,0:T(8,128)(2,1)} %param.23, bf16[8,128,128]{2,0,1:T(8,128)(2,1)S(1)} %fusion.5), kind=kOutput, calls=%fused_computation.26 | convolution fusion | flops 67108864 | bytes 9699328 | tf_op jit(solution)/shard_map/gkl,gla->gka/dot_general | solution.py:112
  48.1 0.7 fusion.4
  48.8 1.0 %reduce.4 = bf16[128,2048]{1,0:T(8,128)(2,1)S(1)} reduce(bf16[128,1,2048]{2,0,1:T(8,128)(2,1)S(1)} %fusion.4, bf16[]{:T(256)} %broadcast.18982), dimensions={1}, to_apply=%copy.91.reduce_sub_computation | reduce | bytes 1048578 | tf_op jit(solution)/shard_map/all_to_all | solution.py:120
  49.8 1.2 %reshape.27208 = bf16[128,2,1024]{2,1,0:T(2,128)(2,1)} reshape(bf16[128,2048]{1,0:T(8,128)(2,1)S(1)} %reduce.4) | data formatting | bytes 1048576
  51.0 9.8 %all-to-all-start.1 = ((bf16[128,2,1024]{2,1,0:T(2,128)(2,1)}), bf16[128,2,1024]{2,1,0:T(2,128)(2,1)S(1)}, u32[]{:S(2)}, u32[]{:S(2)}) async-start(bf16[128,2,1024]{2,1,0:T(2,128)(2,1)} %reshape.27208), calls=%async_computation.1 | async-start | bytes 1048576 | tf_op jit(solution)/shard_map/all_to_all | solution.py:120
  60.9 0.7 pad_maximum_fusion
  61.6 12.2 %all-to-all-done.1 = bf16[128,2,1024]{2,1,0:T(2,128)(2,1)S(1)} async-done(((bf16[128,2,1024]{2,1,0:T(2,128)(2,1)}), bf16[128,2,1024]{2,1,0:T(2,128)(2,1)S(1)}, u32[]{:S(2)}, u32[]{:S(2)}) %all-to-all-start.1) | async-done | bytes 524320 | tf_op jit(solution)/shard_map/all_to_all | solution.py:120
  74.2 1.0 %convert_reduce_fusion = f32[2048]{0:T(1024)S(1)} fusion(bf16[128,1,2048]{2,1,0:T(2,128)(2,1)S(1)} %reshape.27209), kind=kLoop, calls=%fused_computation.25 | loop fusion | flops 522240 | bytes 532480 | tf_op jit(solution)/shard_map/reduce_sum | solution.py:123
  76.5 0.7 copy.107
  (58 shorter events, 3.2 us)
Async XLA Ops:
  0.6 40.7 %copy-start = (f32[4,8,12]{2,1,0:T(8,128)S(1)}, f32[4,8,12]{2,1,0:T(8,128)}, u32[]{:S(2)}) copy-start(f32[4,8,12]{2,1,0:T(8,128)} %param.21) | copy-start | bytes 4612
  0.6 24.1 %copy-start.1 = (f32[32768]{0:T(1024)S(1)}, f32[32768]{0:T(1024)}, u32[]{:S(2)}) copy-start(f32[32768]{0:T(1024)} %param.19) | copy-start | bytes 393220
  7.9 26.3 %all-to-all-start = ((bf16[128,2,256]{2,1,0:T(2,128)(2,1)}), bf16[128,2,256]{2,1,0:T(2,128)(2,1)S(1)}, u32[]{:S(2)}, u32[]{:S(2)}) async-start(bf16[128,2,256]{2,1,0:T(2,128)(2,1)} %reshape.27206), calls=%async_computation | async-start | bytes 262144 | tf_op jit(solution)/shard_map/all_to_all | solution.py:108
  24.7 4.1 %copy-start.4 = (s32[128,128]{1,0:T(8,128)S(1)}, s32[128,128]{1,0:T(8,128)}, u32[]{:S(2)}) copy-start(s32[128,128]{1,0:T(8,128)} %param.17) | copy-start | bytes 196612
  28.8 5.3 %copy-start.2 = (f32[128,128]{1,0:T(8,128)S(1)}, f32[128,128]{1,0:T(8,128)}, u32[]{:S(2)}) copy-start(f32[128,128]{1,0:T(8,128)} %param.15) | copy-start | bytes 196612
  28.8 5.5 %copy-start.7 = (s32[128,1]{0,1:T(1,128)S(1)}, s32[128,1]{0,1:T(1,128)}, u32[]{:S(2)}) copy-start(s32[128,1]{0,1:T(1,128)} %param.22) | copy-start | bytes 1540
  34.1 6.3 %copy-start.5 = (f32[128,128]{1,0:T(8,128)S(1)}, f32[128,128]{1,0:T(8,128)}, u32[]{:S(2)}) copy-start(f32[128,128]{1,0:T(8,128)} %param.16) | copy-start | bytes 196612
  34.1 6.3 %copy-start.8 = (f32[4,12]{1,0:T(4,128)S(1)}, f32[4,12]{1,0:T(4,128)}, u32[]{:S(2)}) copy-start(f32[4,12]{1,0:T(4,128)} %param.20) | copy-start | bytes 580
  43.1 17.6 %copy-start.3 = (f32[8,16,256]{2,1,0:T(8,128)S(1)}, f32[8,16,256]{2,1,0:T(8,128)}, u32[]{:S(2)}) copy-start(f32[8,16,256]{2,1,0:T(8,128)} %param.25) | copy-start | bytes 393220
  47.7 27.4 %copy-start.6 = (f32[8]{0:T(128)S(1)}, f32[8]{0:T(128)}, u32[]{:S(2)}) copy-start(f32[8]{0:T(128)} %param.27) | copy-start | bytes 100
  51.0 22.7 %all-to-all-start.1 = ((bf16[128,2,1024]{2,1,0:T(2,128)(2,1)}), bf16[128,2,1024]{2,1,0:T(2,128)(2,1)S(1)}, u32[]{:S(2)}, u32[]{:S(2)}) async-start(bf16[128,2,1024]{2,1,0:T(2,128)(2,1)} %reshape.27208), calls=%async_computation.1 | async-start | bytes 1048576 | tf_op jit(solution)/shard_map/all_to_all | solution.py:120
where the time goes:
time: 77.7 us; the launch traced here: 77.2 us
  matrix products  27.5 us (35%)
  starting transfers between devices  21.3 us (27%)
  waiting for transfers between devices  12.2 us (16%)
  other arithmetic  8.69 us (11%)
  local copies, waits for them, and re-layouts  6.45 us (8%)
  between operations  1.13 us (1%)
    dot_general x3, matrix products, lookup(): lax.dot_general(p, pick_row, dims, preferred_element_type=jnp.float32)  13.7 us
    all_to_all x1, waiting for transfers between devices, on_device(): lax.all_to_all(outgoing.astype(jnp.bfloat16), ('sec', 'tile'), split_axis...  12.2 us
    all_to_all x1, starting transfers between devices, on_device(): lax.all_to_all(spread, ('sec', 'tile'), split_axis=0, concat_axis=0, tile...  11.5 us
    all_to_all x1, starting transfers between devices, on_device(): lax.all_to_all(outgoing.astype(jnp.bfloat16), ('sec', 'tile'), split_axis...  9.76 us
    dot_general x1, matrix products, on_device(): jnp.einsum('gla,gka->kgl', regrid_w, picked, preferred_element_type=jnp.f...  5.63 us
    dot_general x1, matrix products, on_device(): jnp.einsum('gkl,gla->gka', emission, regrid_w, preferred_element_type=jnp...  4.61 us
    unnamed x32, local copies, waits for them, and re-layouts  3.53 us
    dot_general x1, matrix products, emit(): blasted = jnp.einsum('tkb,bnl->tknl', blast_table, salt, precision=high)  1.81 us
  transfers between devices with their start and end apart: 2, of which 1 were waited for; matrix products, arithmetic and copies ran while one was open for 20% of the time, Pallas kernels for 0%

commit v1 on v0

--- a/solution.py
+++ b/solution.py
@@ -104,8 +104,6 @@
     state = solve(atm_state, mixing, jnp.zeros((3,), jnp.float32))
     speed = jnp.sqrt(state[0, 0] ** 2 + state[1, 0] ** 2 + 0.25)
     surface = jnp.stack([speed, state[2, 0]]).astype(jnp.bfloat16).reshape(1, 2 * columns)
-    spread = jnp.broadcast_to(surface, (devices, 2 * columns))
-    gathered = lax.all_to_all(spread, ("sec", "tile"), split_axis=0, concat_axis=0, tiled=True)
     base_thresh = threshold_table(mass_frac.shape[1])
     erodible = lookup(erod_map, land_index)
     emission = emit(land_wind, land_moist, texture, erodible, mass_frac, blast_table, base_thresh)
@@ -117,10 +115,11 @@
     onehot = (targets[:, None] == jnp.arange(devices)[None, :]).astype(jnp.float32)
     dims = (((0,), (0,)), ((), ()))
     outgoing = lax.dot_general(onehot, flat_flux, dims, precision=high)
-    incoming = lax.all_to_all(
-        outgoing.astype(jnp.bfloat16), ("sec", "tile"), split_axis=0, concat_axis=0, tiled=True
-    )
-    flux = jnp.sum(incoming.astype(jnp.float32), axis=0).reshape(nbins, columns)
+    spread = jnp.broadcast_to(surface, (devices, 2 * columns))
+    payload = jnp.concatenate([outgoing.astype(jnp.bfloat16), spread], axis=1)
+    incoming = lax.all_to_all(payload, ("sec", "tile"), split_axis=0, concat_axis=0, tiled=True)
+    flux = jnp.sum(incoming[:, : nbins * columns].astype(jnp.float32), axis=0).reshape(nbins, columns)
+    gathered = incoming[:, nbins * columns :]
     flux = flux * (float(columns) / float(ncells * nblocks))
     loaded = dust_mix.at[:, 0, :].add(flux)
     dust_out = solve(loaded, mixing, settle)

time: 77.7 us -> 63.5 us (0.82)
  starting transfers between devices: 21.3 us -> 11.5 us
  matrix products: 27.5 us -> 24.1 us
  other arithmetic: 8.69 us -> 6.6 us
  waiting for transfers between devices: 12.2 us -> 14 us
  local copies, waits for them, and re-layouts: 6.45 us -> 5.55 us
    all_to_all x2 -> x1, starting transfers between devices: 21.3 us -> 11.5 us  [on_device(): lax.all_to_all(payload, ('sec', 'tile'), split_axis=0, concat_axis=0, til...]
    dot_general x1, matrix products: 4.61 us -> 1.19 us  [on_device(): jnp.einsum('gkl,gla->gka', emission, regrid_w, preferred_element_type=jnp...]
    all_to_all x2 -> x1, waiting for transfers between devices: 12.2 us -> 14 us  [on_device(): lax.all_to_all(payload, ('sec', 'tile'), split_axis=0, concat_axis=0, til...]
    broadcast_in_dim x1 -> x0, other arithmetic: 1.4 us -> none  [on_device(): spread = jnp.broadcast_to(surface, (devices, 2 * columns))]
    reduce_sum x1, other arithmetic: 0.99 us -> 0.09 us  [on_device(): jnp.sum(incoming[:, :nbins * columns].astype(jnp.float32), axis=0)]
    unnamed x32 -> x35, local copies, waits for them, and re-layouts: 3.53 us -> 2.76 us
  transfers between devices with their start and end apart: 2 -> 1, of which waited for: 1 -> 1; matrix products, arithmetic and copies ran while one was open for 20% -> 0% of each run, Pallas kernels for 0% -> 0%
where the time goes in v1:
time: 63.5 us; the launch traced here: 63 us
  matrix products  24.1 us (38%)
  waiting for transfers between devices  14 us (22%)
  starting transfers between devices  11.5 us (18%)
  other arithmetic  6.6 us (10%)
  local copies, waits for them, and re-layouts  5.55 us (9%)
  between operations  1.18 us (2%)
    all_to_all x1, waiting for transfers between devices, on_device(): lax.all_to_all(payload, ('sec', 'tile'), split_axis=0, concat_axis=0, til...  14 us
    dot_general x3, matrix products, lookup(): lax.dot_general(p, pick_row, dims, preferred_element_type=jnp.float32)  13.7 us
    all_to_all x1, starting transfers between devices, on_device(): lax.all_to_all(payload, ('sec', 'tile'), split_axis=0, concat_axis=0, til...  11.5 us
    dot_general x1, matrix products, on_device(): jnp.einsum('gla,gka->kgl', regrid_w, picked, preferred_element_type=jnp.f...  5.63 us
    unnamed x35, local copies, waits for them, and re-layouts  2.76 us
    dot_general x1, matrix products, emit(): blasted = jnp.einsum('tkb,bnl->tknl', blast_table, salt, precision=high)  1.88 us
  transfers between devices with their start and end apart: 1, of which 1 were waited for; matrix products, arithmetic and copies ran while one was open for 0% of the time, Pallas kernels for 0%

profile of v1, /device:TPU:1, one launch (start us, length us, event | category | flops | bytes accessed | tf_op | source)
XLA Modules:
  0.0 63.0 jit_solution(7381994120261582221)
XLA Ops:
  0.7 1.0 %fusion.85 = (f32[1,256]{1,0:T(1,128)S(1)}, f32[1,256]{1,0:T(1,128)S(1)}, f32[1,256]{1,0:T(1,128)S(1)}, f32[1,256]{1,0:T(1,128)S(1)}, f32[1,256]{1,0:T(1,128)S(1...) fusion(f32[15,256]{1,0:T(8,128)} %param.26), kind=kLoop, calls=%fused_computation.259 | loop fusion | flops 2816 | bytes 24576 | tf_op jit(solution)/shard_map/slice | solution.py:61
  1.6 1.0 %broadcast_add_fusion.1 = (f32[1,256]{1,0:T(1,128)S(1)}, f32[1,256]{1,0:T(1,128)S(1)}, f32[1,256]{1,0:T(1,128)S(1)}, f32[1,256]{1,0:T(1,128)S(1)}, f32[1,256]{1,...) fusion(f32[15,256]{1,0:T(8,128)} %param.26), kind=kLoop, calls=%fused_computation.252 | loop fusion | flops 4608 | bytes 20480 | tf_op jit(solution)/shard_map/add;add | solution.py:62
  2.6 0.9 %fusion.86 = (f32[1,256]{1,0:T(1,128)S(1)}, f32[1,256]{1,0:T(1,128)S(1)}, f32[1,256]{1,0:T(1,128)S(1)}, f32[1,256]{1,0:T(1,128)S(1)}, f32[1,256]{1,0:T(1,128)S(1...) fusion(f32[15,256]{1,0:T(8,128)} %param.26), kind=kLoop, calls=%fused_computation.260 | loop fusion | bytes 14336 | tf_op jit(solution)/shard_map/slice | solution.py:61
  3.5 1.2 %fusion.84 = (f32[3,1,256]{2,1,0:T(1,128)S(1)}, f32[3,1,256]{2,1,0:T(1,128)S(1)}, f32[3,1,256]{2,1,0:T(1,128)S(1)}, f32[3,1,256]{2,1,0:T(1,128)S(1)}, f32[3,1,25...) fusion(f32[3,16,256]{2,1,0:T(8,128)} %param.24), kind=kLoop, calls=%fused_computation.258 | loop fusion | bytes 98304 | tf_op jit(solution)/shard_map/slice | solution.py:65
  5.2 0.9 %add_select_fusion.1 = (s32[16384]{0:T(1024)S(1)}, s32[16384]{0:T(1024)S(1)}) fusion(s32[128,128]{1,0:T(8,128)} %param.18), kind=kLoop, calls=%fused_computation.43 | loop fusion | flops 311296 | bytes 196608 | tf_op jit(solution)/shard_map/jit(remainder)/select_n | solution.py:35
  6.1 4.4 %convolution_bitcast_fusion = f32[128,16384]{1,0:T(8,128)S(1)} fusion(s32[16384]{0:T(1024)S(1)} %get-tuple-element.81, f32[32768]{0:T(1024)} %param.19), kind=kOutput, calls=%fused_computation | convolution fusion | flops 1078001664 | bytes 8585216 | tf_op jit(solution)/shard_map/dot_general | solution.py:45
  10.5 4.0 %convolution_add_fusion.1 = f32[128,16384]{1,0:T(8,128)S(1)} fusion(f32[128,16384]{1,0:T(8,128)S(1)} %convolution_bitcast_fusion, s32[16384]{0:T(1024)S(1)} %get-tuple-element.81, f32[32768]{0:T(1024)S(1)} %copy-done.1), kind=kOutput, calls=%fused_computation.3 | convolution fusion | flops 1080164352 | bytes 16973824 | tf_op jit(solution)/shard_map/dot_general | solution.py:45
  14.6 5.2 %fusion.5 = f32[16384]{0:T(1024)S(1)} fusion(f32[128,16384]{1,0:T(8,128)S(1)} %convolution_add_fusion.1, s32[16384]{0:T(1024)S(1)} %get-tuple-element.81, s32[16384]{0:T(1024)S(1)} %get-tuple-element.80, f32[32768]{0:T(1024)S(1)} %copy-done.1), kind=kOutput, calls=%fused_computation.12 | convolution fusion | flops 1086472192 | bytes 8716288 | tf_op jit(solution)/shard_map/dot_general | solution.py:45
  20.0 0.8 %fusion.9 = f32[12,128,128,1]{2,0,3,1:T(8,128)S(1)} fusion(f32[128,128]{1,0:T(8,128)S(1)} %mul.1908, f32[128,128]{1,0:T(8,128)S(1)} %add_sqrt_fusion, f32[12]{0:T(128)S(1)} %multiply_sqrt_fusion, f32[128,128]{1,0:T(8,128)S(1)} %copy-done.2, f32[128,128]{1,0:T(8,128)S(1)} %multiply_bitcast_fusion, s32[128,128]{1,0:T(8,128)S(1)} %copy-done.5, ...), kind=kOutput, calls=%fused_computation.19 | convolution fusion | flops 11075584 | bytes 1114352 | tf_op jit(solution)/shard_map/tb,tnl->bnl/dot_general | solution.py:17
  20.8 1.9 %fusion.4 = bf16[8,128,128]{2,0,1:T(8,128)(2,1)S(1)} fusion(f32[12,128,128,1]{2,0,3,1:T(8,128)S(1)} %fusion.9, f32[4,128,128]{2,0,1:T(4,128)S(1)} %fusion.16, f32[4,8,12]{2,1,0:T(8,128)S(1)} %copy-done), kind=kOutput, calls=%fused_computation.11 | convolution fusion | flops 76414976 | bytes 1312256 | tf_op jit(solution)/shard_map/tkb,bnl->tknl/dot_general | solution.py:26
  22.8 1.2 %fusion.12 = f32[128,8,256]{2,1,0:T(8,128)S(1)} fusion(bf16[128,128,256]{2,1,0:T(8,128)(2,1)S(1)} %bitcast.245, bf16[8,128,128]{2,0,1:T(8,128)(2,1)S(1)} %fusion.4), kind=kOutput, calls=%fused_computation.27 | convolution fusion | flops 67108864 | bytes 9699328 | tf_op jit(solution)/shard_map/gkl,gla->gka/dot_general | solution.py:110
  24.0 0.3 copy.163
  24.3 0.7 %convolution_convert_fusion = bf16[128,2048]{1,0:T(8,128)(2,1)S(1)} fusion(f32[128,2048]{1,0:T(8,128)S(1)} %bitcast.247, s32[128]{0:T(128)S(1)} %bitcast.420), kind=kOutput, calls=%fused_computation.9 | convolution fusion | flops 402931712 | bytes 1573376 | tf_op jit(solution)/shard_map/dot_general | solution.py:117
  25.2 0.5 broadcast.18980
  25.7 1.1 %reduce.2 = bf16[128,2560]{1,0:T(8,128)(2,1)S(1)} reduce(bf16[128,1,2560]{2,0,1:T(8,128)(2,1)S(1)} %maximum_bitcast_fusion, bf16[]{:T(256)} %broadcast.18980), dimensions={1}, to_apply=%copy.106.reduce_sub_computation | reduce | bytes 1310722 | tf_op jit(solution)/shard_map/all_to_all | solution.py:120
  26.8 1.0 %reshape.27200 = bf16[128,2,1280]{2,1,0:T(2,128)(2,1)} reshape(bf16[128,2560]{1,0:T(8,128)(2,1)S(1)} %reduce.2) | data formatting | bytes 1310720
  27.8 11.5 %all-to-all-start = ((bf16[128,2,1280]{2,1,0:T(2,128)(2,1)}), bf16[128,2,1280]{2,1,0:T(2,128)(2,1)S(1)}, u32[]{:S(2)}, u32[]{:S(2)}) async-start(bf16[128,2,1280]{2,1,0:T(2,128)(2,1)} %reshape.27200), calls=%async_computation | async-start | bytes 1310720 | tf_op jit(solution)/shard_map/all_to_all | solution.py:120
  39.4 14.0 %all-to-all-done = bf16[128,2,1280]{2,1,0:T(2,128)(2,1)S(1)} async-done(((bf16[128,2,1280]{2,1,0:T(2,128)(2,1)}), bf16[128,2,1280]{2,1,0:T(2,128)(2,1)S(1)}, u32[]{:S(2)}, u32[]{:S(2)}) %all-to-all-start) | async-done | bytes 655392 | tf_op jit(solution)/shard_map/all_to_all | solution.py:120
  53.4 0.5 reshape.27201
  54.2 0.2 convolution_convert_fusion.1
  54.6 0.2 constant_dynamic-update-slice_fusion.15
  55.7 0.7 %copy.126 = f32[8,16,256]{2,1,0:T(8,128)} copy(f32[8,16,256]{2,0,1:T(8,128)S(1)} %constant_dynamic-update-slice_fusion) | data formatting | bytes 262144
  56.5 5.6 %convolution_bitcast_fusion.1 = f32[3,128,128]{2,0,1:T(4,128)S(1)} fusion(bf16[128,128,256]{2,1,0:T(8,128)(2,1)} %param.23, bf16[128,2,256]{2,1,0:T(2,128)(2,1)S(1)} %reshape.27195), kind=kOutput, calls=%fused_computation.20 | convolution fusion | flops 25165824 | bytes 8716288 | tf_op jit(solution)/shard_map/gla,gka->kgl/dot_general | solution.py:129
  62.3 0.7 %pad_maximum_fusion = f32[2,128,128]{2,1,0:T(8,128)} fusion(f32[1,128,128]{2,1,0:T(8,128)S(1)} %add_bitcast_fusion, f32[1,128,128]{2,1,0:T(8,128)S(1)} %div.1527), kind=kLoop, calls=%fused_computation.39 | loop fusion | flops 32768 | bytes 262144 | tf_op jit(solution)/shard_map/stack | solution.py:131
  (61 shorter events, 2.1 us)
Async XLA Ops:
  0.6 20.2 %copy-start = (f32[4,8,12]{2,1,0:T(8,128)S(1)}, f32[4,8,12]{2,1,0:T(8,128)}, u32[]{:S(2)}) copy-start(f32[4,8,12]{2,1,0:T(8,128)} %param.21) | copy-start | bytes 4612
  0.6 9.8 %copy-start.1 = (f32[32768]{0:T(1024)S(1)}, f32[32768]{0:T(1024)}, u32[]{:S(2)}) copy-start(f32[32768]{0:T(1024)} %param.19) | copy-start | bytes 393220
  10.5 12.2 %slice-start = ((s8[8388608]{0:T(1024)(128)(4,1)}), s8[4194304]{0:T(1024)(128)(4,1)S(1)}, s32[]{:S(2)}) async-start(s8[8388608]{0:T(1024)(128)(4,1)} %bitcast.244), calls=%async_computation.1 | async-start | bytes 8388608
  14.6 5.3 %copy-start.3 = (f32[128,128]{1,0:T(8,128)S(1)}, f32[128,128]{1,0:T(8,128)}, u32[]{:S(2)}) copy-start(f32[128,128]{1,0:T(8,128)} %param.16) | copy-start | bytes 196612
  14.6 5.3 %copy-start.2 = (f32[128,128]{1,0:T(8,128)S(1)}, f32[128,128]{1,0:T(8,128)}, u32[]{:S(2)}) copy-start(f32[128,128]{1,0:T(8,128)} %param.15) | copy-start | bytes 196612
  14.6 5.3 %copy-start.5 = (s32[128,128]{1,0:T(8,128)S(1)}, s32[128,128]{1,0:T(8,128)}, u32[]{:S(2)}) copy-start(s32[128,128]{1,0:T(8,128)} %param.17) | copy-start | bytes 196612
  14.6 5.4 %copy-start.8 = (f32[4,12]{1,0:T(4,128)S(1)}, f32[4,12]{1,0:T(4,128)}, u32[]{:S(2)}) copy-start(f32[4,12]{1,0:T(4,128)} %param.20) | copy-start | bytes 580
  14.6 8.1 %slice-start.1 = ((s8[8388608]{0:T(1024)(128)(4,1)}), s8[4194304]{0:T(1024)(128)(4,1)S(1)}, s32[]{:S(2)}) async-start(s8[8388608]{0:T(1024)(128)(4,1)} %bitcast.244), calls=%async_computation.2 | async-start | bytes 8388608
  22.8 1.6 %copy-start.7 = (s32[128,1]{0,1:T(1,128)S(1)}, s32[128,1]{0,1:T(1,128)}, u32[]{:S(2)}) copy-start(s32[128,1]{0,1:T(1,128)} %param.22) | copy-start | bytes 1540
  24.0 15.3 %copy-start.4 = (f32[8,16,256]{2,1,0:T(8,128)S(1)}, f32[8,16,256]{2,1,0:T(8,128)}, u32[]{:S(2)}) copy-start(f32[8,16,256]{2,1,0:T(8,128)} %param.25) | copy-start | bytes 393220
  24.0 30.5 %copy-start.6 = (f32[8]{0:T(128)S(1)}, f32[8]{0:T(128)}, u32[]{:S(2)}) copy-start(f32[8]{0:T(128)} %param.27) | copy-start | bytes 100
  27.8 25.7 %all-to-all-start = ((bf16[128,2,1280]{2,1,0:T(2,128)(2,1)}), bf16[128,2,1280]{2,1,0:T(2,128)(2,1)S(1)}, u32[]{:S(2)}, u32[]{:S(2)}) async-start(bf16[128,2,1280]{2,1,0:T(2,128)(2,1)} %reshape.27200), calls=%async_computation | async-start | bytes 1310720 | tf_op jit(solution)/shard_map/all_to_all | solution.py:120

commit v2 on v1

--- a/solution.py
+++ b/solution.py
@@ -1,6 +1,7 @@
 import jax
 import jax.numpy as jnp
 from jax import lax
+from jax.experimental import pallas as pl
 from jax.sharding import PartitionSpec as P
 
 
@@ -28,25 +29,46 @@
     return jnp.transpose(emission, (1, 0, 2)).astype(jnp.bfloat16)
 
 
+def lookup_kernel(index_ref, parts_ref, out_ref):
+    rows_per_step, lanes = index_ref.shape
+    segments = parts_ref.shape[1]
+    for r in range(rows_per_step):
+        cell = index_ref[r : r + 1, :]
+        high_part = cell // 128
+        low_part = cell % 128
+        pick_row = lax.broadcasted_iota(jnp.int32, (segments, lanes), 0) == high_part
+        pick_row = jnp.where(pick_row, 1.0, 0.0).astype(jnp.bfloat16)
+        products = jnp.dot(parts_ref[...], pick_row, preferred_element_type=jnp.float32)
+        row_values = (products[0:128] + products[128:256]) + products[256:384]
+        pick_lane = lax.broadcasted_iota(jnp.int32, (128, lanes), 0) == low_part
+        out_ref[r : r + 1, :] = jnp.sum(jnp.where(pick_lane, row_values, 0.0), axis=0, keepdims=True)
+
+
 def lookup(table, index):
-    rows = table.shape[0] // 128
-    flat = index.reshape(-1)
-    high_part = flat // 128
-    low_part = flat % 128
-    pick_row = (lax.broadcasted_iota(jnp.int32, (rows, flat.shape[0]), 0) == high_part[None, :]).astype(jnp.bfloat16)
-    grid = table.reshape(rows, 128)
+    segments = table.shape[0] // 128
+    grid = table.reshape(segments, 128)
     first_wide = lax.reduce_precision(grid, exponent_bits=8, mantissa_bits=7)
     rest = grid - first_wide
     second_wide = lax.reduce_precision(rest, exponent_bits=8, mantissa_bits=7)
-    first = first_wide.astype(jnp.bfloat16)
-    second = second_wide.astype(jnp.bfloat16)
-    third = (rest - second_wide).astype(jnp.bfloat16)
-    dims = (((0,), (0,)), ((), ()))
-    parts = [lax.dot_general(p, pick_row, dims, preferred_element_type=jnp.float32) for p in (first, second, third)]
-    row_values = (parts[0] + parts[1]) + parts[2]
-    pick_lane = lax.broadcasted_iota(jnp.int32, row_values.shape, 0) == low_part[None, :]
-    return jnp.sum(jnp.where(pick_lane, row_values, 0.0), axis=0).reshape(index.shape)
-
+    parts = jnp.concatenate(
+        [first_wide.T, second_wide.T, (rest - second_wide).T], axis=0
+    ).astype(jnp.bfloat16)
+    rows, lanes = index.shape
+    step = 8
+    return pl.pallas_call(
+        lookup_kernel,
+        out_shape=jax.ShapeDtypeStruct((rows, lanes), jnp.float32),
+        grid=(rows // step,),
+        in_specs=[
+            pl.BlockSpec((step, lanes), lambda i: (i, 0)),
+            pl.BlockSpec((3 * 128, segments), lambda i: (0, 0)),
+        ],
+        out_specs=pl.BlockSpec((step, lanes), lambda i: (i, 0)),
+        cost_estimate=pl.CostEstimate(
+            flops=2 * 384 * segments * rows * lanes, transcendentals=0,
+            bytes_accessed=8 * rows * lanes + 2 * 384 * segments,
+        ),
+    )(index, parts)
 
 def solve(right_side, coupling, sinking):
     levels = right_side.shape[1]

time: 63.5 us -> 69 us (1.087); the launches traced: 63 us -> 67.8 us
  Pallas kernels: 0 us -> 11.8 us
  matrix products: 24.1 us -> 13.8 us
  other arithmetic: 6.6 us -> 9.01 us
  local copies, waits for them, and re-layouts: 5.55 us -> 6.52 us
    dot_general x3 -> x0, matrix products: 13.7 us -> none  [lookup(): lax.dot_general(p, pick_row, dims, preferred_element_type=jnp.float32)]
    pallas_call x0 -> x1, Pallas kernels: none -> 11.8 us  [lookup(): pl.pallas_call(lookup_kernel, out_shape=jax.ShapeDtypeStruct((rows, lanes...]
    dot_general x1, matrix products: 1.19 us -> 4.57 us  [on_device(): jnp.einsum('gkl,gla->gka', emission, regrid_w, preferred_element_type=jnp...]
    reshape x0 -> x1, local copies, waits for them, and re-layouts: none -> 1 us  [lookup(): grid = table.reshape(segments, 128)]
    mul x1, other arithmetic: 0.01 us -> 0.93 us  [emit(): speed * speed - thresh * thresh]
    select_n x1 -> x0, other arithmetic: 0.9 us -> none  [lookup(): low_part = flat % 128]
    convert_element_type x1, other arithmetic: 0.06 us -> 0.9 us  [emit(): onehot = (texture_rows[None] == classes[:, None, None]).astype(jnp.float32)]
    sqrt x1, other arithmetic: 0.03 us -> 0.87 us  [emit(): jnp.sqrt(1.0 + 12.1 * moist_rows)[None]]
where the time goes in v2:
time: 69 us; the launch traced here: 67.8 us
  waiting for transfers between devices  14 us (20%)
  matrix products  13.8 us (20%)
  Pallas kernels  11.8 us (17%)
  starting transfers between devices  11.5 us (17%)
  other arithmetic  9.01 us (13%)
  local copies, waits for them, and re-layouts  6.52 us (9%)
  between operations  1.08 us (2%)
    all_to_all x1, waiting for transfers between devices, on_device(): lax.all_to_all(payload, ('sec', 'tile'), split_axis=0, concat_axis=0, til...  14 us
    pallas_call x1, Pallas kernels, lookup(): pl.pallas_call(lookup_kernel, out_shape=jax.ShapeDtypeStruct((rows, lanes...  11.8 us
    all_to_all x1, starting transfers between devices, on_device(): lax.all_to_all(payload, ('sec', 'tile'), split_axis=0, concat_axis=0, til...  11.5 us
    dot_general x1, matrix products, on_device(): jnp.einsum('gla,gka->kgl', regrid_w, picked, preferred_element_type=jnp.f...  5.64 us
    dot_general x1, matrix products, on_device(): jnp.einsum('gkl,gla->gka', emission, regrid_w, preferred_element_type=jnp...  4.57 us
    unnamed x29, local copies, waits for them, and re-layouts  2.73 us
    dot_general x1, matrix products, emit(): blasted = jnp.einsum('tkb,bnl->tknl', blast_table, salt, precision=high)  1.87 us
  transfers between devices with their start and end apart: 1, of which 1 were waited for; matrix products, arithmetic and copies ran while one was open for 0% of the time, Pallas kernels for 0%

profile of v2, /device:TPU:1, one launch (start us, length us, event | category | flops | bytes accessed | tf_op | source)
XLA Modules:
  0.0 67.8 jit_solution(4946527689121269574)
XLA Ops:
  0.7 1.0 %fusion.79 = (f32[1,256]{1,0:T(1,128)S(1)}, f32[1,256]{1,0:T(1,128)S(1)}, f32[1,256]{1,0:T(1,128)S(1)}, f32[1,256]{1,0:T(1,128)S(1)}, f32[1,256]{1,0:T(1,128)S(1...) fusion(f32[15,256]{1,0:T(8,128)} %param.26), kind=kLoop, calls=%fused_computation.243 | loop fusion | flops 2816 | bytes 24576 | tf_op jit(solution)/shard_map/slice | solution.py:83
  1.7 0.9 %fusion.80 = (f32[1,256]{1,0:T(1,128)S(1)}, f32[1,256]{1,0:T(1,128)S(1)}, f32[1,256]{1,0:T(1,128)S(1)}, f32[1,256]{1,0:T(1,128)S(1)}, f32[1,256]{1,0:T(1,128)S(1...) fusion(f32[15,256]{1,0:T(8,128)} %param.26), kind=kLoop, calls=%fused_computation.244 | loop fusion | bytes 14336 | tf_op jit(solution)/shard_map/slice | solution.py:83
  2.6 1.0 %broadcast_add_fusion.1 = (f32[1,256]{1,0:T(1,128)S(1)}, f32[1,256]{1,0:T(1,128)S(1)}, f32[1,256]{1,0:T(1,128)S(1)}, f32[1,256]{1,0:T(1,128)S(1)}, f32[1,256]{1,...) fusion(f32[15,256]{1,0:T(8,128)} %param.26), kind=kLoop, calls=%fused_computation.236 | loop fusion | flops 4608 | bytes 20480 | tf_op jit(solution)/shard_map/add;add | solution.py:84
  3.6 1.2 %fusion.78 = (f32[3,1,256]{2,1,0:T(1,128)S(1)}, f32[3,1,256]{2,1,0:T(1,128)S(1)}, f32[3,1,256]{2,1,0:T(1,128)S(1)}, f32[3,1,256]{2,1,0:T(1,128)S(1)}, f32[3,1,25...) fusion(f32[3,16,256]{2,1,0:T(8,128)} %param.24), kind=kLoop, calls=%fused_computation.242 | loop fusion | bytes 98304 | tf_op jit(solution)/shard_map/slice | solution.py:87
  5.2 0.9 %mul.1905 = f32[128,128]{1,0:T(8,128)S(1)} multiply(f32[128,128]{1,0:T(8,128)} %param.15, f32[128,128]{1,0:T(8,128)} %param.15) | non-fusion elementwise | flops 16384 | bytes 196608 | tf_op jit(solution)/shard_map/mul | solution.py:25
  6.1 1.0 %copy.97 = f32[256,128]{0,1:T(8,128)S(1)} copy(f32[256,128]{1,0:T(8,128)} %bitcast.218) | data formatting | bytes 262144 | tf_op jit(solution)/shard_map/reshape | solution.py:49
  7.1 0.9 %fusion.11 = f32[4,128,128]{2,0,1:T(4,128)S(1)} fusion(s32[128,128]{1,0:T(8,128)} %param.17), kind=kLoop, calls=%fused_computation.22 | loop fusion | flops 131072 | bytes 327680 | tf_op jit(solution)/shard_map/convert_element_type | solution.py:17
  8.0 0.7 %pad_maximum_fusion.parts_ref = bf16[384,256]{1,0:T(8,128)(2,1)} fusion(bf16[128,256]{1,0:T(8,128)(2,1)S(1)} %get-tuple-element.81, bf16[128,256]{1,0:T(8,128)(2,1)S(1)} %get-tuple-element.82, bf16[128,256]{1,0:T(8,128)(2,1)S(1)} %get-tuple-element.80), kind=kLoop, calls=%fused_computation.23 | loop fusion | flops 589824 | bytes 393216 | tf_op jit(solution)/shard_map/concatenate | solution.py:53
  8.7 11.8 %shard_map.140 = f32[128,128]{1,0:T(8,128)} custom-call(s32[128,128]{1,0:T(8,128)} %index_ref.1, bf16[384,256]{1,0:T(8,128)(2,1)} %pad_maximum_fusion.parts_ref), custom_call_target="tpu_custom_call" | custom-call | flops 3221225472 | bytes 327680 | tf_op jit(solution)/shard_map/pallas_call | solution.py:58
  20.5 0.9 %add_sqrt_fusion = (f32[128,128]{1,0:T(8,128)S(1)}, f32[128,128]{1,0:T(8,128)S(1)}) fusion(f32[128,128]{1,0:T(8,128)S(1)} %copy-done.2, f32[128,128]{1,0:T(8,128)} %shard_map.140), kind=kLoop, calls=%fused_computation.38 | loop fusion | flops 49152 | bytes 262144 | tf_op jit(solution)/shard_map/sqrt | solution.py:15
  21.4 0.8 %fusion.4 = f32[12,128,128,1]{2,0,3,1:T(8,128)S(1)} fusion(f32[128,128]{1,0:T(8,128)S(1)} %mul.1905, f32[128,128]{1,0:T(8,128)S(1)} %get-tuple-element.130, f32[12]{0:T(128)S(1)} %multiply_sqrt_fusion, f32[128,128]{1,0:T(8,128)S(1)} %copy-done.1, f32[128,128]{1,0:T(8,128)S(1)} %get-tuple-element.131, s32[128,128]{1,0:T(8,128)S(1)} %copy-done.4, ...), kind=kOutput, calls=%fused_computation.9 | convolution fusion | flops 11075584 | bytes 1114352 | tf_op jit(solution)/shard_map/tb,tnl->bnl/dot_general | solution.py:18
  22.2 1.9 %fusion = bf16[8,128,128]{2,0,1:T(8,128)(2,1)S(1)} fusion(f32[12,128,128,1]{2,0,3,1:T(8,128)S(1)} %fusion.4, f32[4,128,128]{2,0,1:T(4,128)S(1)} %fusion.11, f32[4,8,12]{2,1,0:T(8,128)S(1)} %copy-done), kind=kOutput, calls=%fused_computation.2 | convolution fusion | flops 76414976 | bytes 1312256 | tf_op jit(solution)/shard_map/tkb,bnl->tknl/dot_general | solution.py:27
  24.1 4.6 %fusion.7 = f32[128,8,256]{2,1,0:T(8,128)S(1)} fusion(bf16[128,128,256]{2,1,0:T(8,128)(2,1)} %param.23, bf16[8,128,128]{2,0,1:T(8,128)(2,1)S(1)} %fusion), kind=kOutput, calls=%fused_computation.17 | convolution fusion | flops 67108864 | bytes 9699328 | tf_op jit(solution)/shard_map/gkl,gla->gka/dot_general | solution.py:132
  28.7 0.3 copy.171
  29.1 0.7 %convolution_convert_fusion = bf16[128,2048]{1,0:T(8,128)(2,1)S(1)} fusion(f32[128,2048]{1,0:T(8,128)S(1)} %bitcast.212, s32[128]{0:T(128)S(1)} %bitcast.386), kind=kOutput, calls=%fused_computation | convolution fusion | flops 402931712 | bytes 1573376 | tf_op jit(solution)/shard_map/dot_general | solution.py:139
  30.0 0.5 broadcast.18920
  30.5 1.1 %reduce.2 = bf16[128,2560]{1,0:T(8,128)(2,1)S(1)} reduce(bf16[128,1,2560]{2,0,1:T(8,128)(2,1)S(1)} %maximum_bitcast_fusion, bf16[]{:T(256)} %broadcast.18920), dimensions={1}, to_apply=%copy.114.reduce_sub_computation | reduce | bytes 1310722 | tf_op jit(solution)/shard_map/all_to_all | solution.py:142
  31.6 1.0 %reshape.27145 = bf16[128,2,1280]{2,1,0:T(2,128)(2,1)} reshape(bf16[128,2560]{1,0:T(8,128)(2,1)S(1)} %reduce.2) | data formatting | bytes 1310720
  32.6 11.5 %all-to-all-start = ((bf16[128,2,1280]{2,1,0:T(2,128)(2,1)}), bf16[128,2,1280]{2,1,0:T(2,128)(2,1)S(1)}, u32[]{:S(2)}, u32[]{:S(2)}) async-start(bf16[128,2,1280]{2,1,0:T(2,128)(2,1)} %reshape.27145), calls=%async_computation | async-start | bytes 1310720 | tf_op jit(solution)/shard_map/all_to_all | solution.py:142
  44.2 14.0 %all-to-all-done = bf16[128,2,1280]{2,1,0:T(2,128)(2,1)S(1)} async-done(((bf16[128,2,1280]{2,1,0:T(2,128)(2,1)}), bf16[128,2,1280]{2,1,0:T(2,128)(2,1)S(1)}, u32[]{:S(2)}, u32[]{:S(2)}) %all-to-all-start) | async-done | bytes 655392 | tf_op jit(solution)/shard_map/all_to_all | solution.py:142
  58.2 0.5 reshape.27146
  59.2 5.6 %convolution_bitcast_fusion = f32[3,128,128]{2,0,1:T(4,128)S(1)} fusion(bf16[128,128,256]{2,1,0:T(8,128)(2,1)} %param.23, bf16[128,2,256]{2,1,0:T(2,128)(2,1)S(1)} %reshape.27140), kind=kOutput, calls=%fused_computation.10 | convolution fusion | flops 25165824 | bytes 8716288 | tf_op jit(solution)/shard_map/gla,gka->kgl/dot_general | solution.py:151
  66.4 0.7 %copy.134 = f32[8,16,256]{2,1,0:T(8,128)} copy(f32[8,16,256]{2,0,1:T(8,128)S(1)} %constant_dynamic-update-slice_fusion) | data formatting | bytes 262144
  67.1 0.7 pad_maximum_fusion.1
  (53 shorter events, 2.4 us)
Async XLA Ops:
  0.6 21.6 %copy-start = (f32[4,8,12]{2,1,0:T(8,128)S(1)}, f32[4,8,12]{2,1,0:T(8,128)}, u32[]{:S(2)}) copy-start(f32[4,8,12]{2,1,0:T(8,128)} %param.21) | copy-start | bytes 4612
  0.6 20.7 %copy-start.1 = (f32[128,128]{1,0:T(8,128)S(1)}, f32[128,128]{1,0:T(8,128)}, u32[]{:S(2)}) copy-start(f32[128,128]{1,0:T(8,128)} %param.15) | copy-start | bytes 196612
  0.7 20.7 %copy-start.4 = (s32[128,128]{1,0:T(8,128)S(1)}, s32[128,128]{1,0:T(8,128)}, u32[]{:S(2)}) copy-start(s32[128,128]{1,0:T(8,128)} %param.17) | copy-start | bytes 196612
  0.7 19.8 %copy-start.2 = (f32[128,128]{1,0:T(8,128)S(1)}, f32[128,128]{1,0:T(8,128)}, u32[]{:S(2)}) copy-start(f32[128,128]{1,0:T(8,128)} %param.16) | copy-start | bytes 196612
  0.7 20.7 %copy-start.7 = (f32[4,12]{1,0:T(4,128)S(1)}, f32[4,12]{1,0:T(4,128)}, u32[]{:S(2)}) copy-start(f32[4,12]{1,0:T(4,128)} %param.20) | copy-start | bytes 580
  24.1 5.0 %copy-start.6 = (s32[128,1]{0,1:T(1,128)S(1)}, s32[128,1]{0,1:T(1,128)}, u32[]{:S(2)}) copy-start(s32[128,1]{0,1:T(1,128)} %param.22) | copy-start | bytes 1540
  28.7 15.4 %copy-start.3 = (f32[8,16,256]{2,1,0:T(8,128)S(1)}, f32[8,16,256]{2,1,0:T(8,128)}, u32[]{:S(2)}) copy-start(f32[8,16,256]{2,1,0:T(8,128)} %param.25) | copy-start | bytes 393220
  31.6 33.5 %copy-start.5 = (f32[8]{0:T(128)S(1)}, f32[8]{0:T(128)}, u32[]{:S(2)}) copy-start(f32[8]{0:T(128)} %param.27) | copy-start | bytes 100
  32.6 25.7 %all-to-all-start = ((bf16[128,2,1280]{2,1,0:T(2,128)(2,1)}), bf16[128,2,1280]{2,1,0:T(2,128)(2,1)S(1)}, u32[]{:S(2)}, u32[]{:S(2)}) async-start(bf16[128,2,1280]{2,1,0:T(2,128)(2,1)} %reshape.27145), calls=%async_computation | async-start | bytes 1310720 | tf_op jit(solution)/shard_map/all_to_all | solution.py:142

commit v3 on v1

--- a/solution.py
+++ b/solution.py
@@ -117,7 +117,12 @@
     outgoing = lax.dot_general(onehot, flat_flux, dims, precision=high)
     spread = jnp.broadcast_to(surface, (devices, 2 * columns))
     payload = jnp.concatenate([outgoing.astype(jnp.bfloat16), spread], axis=1)
-    incoming = lax.all_to_all(payload, ("sec", "tile"), split_axis=0, concat_axis=0, tiled=True)
+    pairs = lax.axis_size("sec")
+    width = payload.shape[1]
+    payload = payload.reshape(pairs, devices // pairs, width)
+    payload = lax.all_to_all(payload, "tile", split_axis=1, concat_axis=1, tiled=True)
+    incoming = lax.all_to_all(payload, "sec", split_axis=0, concat_axis=0, tiled=True)
+    incoming = incoming.reshape(devices, width)
     flux = jnp.sum(incoming[:, : nbins * columns].astype(jnp.float32), axis=0).reshape(nbins, columns)
     gathered = incoming[:, nbins * columns :]
     flux = flux * (float(columns) / float(ncells * nblocks))

time: 63.5 us -> 67.7 us (1.066)
  blocking collectives: 0 us -> 6.28 us
  other arithmetic: 6.6 us -> 5.5 us
  waiting for transfers between devices: 14 us -> 13.1 us
    all_to_all x0 -> x1, blocking collectives: none -> 6.28 us  [on_device(): lax.all_to_all(payload, 'sec', split_axis=0, concat_axis=0, tiled=True)]
    unnamed x35 -> x32, local copies, waits for them, and re-layouts: 2.76 us -> 1.15 us
    reshape x0 -> x1, local copies, waits for them, and re-layouts: none -> 1.52 us  [on_device(): payload = payload.reshape(pairs, devices // pairs, width)]
    all_to_all x2 -> x0, other arithmetic: 1.2 us -> none  [on_device(): lax.all_to_all(payload, ('sec', 'tile'), split_axis=0, concat_axis=0, til...]
    all_to_all x1, waiting for transfers between devices: 14 us -> 13.1 us  [on_device(): lax.all_to_all(payload, 'tile', split_axis=1, concat_axis=1, tiled=True)]
where the time goes in v3:
time: 67.7 us; the launch traced here: 67.1 us
  matrix products  24.1 us (36%)
  waiting for transfers between devices  13.1 us (19%)
  starting transfers between devices  12 us (18%)
  blocking collectives  6.28 us (9%)
  other arithmetic  5.5 us (8%)
  local copies, waits for them, and re-layouts  5.01 us (7%)
  between operations  1.16 us (2%)
    dot_general x3, matrix products, lookup(): lax.dot_general(p, pick_row, dims, preferred_element_type=jnp.float32)  13.7 us
    all_to_all x1, waiting for transfers between devices, on_device(): lax.all_to_all(payload, 'tile', split_axis=1, concat_axis=1, tiled=True)  13.1 us
    all_to_all x1, starting transfers between devices, on_device(): lax.all_to_all(payload, 'tile', split_axis=1, concat_axis=1, tiled=True)  12 us
    all_to_all x1, blocking collectives, on_device(): lax.all_to_all(payload, 'sec', split_axis=0, concat_axis=0, tiled=True)  6.28 us
    dot_general x1, matrix products, on_device(): jnp.einsum('gla,gka->kgl', regrid_w, picked, preferred_element_type=jnp.f...  5.63 us
    dot_general x1, matrix products, emit(): blasted = jnp.einsum('tkb,bnl->tknl', blast_table, salt, precision=high)  1.88 us
    reshape x1, local copies, waits for them, and re-layouts, on_device(): payload = payload.reshape(pairs, devices // pairs, width)  1.52 us
  transfers between devices with their start and end apart: 1, of which 1 were waited for; matrix products, arithmetic and copies ran while one was open for 0% of the time, Pallas kernels for 0%

profile of v3, /device:TPU:1, one launch (start us, length us, event | category | flops | bytes accessed | tf_op | source)
XLA Modules:
  0.0 67.1 jit_solution(13413805842256864008)
XLA Ops:
  0.7 1.0 %fusion.85 = (f32[1,256]{1,0:T(1,128)S(1)}, f32[1,256]{1,0:T(1,128)S(1)}, f32[1,256]{1,0:T(1,128)S(1)}, f32[1,256]{1,0:T(1,128)S(1)}, f32[1,256]{1,0:T(1,128)S(1...) fusion(f32[15,256]{1,0:T(8,128)} %param.26), kind=kLoop, calls=%fused_computation.258 | loop fusion | flops 2816 | bytes 24576 | tf_op jit(solution)/shard_map/slice | solution.py:61
  1.6 1.0 %broadcast_add_fusion.1 = (f32[1,256]{1,0:T(1,128)S(1)}, f32[1,256]{1,0:T(1,128)S(1)}, f32[1,256]{1,0:T(1,128)S(1)}, f32[1,256]{1,0:T(1,128)S(1)}, f32[1,256]{1,...) fusion(f32[15,256]{1,0:T(8,128)} %param.26), kind=kLoop, calls=%fused_computation.251 | loop fusion | flops 4608 | bytes 20480 | tf_op jit(solution)/shard_map/add;add | solution.py:62
  2.6 0.9 %fusion.86 = (f32[1,256]{1,0:T(1,128)S(1)}, f32[1,256]{1,0:T(1,128)S(1)}, f32[1,256]{1,0:T(1,128)S(1)}, f32[1,256]{1,0:T(1,128)S(1)}, f32[1,256]{1,0:T(1,128)S(1...) fusion(f32[15,256]{1,0:T(8,128)} %param.26), kind=kLoop, calls=%fused_computation.259 | loop fusion | bytes 14336 | tf_op jit(solution)/shard_map/slice | solution.py:61
  3.5 1.2 %fusion.84 = (f32[3,1,256]{2,1,0:T(1,128)S(1)}, f32[3,1,256]{2,1,0:T(1,128)S(1)}, f32[3,1,256]{2,1,0:T(1,128)S(1)}, f32[3,1,256]{2,1,0:T(1,128)S(1)}, f32[3,1,25...) fusion(f32[3,16,256]{2,1,0:T(8,128)} %param.24), kind=kLoop, calls=%fused_computation.257 | loop fusion | bytes 98304 | tf_op jit(solution)/shard_map/slice | solution.py:65
  5.2 0.9 %add_select_fusion.1 = (s32[16384]{0:T(1024)S(1)}, s32[16384]{0:T(1024)S(1)}) fusion(s32[128,128]{1,0:T(8,128)} %param.18), kind=kLoop, calls=%fused_computation.42 | loop fusion | flops 311296 | bytes 196608 | tf_op jit(solution)/shard_map/jit(remainder)/select_n | solution.py:35
  6.1 4.4 %convolution_bitcast_fusion = f32[128,16384]{1,0:T(8,128)S(1)} fusion(s32[16384]{0:T(1024)S(1)} %get-tuple-element.81, f32[32768]{0:T(1024)} %param.19), kind=kOutput, calls=%fused_computation | convolution fusion | flops 1078001664 | bytes 8585216 | tf_op jit(solution)/shard_map/dot_general | solution.py:45
  10.5 4.0 %convolution_add_fusion.1 = f32[128,16384]{1,0:T(8,128)S(1)} fusion(f32[128,16384]{1,0:T(8,128)S(1)} %convolution_bitcast_fusion, s32[16384]{0:T(1024)S(1)} %get-tuple-element.81, f32[32768]{0:T(1024)S(1)} %copy-done.1), kind=kOutput, calls=%fused_computation.3 | convolution fusion | flops 1080164352 | bytes 16973824 | tf_op jit(solution)/shard_map/dot_general | solution.py:45
  14.6 5.2 %fusion.5 = f32[16384]{0:T(1024)S(1)} fusion(f32[128,16384]{1,0:T(8,128)S(1)} %convolution_add_fusion.1, s32[16384]{0:T(1024)S(1)} %get-tuple-element.81, s32[16384]{0:T(1024)S(1)} %get-tuple-element.80, f32[32768]{0:T(1024)S(1)} %copy-done.1), kind=kOutput, calls=%fused_computation.12 | convolution fusion | flops 1086472192 | bytes 8716288 | tf_op jit(solution)/shard_map/dot_general | solution.py:45
  20.0 0.8 %fusion.9 = f32[12,128,128,1]{2,0,3,1:T(8,128)S(1)} fusion(f32[128,128]{1,0:T(8,128)S(1)} %mul.1908, f32[128,128]{1,0:T(8,128)S(1)} %add_sqrt_fusion, f32[12]{0:T(128)S(1)} %multiply_sqrt_fusion, f32[128,128]{1,0:T(8,128)S(1)} %copy-done.2, f32[128,128]{1,0:T(8,128)S(1)} %multiply_bitcast_fusion, s32[128,128]{1,0:T(8,128)S(1)} %copy-done.5, ...), kind=kOutput, calls=%fused_computation.19 | convolution fusion | flops 11075584 | bytes 1114352 | tf_op jit(solution)/shard_map/tb,tnl->bnl/dot_general | solution.py:17
  20.8 1.9 %fusion.4 = bf16[8,128,128]{2,0,1:T(8,128)(2,1)S(1)} fusion(f32[12,128,128,1]{2,0,3,1:T(8,128)S(1)} %fusion.9, f32[4,128,128]{2,0,1:T(4,128)S(1)} %fusion.16, f32[4,8,12]{2,1,0:T(8,128)S(1)} %copy-done), kind=kOutput, calls=%fused_computation.11 | convolution fusion | flops 76414976 | bytes 1312256 | tf_op jit(solution)/shard_map/tkb,bnl->tknl/dot_general | solution.py:26
  22.8 1.2 %fusion.12 = f32[128,8,256]{2,1,0:T(8,128)S(1)} fusion(bf16[128,128,256]{2,1,0:T(8,128)(2,1)S(1)} %bitcast.242, bf16[8,128,128]{2,0,1:T(8,128)(2,1)S(1)} %fusion.4), kind=kOutput, calls=%fused_computation.26 | convolution fusion | flops 67108864 | bytes 9699328 | tf_op jit(solution)/shard_map/gkl,gla->gka/dot_general | solution.py:110
  24.0 0.3 copy.164
  24.4 0.7 %convolution_convert_fusion = bf16[128,2048]{1,0:T(8,128)(2,1)S(1)} fusion(f32[128,2048]{1,0:T(8,128)S(1)} %bitcast.244, s32[128]{0:T(128)S(1)} %bitcast.418), kind=kOutput, calls=%fused_computation.9 | convolution fusion | flops 402931712 | bytes 1573376 | tf_op jit(solution)/shard_map/dot_general | solution.py:117
  25.2 1.5 %copy.107 = bf16[2,64,2560]{2,0,1:T(2,128)(2,1)} copy(bf16[2,64,2560]{2,1,0:T(8,128)(2,1)S(1)} %bitcast.245) | data formatting | bytes 1310720 | tf_op jit(solution)/shard_map/reshape | solution.py:122
  26.7 12.0 %all-to-all-start = ((bf16[2,64,2560]{2,0,1:T(2,128)(2,1)}), bf16[2,64,2560]{2,0,1:T(2,128)(2,1)S(1)}, u32[]{:S(2)}, u32[]{:S(2)}) async-start(bf16[2,64,2560]{2,0,1:T(2,128)(2,1)} %copy.107), calls=%async_computation | async-start | bytes 1310720 | tf_op jit(solution)/shard_map/all_to_all | solution.py:123
  38.8 13.1 %all-to-all-done = bf16[2,64,2560]{2,0,1:T(2,128)(2,1)S(1)} async-done(((bf16[2,64,2560]{2,0,1:T(2,128)(2,1)}), bf16[2,64,2560]{2,0,1:T(2,128)(2,1)S(1)}, u32[]{:S(2)}, u32[]{:S(2)}) %all-to-all-start) | async-done | bytes 655392 | tf_op jit(solution)/shard_map/all_to_all | solution.py:123
  51.9 6.3 %all_to_all.10 = bf16[2,64,2560]{2,1,0:T(8,128)(2,1)S(1)} all-to-all(bf16[2,64,2560]{2,1,0:T(8,128)(2,1)S(1)} %copy.108), channel_id=1, replica_groups=mesh['sec'=2,'tile'=64] {'sec'}, dimensions={0} | all-to-all | bytes 1310720 | tf_op jit(solution)/shard_map/all_to_all | solution.py:124
  58.3 0.2 convolution_convert_fusion.1
  58.6 0.2 fusion.34
  58.8 0.2 constant_dynamic-update-slice_fusion.15
  59.9 0.7 %copy.128 = f32[8,16,256]{2,1,0:T(8,128)} copy(f32[8,16,256]{2,0,1:T(8,128)S(1)} %constant_dynamic-update-slice_fusion) | data formatting | bytes 262144
  60.6 5.6 %convolution_bitcast_fusion.1 = f32[3,128,128]{2,0,1:T(4,128)S(1)} fusion(bf16[128,128,256]{2,1,0:T(8,128)(2,1)} %param.23, bf16[128,2,256]{2,1,0:T(2,128)(2,1)S(1)} %reshape.27201), kind=kOutput, calls=%fused_computation.20 | convolution fusion | flops 25165824 | bytes 8716288 | tf_op jit(solution)/shard_map/gla,gka->kgl/dot_general | solution.py:134
  66.2 0.2 fusion.82
  66.5 0.7 pad_maximum_fusion.1
  (59 shorter events, 1.7 us)
Async XLA Ops:
  0.6 20.2 %copy-start = (f32[4,8,12]{2,1,0:T(8,128)S(1)}, f32[4,8,12]{2,1,0:T(8,128)}, u32[]{:S(2)}) copy-start(f32[4,8,12]{2,1,0:T(8,128)} %param.21) | copy-start | bytes 4612
  0.6 9.8 %copy-start.1 = (f32[32768]{0:T(1024)S(1)}, f32[32768]{0:T(1024)}, u32[]{:S(2)}) copy-start(f32[32768]{0:T(1024)} %param.19) | copy-start | bytes 393220
  10.5 12.2 %slice-start = ((s8[8388608]{0:T(1024)(128)(4,1)}), s8[4194304]{0:T(1024)(128)(4,1)S(1)}, s32[]{:S(2)}) async-start(s8[8388608]{0:T(1024)(128)(4,1)} %bitcast.241), calls=%async_computation.2 | async-start | bytes 8388608
  14.6 5.3 %copy-start.3 = (f32[128,128]{1,0:T(8,128)S(1)}, f32[128,128]{1,0:T(8,128)}, u32[]{:S(2)}) copy-start(f32[128,128]{1,0:T(8,128)} %param.16) | copy-start | bytes 196612
  14.6 5.3 %copy-start.2 = (f32[128,128]{1,0:T(8,128)S(1)}, f32[128,128]{1,0:T(8,128)}, u32[]{:S(2)}) copy-start(f32[128,128]{1,0:T(8,128)} %param.15) | copy-start | bytes 196612
  14.6 5.3 %copy-start.5 = (s32[128,128]{1,0:T(8,128)S(1)}, s32[128,128]{1,0:T(8,128)}, u32[]{:S(2)}) copy-start(s32[128,128]{1,0:T(8,128)} %param.17) | copy-start | bytes 196612
  14.6 5.4 %copy-start.8 = (f32[4,12]{1,0:T(4,128)S(1)}, f32[4,12]{1,0:T(4,128)}, u32[]{:S(2)}) copy-start(f32[4,12]{1,0:T(4,128)} %param.20) | copy-start | bytes 580
  14.6 8.1 %slice-start.1 = ((s8[8388608]{0:T(1024)(128)(4,1)}), s8[4194304]{0:T(1024)(128)(4,1)S(1)}, s32[]{:S(2)}) async-start(s8[8388608]{0:T(1024)(128)(4,1)} %bitcast.241), calls=%async_computation.3 | async-start | bytes 8388608
  22.8 1.6 %copy-start.7 = (s32[128,1]{0,1:T(1,128)S(1)}, s32[128,1]{0,1:T(1,128)}, u32[]{:S(2)}) copy-start(s32[128,1]{0,1:T(1,128)} %param.22) | copy-start | bytes 1540
  22.8 15.9 %copy-start.4 = (f32[8,16,256]{2,1,0:T(8,128)S(1)}, f32[8,16,256]{2,1,0:T(8,128)}, u32[]{:S(2)}) copy-start(f32[8,16,256]{2,1,0:T(8,128)} %param.25) | copy-start | bytes 393220
  24.0 34.6 %copy-start.6 = (f32[8]{0:T(128)S(1)}, f32[8]{0:T(128)}, u32[]{:S(2)}) copy-start(f32[8]{0:T(128)} %param.27) | copy-start | bytes 100
  26.7 25.2 %all-to-all-start = ((bf16[2,64,2560]{2,0,1:T(2,128)(2,1)}), bf16[2,64,2560]{2,0,1:T(2,128)(2,1)S(1)}, u32[]{:S(2)}, u32[]{:S(2)}) async-start(bf16[2,64,2560]{2,0,1:T(2,128)(2,1)} %copy.107), calls=%async_computation | async-start | bytes 1310720 | tf_op jit(solution)/shard_map/all_to_all | solution.py:123

commit v4 on v1

--- a/solution.py
+++ b/solution.py
@@ -1,6 +1,7 @@
 import jax
 import jax.numpy as jnp
 from jax import lax
+from jax.experimental import pallas as pl
 from jax.sharding import PartitionSpec as P
 
 
@@ -81,6 +82,48 @@
     return jnp.stack(result, axis=1)
 
 
+def back_kernel(dest_ref, gathered_ref, weights_ref, moist_ref, out_ref):
+    blocks, _, columns = weights_ref.shape
+    tiles = gathered_ref.shape[0]
+    pick = lax.broadcasted_iota(jnp.int32, (blocks, tiles), 1) == dest_ref[...]
+    pick = jnp.where(pick, 1.0, 0.0).astype(jnp.bfloat16)
+    surfaces = jnp.dot(pick, gathered_ref[...], preferred_element_type=jnp.float32)
+    rows = lax.broadcasted_iota(jnp.int32, (8, columns), 0)
+    contract = (((1,), (1,)), ((), ()))
+    for b in range(blocks):
+        speed = surfaces[b : b + 1, :columns]
+        humid = surfaces[b : b + 1, columns:]
+        lhs = jnp.where(rows == 0, speed, jnp.where(rows == 1, humid, jnp.where(rows == 2, 1.0, 0.0)))
+        sums = lax.dot_general(
+            lhs.astype(jnp.bfloat16), weights_ref[b], contract, preferred_element_type=jnp.float32
+        )
+        denom = sums[2:3]
+        out_ref[0, b : b + 1, :] = sums[0:1] / denom
+        out_ref[1, b : b + 1, :] = 0.5 * moist_ref[b : b + 1, :] + 0.5 * (sums[1:2] / denom)
+
+
+def regrid_back(dest_tile, gathered, regrid_w, land_moist):
+    nblocks, ncells, columns = regrid_w.shape
+    tiles, width = gathered.shape
+    step = 16
+    return pl.pallas_call(
+        back_kernel,
+        out_shape=jax.ShapeDtypeStruct((2, nblocks, ncells), jnp.float32),
+        grid=(nblocks // step,),
+        in_specs=[
+            pl.BlockSpec((step, 1), lambda i: (i, 0)),
+            pl.BlockSpec((tiles, width), lambda i: (0, 0)),
+            pl.BlockSpec((step, ncells, columns), lambda i: (i, 0, 0)),
+            pl.BlockSpec((step, ncells), lambda i: (i, 0)),
+        ],
+        out_specs=pl.BlockSpec((2, step, ncells), lambda i: (0, i, 0)),
+        cost_estimate=pl.CostEstimate(
+            flops=2 * 8 * columns * ncells * nblocks, transcendentals=0,
+            bytes_accessed=2 * nblocks * ncells * columns + 12 * nblocks * ncells,
+        ),
+    )(dest_tile, gathered, regrid_w, land_moist)
+
+
 def on_device(
     land_wind,
     land_moist,
@@ -123,12 +166,7 @@
     flux = flux * (float(columns) / float(ncells * nblocks))
     loaded = dust_mix.at[:, 0, :].add(flux)
     dust_out = solve(loaded, mixing, settle)
-    picked = jnp.dot(onehot.astype(jnp.bfloat16), gathered, preferred_element_type=jnp.float32)
-    picked = picked.astype(jnp.bfloat16).reshape(nblocks, 2, columns)
-    picked = jnp.concatenate([picked, jnp.ones((nblocks, 1, columns), jnp.bfloat16)], axis=1)
-    numer = jnp.einsum("gla,gka->kgl", regrid_w, picked, preferred_element_type=jnp.float32)
-    denom = numer[2]
-    land_fields = jnp.stack([numer[0] / denom, 0.5 * land_moist + 0.5 * numer[1] / denom])
+    land_fields = regrid_back(dest_tile, gathered, regrid_w, land_moist)
     return (land_fields, dust_out)
 
 

time: 63.5 us -> 66.4 us (1.046)
  Pallas kernels: 0 us -> 8.92 us
  matrix products: 24.1 us -> 18.3 us
  local copies, waits for them, and re-layouts: 5.55 us -> 6.9 us
  other arithmetic: 6.6 us -> 5.72 us
  waiting for transfers between devices: 14 us -> 13.3 us
    pallas_call x0 -> x1, Pallas kernels: none -> 8.92 us  [regrid_back(): pl.pallas_call(back_kernel, out_shape=jax.ShapeDtypeStruct((2, nblocks, n...]
    dot_general x2 -> x0, matrix products: 5.86 us -> none  [the longest x1 5.63 us: on_device(): jnp.einsum('gla,gka->kgl', regrid_w, picked, preferred_element_type=jnp.f...]
    unnamed x35 -> x36, local copies, waits for them, and re-layouts: 2.76 us -> 3.49 us
    all_to_all x1, waiting for transfers between devices: 14 us -> 13.3 us  [on_device(): lax.all_to_all(payload, ('sec', 'tile'), split_axis=0, concat_axis=0, til...]
    another operation x3 -> x1, other arithmetic: 0.69 us -> 0.01 us  [the longest x2 0.68 us: on_device(): jnp.stack([numer[0] / denom, 0.5 * land_moist + 0.5 * numer[1] / denom])]
  transfers between devices with their start and end apart: 1 -> 1, of which waited for: 1 -> 1; matrix products, arithmetic and copies ran while one was open for 0% -> 1% of each run, Pallas kernels for 0% -> 0%
where the time goes in v4:
time: 66.4 us; the launch traced here: 65.7 us
  matrix products  18.3 us (28%)
  waiting for transfers between devices  13.3 us (20%)
  starting transfers between devices  11.5 us (17%)
  Pallas kernels  8.92 us (13%)
  local copies, waits for them, and re-layouts  6.9 us (10%)
  other arithmetic  5.72 us (9%)
  between operations  1.11 us (2%)
    dot_general x3, matrix products, lookup(): lax.dot_general(p, pick_row, dims, preferred_element_type=jnp.float32)  13.7 us
    all_to_all x1, waiting for transfers between devices, on_device(): lax.all_to_all(payload, ('sec', 'tile'), split_axis=0, concat_axis=0, til...  13.3 us
    all_to_all x1, starting transfers between devices, on_device(): lax.all_to_all(payload, ('sec', 'tile'), split_axis=0, concat_axis=0, til...  11.5 us
    pallas_call x1, Pallas kernels, regrid_back(): pl.pallas_call(back_kernel, out_shape=jax.ShapeDtypeStruct((2, nblocks, n...  8.92 us
    unnamed x36, local copies, waits for them, and re-layouts  3.49 us
    dot_general x1, matrix products, emit(): blasted = jnp.einsum('tkb,bnl->tknl', blast_table, salt, precision=high)  1.88 us
  transfers between devices with their start and end apart: 1, of which 1 were waited for; matrix products, arithmetic and copies ran while one was open for 1% of the time, Pallas kernels for 0%

profile of v4, /device:TPU:1, one launch (start us, length us, event | category | flops | bytes accessed | tf_op | source)
XLA Modules:
  0.0 65.7 jit_solution(5060255293817574081)
XLA Ops:
  0.7 1.0 %fusion.79 = (f32[1,256]{1,0:T(1,128)S(1)}, f32[1,256]{1,0:T(1,128)S(1)}, f32[1,256]{1,0:T(1,128)S(1)}, f32[1,256]{1,0:T(1,128)S(1)}, f32[1,256]{1,0:T(1,128)S(1...) fusion(f32[15,256]{1,0:T(8,128)} %param.26), kind=kLoop, calls=%fused_computation.247 | loop fusion | flops 2816 | bytes 24576 | tf_op jit(solution)/shard_map/slice | solution.py:62
  1.6 1.0 %broadcast_add_fusion.1 = (f32[1,256]{1,0:T(1,128)S(1)}, f32[1,256]{1,0:T(1,128)S(1)}, f32[1,256]{1,0:T(1,128)S(1)}, f32[1,256]{1,0:T(1,128)S(1)}, f32[1,256]{1,...) fusion(f32[15,256]{1,0:T(8,128)} %param.26), kind=kLoop, calls=%fused_computation.242 | loop fusion | flops 4608 | bytes 20480 | tf_op jit(solution)/shard_map/add;add | solution.py:63
  2.6 0.9 %fusion.80 = (f32[1,256]{1,0:T(1,128)S(1)}, f32[1,256]{1,0:T(1,128)S(1)}, f32[1,256]{1,0:T(1,128)S(1)}, f32[1,256]{1,0:T(1,128)S(1)}, f32[1,256]{1,0:T(1,128)S(1...) fusion(f32[15,256]{1,0:T(8,128)} %param.26), kind=kLoop, calls=%fused_computation.248 | loop fusion | bytes 14336 | tf_op jit(solution)/shard_map/slice | solution.py:62
  3.5 1.2 %fusion.78 = (f32[3,1,256]{2,1,0:T(1,128)S(1)}, f32[3,1,256]{2,1,0:T(1,128)S(1)}, f32[3,1,256]{2,1,0:T(1,128)S(1)}, f32[3,1,256]{2,1,0:T(1,128)S(1)}, f32[3,1,25...) fusion(f32[3,16,256]{2,1,0:T(8,128)} %param.24), kind=kLoop, calls=%fused_computation.246 | loop fusion | bytes 98304 | tf_op jit(solution)/shard_map/slice | solution.py:66
  5.2 0.9 %add_select_fusion.1 = (s32[16384]{0:T(1024)S(1)}, s32[16384]{0:T(1024)S(1)}) fusion(s32[128,128]{1,0:T(8,128)} %param.18), kind=kLoop, calls=%fused_computation.38 | loop fusion | flops 311296 | bytes 196608 | tf_op jit(solution)/shard_map/jit(remainder)/select_n | solution.py:36
  6.1 4.4 %convolution_bitcast_fusion = f32[128,16384]{1,0:T(8,128)S(1)} fusion(s32[16384]{0:T(1024)S(1)} %get-tuple-element.78, f32[32768]{0:T(1024)} %param.19), kind=kOutput, calls=%fused_computation | convolution fusion | flops 1078001664 | bytes 8585216 | tf_op jit(solution)/shard_map/dot_general | solution.py:46
  10.5 4.0 %convolution_add_fusion.1 = f32[128,16384]{1,0:T(8,128)S(1)} fusion(f32[128,16384]{1,0:T(8,128)S(1)} %convolution_bitcast_fusion, s32[16384]{0:T(1024)S(1)} %get-tuple-element.78, f32[32768]{0:T(1024)S(1)} %copy-done.1), kind=kOutput, calls=%fused_computation.3 | convolution fusion | flops 1080164352 | bytes 16973824 | tf_op jit(solution)/shard_map/dot_general | solution.py:46
  14.6 5.2 %fusion.5 = f32[16384]{0:T(1024)S(1)} fusion(f32[128,16384]{1,0:T(8,128)S(1)} %convolution_add_fusion.1, s32[16384]{0:T(1024)S(1)} %get-tuple-element.78, s32[16384]{0:T(1024)S(1)} %get-tuple-element.77, f32[32768]{0:T(1024)S(1)} %copy-done.1), kind=kOutput, calls=%fused_computation.12 | convolution fusion | flops 1086472192 | bytes 8716288 | tf_op jit(solution)/shard_map/dot_general | solution.py:46
  20.0 0.8 %fusion.9 = f32[12,128,128,1]{2,0,3,1:T(8,128)S(1)} fusion(f32[128,128]{1,0:T(8,128)S(1)} %mul.1901, f32[128,128]{1,0:T(8,128)S(1)} %add_sqrt_fusion, f32[12]{0:T(128)S(1)} %multiply_sqrt_fusion, f32[128,128]{1,0:T(8,128)S(1)} %copy-done.3, f32[128,128]{1,0:T(8,128)S(1)} %multiply_bitcast_fusion, s32[128,128]{1,0:T(8,128)S(1)} %copy-done.5, ...), kind=kOutput, calls=%fused_computation.19 | convolution fusion | flops 11075584 | bytes 1114352 | tf_op jit(solution)/shard_map/tb,tnl->bnl/dot_general | solution.py:18
  20.8 1.9 %fusion.4 = bf16[8,128,128]{2,0,1:T(8,128)(2,1)S(1)} fusion(f32[12,128,128,1]{2,0,3,1:T(8,128)S(1)} %fusion.9, f32[4,128,128]{2,0,1:T(4,128)S(1)} %fusion.15, f32[4,8,12]{2,1,0:T(8,128)S(1)} %copy-done), kind=kOutput, calls=%fused_computation.11 | convolution fusion | flops 76414976 | bytes 1312256 | tf_op jit(solution)/shard_map/tkb,bnl->tknl/dot_general | solution.py:27
  22.8 1.2 %fusion.12 = f32[128,8,256]{2,1,0:T(8,128)S(1)} fusion(bf16[128,128,256]{2,1,0:T(8,128)(2,1)S(1)} %bitcast.235, bf16[8,128,128]{2,0,1:T(8,128)(2,1)S(1)} %fusion.4), kind=kOutput, calls=%fused_computation.25 | convolution fusion | flops 67108864 | bytes 9699328 | tf_op jit(solution)/shard_map/gkl,gla->gka/dot_general | solution.py:153
  24.0 0.3 copy.151
  24.3 0.7 %convolution_convert_fusion = bf16[128,2048]{1,0:T(8,128)(2,1)S(1)} fusion(f32[128,2048]{1,0:T(8,128)S(1)} %bitcast.237, s32[128]{0:T(128)S(1)} %bitcast.407), kind=kOutput, calls=%fused_computation.9 | convolution fusion | flops 402931712 | bytes 1573376 | tf_op jit(solution)/shard_map/dot_general | solution.py:160
  25.2 0.5 broadcast.18967
  25.7 1.1 %reduce.2 = bf16[128,2560]{1,0:T(8,128)(2,1)S(1)} reduce(bf16[128,1,2560]{2,0,1:T(8,128)(2,1)S(1)} %maximum_bitcast_fusion, bf16[]{:T(256)} %broadcast.18967), dimensions={1}, to_apply=%copy.98.reduce_sub_computation | reduce | bytes 1310722 | tf_op jit(solution)/shard_map/all_to_all | solution.py:163
  26.8 1.0 %reshape.27193 = bf16[128,2,1280]{2,1,0:T(2,128)(2,1)} reshape(bf16[128,2560]{1,0:T(8,128)(2,1)S(1)} %reduce.2) | data formatting | bytes 1310720
  27.8 11.5 %all-to-all-start = ((bf16[128,2,1280]{2,1,0:T(2,128)(2,1)}), bf16[128,2,1280]{2,1,0:T(2,128)(2,1)S(1)}, u32[]{:S(2)}, u32[]{:S(2)}) async-start(bf16[128,2,1280]{2,1,0:T(2,128)(2,1)} %reshape.27193), calls=%async_computation | async-start | bytes 1310720 | tf_op jit(solution)/shard_map/all_to_all | solution.py:163
  39.3 0.7 %copy.99.dest_ref = s32[128,1]{1,0:T(8,128)} copy(s32[128,1]{0,1:T(1,128)S(1)} %copy-done.7) | data formatting | bytes 1024 | tf_op args[7]
  40.1 13.3 %all-to-all-done = bf16[128,2,1280]{2,1,0:T(2,128)(2,1)S(1)} async-done(((bf16[128,2,1280]{2,1,0:T(2,128)(2,1)}), bf16[128,2,1280]{2,1,0:T(2,128)(2,1)S(1)}, u32[]{:S(2)}, u32[]{:S(2)}) %all-to-all-start) | async-done | bytes 655392 | tf_op jit(solution)/shard_map/all_to_all | solution.py:163
  53.4 0.5 reshape.27194
  54.2 0.7 %slice.280.gathered_ref = bf16[128,512]{1,0:T(8,128)(2,1)} slice(bf16[128,2560]{1,0:T(8,128)(2,1)S(1)} %bitcast.239), slice={[0:128], [2048:2560]} | slice | bytes 262144 | tf_op jit(solution)/shard_map/slice | solution.py:165
  55.0 0.2 constant_dynamic-update-slice_fusion.15
  56.1 0.7 %copy.116 = f32[8,16,256]{2,1,0:T(8,128)} copy(f32[8,16,256]{2,0,1:T(8,128)S(1)} %constant_dynamic-update-slice_fusion) | data formatting | bytes 262144
  56.8 8.9 %shard_map.140 = f32[2,128,128]{2,1,0:T(8,128)} custom-call(s32[128,1]{1,0:T(8,128)} %copy.99.dest_ref, bf16[128,512]{1,0:T(8,128)(2,1)} %slice.280.gathered_ref, bf16[128,128,256]{2,1,0:T(8,128)(2,1)} %weights_ref.1, f32[128,128]{1,0:T(8,128)} %moist_ref.1), custom_call_target="tpu_custom_call" | custom-call | flops 67108864 | bytes 8585216 | tf_op jit(solution)/shard_map/pallas_call | solution.py:109
  (57 shorter events, 1.8 us)
Async XLA Ops:
  0.6 20.2 %copy-start = (f32[4,8,12]{2,1,0:T(8,128)S(1)}, f32[4,8,12]{2,1,0:T(8,128)}, u32[]{:S(2)}) copy-start(f32[4,8,12]{2,1,0:T(8,128)} %param.21) | copy-start | bytes 4612
  0.6 9.8 %copy-start.1 = (f32[32768]{0:T(1024)S(1)}, f32[32768]{0:T(1024)}, u32[]{:S(2)}) copy-start(f32[32768]{0:T(1024)} %param.19) | copy-start | bytes 393220
  10.5 12.2 %slice-start = ((s8[8388608]{0:T(1024)(128)(4,1)}), s8[4194304]{0:T(1024)(128)(4,1)S(1)}, s32[]{:S(2)}) async-start(s8[8388608]{0:T(1024)(128)(4,1)} %bitcast.234), calls=%async_computation.1 | async-start | bytes 8388608
  14.6 5.3 %copy-start.2 = (f32[128,128]{1,0:T(8,128)S(1)}, f32[128,128]{1,0:T(8,128)}, u32[]{:S(2)}) copy-start(f32[128,128]{1,0:T(8,128)} %moist_ref.1) | copy-start | bytes 196612
  14.6 5.3 %copy-start.3 = (f32[128,128]{1,0:T(8,128)S(1)}, f32[128,128]{1,0:T(8,128)}, u32[]{:S(2)}) copy-start(f32[128,128]{1,0:T(8,128)} %param.15) | copy-start | bytes 196612
  14.6 5.3 %copy-start.5 = (s32[128,128]{1,0:T(8,128)S(1)}, s32[128,128]{1,0:T(8,128)}, u32[]{:S(2)}) copy-start(s32[128,128]{1,0:T(8,128)} %param.17) | copy-start | bytes 196612
  14.6 5.4 %copy-start.8 = (f32[4,12]{1,0:T(4,128)S(1)}, f32[4,12]{1,0:T(4,128)}, u32[]{:S(2)}) copy-start(f32[4,12]{1,0:T(4,128)} %param.20) | copy-start | bytes 580
  14.6 8.1 %slice-start.1 = ((s8[8388608]{0:T(1024)(128)(4,1)}), s8[4194304]{0:T(1024)(128)(4,1)S(1)}, s32[]{:S(2)}) async-start(s8[8388608]{0:T(1024)(128)(4,1)} %bitcast.234), calls=%async_computation.2 | async-start | bytes 8388608
  22.8 1.6 %copy-start.7 = (s32[128,1]{0,1:T(1,128)S(1)}, s32[128,1]{0,1:T(1,128)}, u32[]{:S(2)}) copy-start(s32[128,1]{0,1:T(1,128)} %param.22) | copy-start | bytes 1540
  24.0 16.1 %copy-start.4 = (f32[8,16,256]{2,1,0:T(8,128)S(1)}, f32[8,16,256]{2,1,0:T(8,128)}, u32[]{:S(2)}) copy-start(f32[8,16,256]{2,1,0:T(8,128)} %param.25) | copy-start | bytes 393220
  24.0 30.9 %copy-start.6 = (f32[8]{0:T(128)S(1)}, f32[8]{0:T(128)}, u32[]{:S(2)}) copy-start(f32[8]{0:T(128)} %param.27) | copy-start | bytes 100
  27.8 25.7 %all-to-all-start = ((bf16[128,2,1280]{2,1,0:T(2,128)(2,1)}), bf16[128,2,1280]{2,1,0:T(2,128)(2,1)S(1)}, u32[]{:S(2)}, u32[]{:S(2)}) async-start(bf16[128,2,1280]{2,1,0:T(2,128)(2,1)} %reshape.27193), calls=%async_computation | async-start | bytes 1310720 | tf_op jit(solution)/shard_map/all_to_all | solution.py:163

commit v5 on v1

--- a/solution.py
+++ b/solution.py
@@ -33,20 +33,17 @@
     flat = index.reshape(-1)
     high_part = flat // 128
     low_part = flat % 128
-    pick_row = (lax.broadcasted_iota(jnp.int32, (rows, flat.shape[0]), 0) == high_part[None, :]).astype(jnp.bfloat16)
     grid = table.reshape(rows, 128)
     first_wide = lax.reduce_precision(grid, exponent_bits=8, mantissa_bits=7)
     rest = grid - first_wide
     second_wide = lax.reduce_precision(rest, exponent_bits=8, mantissa_bits=7)
-    first = first_wide.astype(jnp.bfloat16)
-    second = second_wide.astype(jnp.bfloat16)
-    third = (rest - second_wide).astype(jnp.bfloat16)
+    parts = jnp.concatenate([first_wide, second_wide, rest - second_wide], axis=0).astype(jnp.bfloat16)
+    pick_row = lax.broadcasted_iota(jnp.int32, (3 * rows, flat.shape[0]), 0) % rows == high_part[None, :]
+    pick_row = pick_row.astype(jnp.bfloat16)
     dims = (((0,), (0,)), ((), ()))
-    parts = [lax.dot_general(p, pick_row, dims, preferred_element_type=jnp.float32) for p in (first, second, third)]
-    row_values = (parts[0] + parts[1]) + parts[2]
+    row_values = lax.dot_general(parts, pick_row, dims, preferred_element_type=jnp.float32)
     pick_lane = lax.broadcasted_iota(jnp.int32, row_values.shape, 0) == low_part[None, :]
     return jnp.sum(jnp.where(pick_lane, row_values, 0.0), axis=0).reshape(index.shape)
-
 
 def solve(right_side, coupling, sinking):
     levels = right_side.shape[1]

time: 63.5 us -> 67 us (1.055)
  other arithmetic: 6.6 us -> 9.3 us
  matrix products: 24.1 us -> 24.9 us
    dot_general x1, matrix products: 1.19 us -> 4.57 us  [on_device(): jnp.einsum('gkl,gla->gka', emission, regrid_w, preferred_element_type=jnp...]
    dot_general x3 -> x1, matrix products: 13.7 us -> 10.8 us  [lookup(): lax.dot_general(parts, pick_row, dims, preferred_element_type=jnp.float32)]
    another operation x1 -> x2, other arithmetic: 0.01 us -> 0.96 us
    mul x1, other arithmetic: 0.01 us -> 0.93 us  [emit(): speed * speed - thresh * thresh]
    sqrt x1, other arithmetic: 0.03 us -> 0.87 us  [emit(): jnp.sqrt(1.0 + 12.1 * moist_rows)[None]]
    unnamed x35 -> x29, local copies, waits for them, and re-layouts: 2.76 us -> 2.75 us
where the time goes in v5:
time: 67 us; the launch traced here: 66.3 us
  matrix products  24.9 us (37%)
  waiting for transfers between devices  14 us (21%)
  starting transfers between devices  11.5 us (17%)
  other arithmetic  9.3 us (14%)
  local copies, waits for them, and re-layouts  5.53 us (8%)
  between operations  1.11 us (2%)
    all_to_all x1, waiting for transfers between devices, on_device(): lax.all_to_all(payload, ('sec', 'tile'), split_axis=0, concat_axis=0, til...  14 us
    all_to_all x1, starting transfers between devices, on_device(): lax.all_to_all(payload, ('sec', 'tile'), split_axis=0, concat_axis=0, til...  11.5 us
    dot_general x1, matrix products, lookup(): lax.dot_general(parts, pick_row, dims, preferred_element_type=jnp.float32)  10.8 us
    dot_general x1, matrix products, on_device(): jnp.einsum('gla,gka->kgl', regrid_w, picked, preferred_element_type=jnp.f...  5.63 us
    dot_general x1, matrix products, on_device(): jnp.einsum('gkl,gla->gka', emission, regrid_w, preferred_element_type=jnp...  4.57 us
    unnamed x29, local copies, waits for them, and re-layouts  2.75 us
    dot_general x1, matrix products, emit(): blasted = jnp.einsum('tkb,bnl->tknl', blast_table, salt, precision=high)  2.07 us
  transfers between devices with their start and end apart: 1, of which 1 were waited for; matrix products, arithmetic and copies ran while one was open for 0% of the time, Pallas kernels for 0%

profile of v5, /device:TPU:1, one launch (start us, length us, event | category | flops | bytes accessed | tf_op | source)
XLA Modules:
  0.0 66.3 jit_solution(1341995797671603882)
XLA Ops:
  0.7 1.0 %fusion.96 = (f32[1,256]{1,0:T(1,128)S(1)}, f32[1,256]{1,0:T(1,128)S(1)}, f32[1,256]{1,0:T(1,128)S(1)}, f32[1,256]{1,0:T(1,128)S(1)}, f32[1,256]{1,0:T(1,128)S(1...) fusion(f32[15,256]{1,0:T(8,128)} %param.26), kind=kLoop, calls=%fused_computation.269 | loop fusion | flops 2816 | bytes 24576 | tf_op jit(solution)/shard_map/slice | solution.py:58
  1.7 0.9 %fusion.97 = (f32[1,256]{1,0:T(1,128)S(1)}, f32[1,256]{1,0:T(1,128)S(1)}, f32[1,256]{1,0:T(1,128)S(1)}, f32[1,256]{1,0:T(1,128)S(1)}, f32[1,256]{1,0:T(1,128)S(1...) fusion(f32[15,256]{1,0:T(8,128)} %param.26), kind=kLoop, calls=%fused_computation.270 | loop fusion | bytes 14336 | tf_op jit(solution)/shard_map/slice | solution.py:58
  2.6 1.0 %broadcast_add_fusion.1 = (f32[1,256]{1,0:T(1,128)S(1)}, f32[1,256]{1,0:T(1,128)S(1)}, f32[1,256]{1,0:T(1,128)S(1)}, f32[1,256]{1,0:T(1,128)S(1)}, f32[1,256]{1,...) fusion(f32[15,256]{1,0:T(8,128)} %param.26), kind=kLoop, calls=%fused_computation.261 | loop fusion | flops 4608 | bytes 20480 | tf_op jit(solution)/shard_map/add;add | solution.py:59
  3.6 1.2 %fusion.95 = (f32[3,1,256]{2,1,0:T(1,128)S(1)}, f32[3,1,256]{2,1,0:T(1,128)S(1)}, f32[3,1,256]{2,1,0:T(1,128)S(1)}, f32[3,1,256]{2,1,0:T(1,128)S(1)}, f32[3,1,25...) fusion(f32[3,16,256]{2,1,0:T(8,128)} %param.24), kind=kLoop, calls=%fused_computation.268 | loop fusion | bytes 98304 | tf_op jit(solution)/shard_map/slice | solution.py:62
  5.1 0.9 %mul.1908 = f32[128,128]{1,0:T(8,128)S(1)} multiply(f32[128,128]{1,0:T(8,128)} %param.15, f32[128,128]{1,0:T(8,128)} %param.15) | non-fusion elementwise | flops 16384 | bytes 196608 | tf_op jit(solution)/shard_map/mul | solution.py:24
  6.1 0.9 %add_sqrt_fusion = f32[128,128]{1,0:T(8,128)S(1)} fusion(f32[128,128]{1,0:T(8,128)} %param.16), kind=kLoop, calls=%fused_computation.56 | loop fusion | flops 32768 | bytes 131072 | tf_op jit(solution)/shard_map/sqrt | solution.py:14
  6.9 0.9 %add_select_fusion.1 = (s32[16384]{0:T(1024)S(1)}, s32[16384]{0:T(1024)S(1)}) fusion(s32[128,128]{1,0:T(8,128)} %param.18), kind=kLoop, calls=%fused_computation.47 | loop fusion | flops 311296 | bytes 196608 | tf_op jit(solution)/shard_map/jit(remainder)/select_n | solution.py:35
  7.8 0.9 %reduce-precision_convert_fusion.1 = (bf16[256,128]{1,0:T(8,128)(2,1)S(1)}, bf16[256,128]{1,0:T(8,128)(2,1)S(1)}, bf16[256,128]{1,0:T(8,128)(2,1)S(1)}) fusion(f32[32768]{0:T(1024)} %param.19), kind=kLoop, calls=%fused_computation.40 | loop fusion | flops 229376 | bytes 327680 | tf_op jit(solution)/shard_map/convert.3
  8.8 10.8 %fusion.7 = f32[16384]{0:T(1024)S(1)} fusion(s32[16384]{0:T(1024)S(1)} %get-tuple-element.84, s32[768]{0:T(1024)S(1)} %get-tuple-element.132, s32[768]{0:T(1024)S(1)} %get-tuple-element.133, pred[768]{0:T(1024)(128)(4,1)S(1)} %fusion.82, s32[16384]{0:T(1024)S(1)} %get-tuple-element.83, bf16[256,128]{1,0:T(8,128)(2,1)S(1)} %get-tuple-element.81, ...), kind=kOutput, calls=%fused_computation.11 | convolution fusion | flops 3253256192 | bytes 400128 | tf_op jit(solution)/shard_map/dot_general | solution.py:44
  19.8 0.8 %fusion.11 = f32[12,128,128,1]{2,0,3,1:T(8,128)S(1)} fusion(f32[128,128]{1,0:T(8,128)S(1)} %mul.1908, f32[128,128]{1,0:T(8,128)S(1)} %add_sqrt_fusion, f32[12]{0:T(128)S(1)} %multiply_sqrt_fusion, f32[128,128]{1,0:T(8,128)S(1)} %copy-done.1, f32[128,128]{1,0:T(8,128)S(1)} %multiply_bitcast_fusion, s32[128,128]{1,0:T(8,128)S(1)} %copy-done.4, ...), kind=kOutput, calls=%fused_computation.18 | convolution fusion | flops 11075584 | bytes 1114352 | tf_op jit(solution)/shard_map/tb,tnl->bnl/dot_general | solution.py:17
  20.6 2.1 %fusion.6 = bf16[8,128,128]{2,0,1:T(8,128)(2,1)S(1)} fusion(f32[12,128,128,1]{2,0,3,1:T(8,128)S(1)} %fusion.11, f32[4,128,128]{2,0,1:T(4,128)S(1)} %fusion.18, f32[4,8,12]{2,1,0:T(8,128)S(1)} %copy-done), kind=kOutput, calls=%fused_computation.10 | convolution fusion | flops 76414976 | bytes 1312256 | tf_op jit(solution)/shard_map/tkb,bnl->tknl/dot_general | solution.py:26
  22.7 4.6 %fusion.14 = f32[128,8,256]{2,1,0:T(8,128)S(1)} fusion(bf16[128,128,256]{2,1,0:T(8,128)(2,1)} %param.23, bf16[8,128,128]{2,0,1:T(8,128)(2,1)S(1)} %fusion.6), kind=kOutput, calls=%fused_computation.26 | convolution fusion | flops 67108864 | bytes 9699328 | tf_op jit(solution)/shard_map/gkl,gla->gka/dot_general | solution.py:107
  27.3 0.3 copy.163
  27.7 0.7 %convolution_convert_fusion = bf16[128,2048]{1,0:T(8,128)(2,1)S(1)} fusion(f32[128,2048]{1,0:T(8,128)S(1)} %bitcast.240, s32[128]{0:T(128)S(1)} %bitcast.413), kind=kOutput, calls=%fused_computation.8 | convolution fusion | flops 402931712 | bytes 1573376 | tf_op jit(solution)/shard_map/dot_general | solution.py:114
  28.5 0.5 broadcast.18994
  29.0 1.1 %reduce.2 = bf16[128,2560]{1,0:T(8,128)(2,1)S(1)} reduce(bf16[128,1,2560]{2,0,1:T(8,128)(2,1)S(1)} %maximum_bitcast_fusion, bf16[]{:T(256)} %broadcast.18994), dimensions={1}, to_apply=%copy.106.reduce_sub_computation | reduce | bytes 1310722 | tf_op jit(solution)/shard_map/all_to_all | solution.py:117
  30.1 1.0 %reshape.27200 = bf16[128,2,1280]{2,1,0:T(2,128)(2,1)} reshape(bf16[128,2560]{1,0:T(8,128)(2,1)S(1)} %reduce.2) | data formatting | bytes 1310720
  31.1 11.5 %all-to-all-start = ((bf16[128,2,1280]{2,1,0:T(2,128)(2,1)}), bf16[128,2,1280]{2,1,0:T(2,128)(2,1)S(1)}, u32[]{:S(2)}, u32[]{:S(2)}) async-start(bf16[128,2,1280]{2,1,0:T(2,128)(2,1)} %reshape.27200), calls=%async_computation | async-start | bytes 1310720 | tf_op jit(solution)/shard_map/all_to_all | solution.py:117
  42.8 14.0 %all-to-all-done = bf16[128,2,1280]{2,1,0:T(2,128)(2,1)S(1)} async-done(((bf16[128,2,1280]{2,1,0:T(2,128)(2,1)}), bf16[128,2,1280]{2,1,0:T(2,128)(2,1)S(1)}, u32[]{:S(2)}, u32[]{:S(2)}) %all-to-all-start) | async-done | bytes 655392 | tf_op jit(solution)/shard_map/all_to_all | solution.py:117
  56.8 0.5 reshape.27201
  57.4 0.2 convolution_convert_fusion.1
  57.8 5.6 %convolution_bitcast_fusion = f32[3,128,128]{2,0,1:T(4,128)S(1)} fusion(bf16[128,128,256]{2,1,0:T(8,128)(2,1)} %param.23, bf16[128,2,256]{2,1,0:T(2,128)(2,1)S(1)} %reshape.27195), kind=kOutput, calls=%fused_computation.19 | convolution fusion | flops 25165824 | bytes 8716288 | tf_op jit(solution)/shard_map/gla,gka->kgl/dot_general | solution.py:126
  64.9 0.7 %copy.126 = f32[8,16,256]{2,1,0:T(8,128)} copy(f32[8,16,256]{2,0,1:T(8,128)S(1)} %constant_dynamic-update-slice_fusion) | data formatting | bytes 262144
  65.7 0.7 %pad_maximum_fusion = f32[2,128,128]{2,1,0:T(8,128)} fusion(f32[1,128,128]{2,1,0:T(8,128)S(1)} %add_bitcast_fusion, f32[1,128,128]{2,1,0:T(8,128)S(1)} %div.1527), kind=kLoop, calls=%fused_computation.43 | loop fusion | flops 32768 | bytes 262144 | tf_op jit(solution)/shard_map/stack | solution.py:128
  (55 shorter events, 2.2 us)
Async XLA Ops:
  0.6 20.0 %copy-start = (f32[4,8,12]{2,1,0:T(8,128)S(1)}, f32[4,8,12]{2,1,0:T(8,128)}, u32[]{:S(2)}) copy-start(f32[4,8,12]{2,1,0:T(8,128)} %param.21) | copy-start | bytes 4612
  8.8 10.9 %copy-start.4 = (s32[128,128]{1,0:T(8,128)S(1)}, s32[128,128]{1,0:T(8,128)}, u32[]{:S(2)}) copy-start(s32[128,128]{1,0:T(8,128)} %param.17) | copy-start | bytes 196612
  8.8 10.9 %copy-start.1 = (f32[128,128]{1,0:T(8,128)S(1)}, f32[128,128]{1,0:T(8,128)}, u32[]{:S(2)}) copy-start(f32[128,128]{1,0:T(8,128)} %param.15) | copy-start | bytes 196612
  8.8 10.9 %copy-start.7 = (f32[4,12]{1,0:T(4,128)S(1)}, f32[4,12]{1,0:T(4,128)}, u32[]{:S(2)}) copy-start(f32[4,12]{1,0:T(4,128)} %param.20) | copy-start | bytes 580
  22.7 5.0 %copy-start.6 = (s32[128,1]{0,1:T(1,128)S(1)}, s32[128,1]{0,1:T(1,128)}, u32[]{:S(2)}) copy-start(s32[128,1]{0,1:T(1,128)} %param.22) | copy-start | bytes 1540
  27.3 15.4 %copy-start.3 = (f32[8,16,256]{2,1,0:T(8,128)S(1)}, f32[8,16,256]{2,1,0:T(8,128)}, u32[]{:S(2)}) copy-start(f32[8,16,256]{2,1,0:T(8,128)} %param.25) | copy-start | bytes 393220
  30.1 33.5 %copy-start.2 = (f32[128,128]{1,0:T(8,128)S(1)}, f32[128,128]{1,0:T(8,128)}, u32[]{:S(2)}) copy-start(f32[128,128]{1,0:T(8,128)} %param.16) | copy-start | bytes 196612
  30.1 33.5 %copy-start.5 = (f32[8]{0:T(128)S(1)}, f32[8]{0:T(128)}, u32[]{:S(2)}) copy-start(f32[8]{0:T(128)} %param.27) | copy-start | bytes 100
  31.1 25.6 %all-to-all-start = ((bf16[128,2,1280]{2,1,0:T(2,128)(2,1)}), bf16[128,2,1280]{2,1,0:T(2,128)(2,1)S(1)}, u32[]{:S(2)}, u32[]{:S(2)}) async-start(bf16[128,2,1280]{2,1,0:T(2,128)(2,1)} %reshape.27200), calls=%async_computation | async-start | bytes 1310720 | tf_op jit(solution)/shard_map/all_to_all | solution.py:117

commit v6 on v5

--- a/solution.py
+++ b/solution.py
@@ -38,12 +38,15 @@
     rest = grid - first_wide
     second_wide = lax.reduce_precision(rest, exponent_bits=8, mantissa_bits=7)
     parts = jnp.concatenate([first_wide, second_wide, rest - second_wide], axis=0).astype(jnp.bfloat16)
-    pick_row = lax.broadcasted_iota(jnp.int32, (3 * rows, flat.shape[0]), 0) % rows == high_part[None, :]
-    pick_row = pick_row.astype(jnp.bfloat16)
     dims = (((0,), (0,)), ((), ()))
-    row_values = lax.dot_general(parts, pick_row, dims, preferred_element_type=jnp.float32)
-    pick_lane = lax.broadcasted_iota(jnp.int32, row_values.shape, 0) == low_part[None, :]
-    return jnp.sum(jnp.where(pick_lane, row_values, 0.0), axis=0).reshape(index.shape)
+    halves = []
+    for high_half, low_half in zip(jnp.split(high_part, 2), jnp.split(low_part, 2)):
+        pick_row = lax.broadcasted_iota(jnp.int32, (3 * rows, high_half.shape[0]), 0) % rows == high_half[None, :]
+        pick_row = pick_row.astype(jnp.bfloat16)
+        row_values = lax.dot_general(parts, pick_row, dims, preferred_element_type=jnp.float32)
+        pick_lane = lax.broadcasted_iota(jnp.int32, row_values.shape, 0) == low_half[None, :]
+        halves.append(jnp.sum(jnp.where(pick_lane, row_values, 0.0), axis=0))
+    return jnp.concatenate(halves).reshape(index.shape)
 
 def solve(right_side, coupling, sinking):
     levels = right_side.shape[1]
@@ -111,9 +114,14 @@
     targets = dest_tile[:, 0]
     onehot = (targets[:, None] == jnp.arange(devices)[None, :]).astype(jnp.float32)
     dims = (((0,), (0,)), ((), ()))
-    outgoing = lax.dot_general(onehot, flat_flux, dims, precision=high)
-    spread = jnp.broadcast_to(surface, (devices, 2 * columns))
-    payload = jnp.concatenate([outgoing.astype(jnp.bfloat16), spread], axis=1)
+    surface_row = jnp.concatenate(
+        [jnp.zeros((1, nbins * columns), jnp.float32), surface.astype(jnp.float32)], axis=1
+    )
+    stacked = jnp.concatenate(
+        [jnp.pad(flat_flux, ((0, 0), (0, 2 * columns))), surface_row], axis=0
+    )
+    placing = jnp.concatenate([onehot, jnp.ones((1, devices), jnp.float32)], axis=0)
+    payload = lax.dot_general(placing, stacked, dims, precision=high).astype(jnp.bfloat16)
     incoming = lax.all_to_all(payload, ("sec", "tile"), split_axis=0, concat_axis=0, tiled=True)
     flux = jnp.sum(incoming[:, : nbins * columns].astype(jnp.float32), axis=0).reshape(nbins, columns)
     gathered = incoming[:, nbins * columns :]

time: 67 us -> 65.2 us (0.973)
  matrix products: 24.9 us -> 22.1 us
  other arithmetic: 9.3 us -> 10.1 us
    dot_general x1, matrix products: 4.57 us -> 1.19 us  [on_device(): jnp.einsum('gkl,gla->gka', emission, regrid_w, preferred_element_type=jnp...]
    convert_element_type x1, other arithmetic: 0.06 us -> 0.9 us  [emit(): onehot = (texture_rows[None] == classes[:, None, None]).astype(jnp.float32)]
    dot_general x1 -> x2, matrix products: 10.8 us -> 10.8 us  [lookup(): lax.dot_general(parts, pick_row, dims, preferred_element_type=jnp.float32)]
    unnamed x29 -> x33, local copies, waits for them, and re-layouts: 2.75 us -> 2.75 us
where the time goes in v6:
time: 65.2 us; the launch traced here: 64.5 us
  matrix products  22.1 us (34%)
  waiting for transfers between devices  14 us (21%)
  starting transfers between devices  11.5 us (18%)
  other arithmetic  10.1 us (15%)
  local copies, waits for them, and re-layouts  5.54 us (8%)
  between operations  1.17 us (2%)
    all_to_all x1, waiting for transfers between devices, on_device(): lax.all_to_all(payload, ('sec', 'tile'), split_axis=0, concat_axis=0, til...  14 us
    all_to_all x1, starting transfers between devices, on_device(): lax.all_to_all(payload, ('sec', 'tile'), split_axis=0, concat_axis=0, til...  11.5 us
    dot_general x2, matrix products, lookup(): lax.dot_general(parts, pick_row, dims, preferred_element_type=jnp.float32)  10.8 us
    dot_general x1, matrix products, on_device(): jnp.einsum('gla,gka->kgl', regrid_w, picked, preferred_element_type=jnp.f...  5.66 us
    unnamed x33, local copies, waits for them, and re-layouts  2.75 us
    dot_general x1, matrix products, emit(): blasted = jnp.einsum('tkb,bnl->tknl', blast_table, salt, precision=high)  2.08 us
  transfers between devices with their start and end apart: 1, of which 1 were waited for; matrix products, arithmetic and copies ran while one was open for 0% of the time, Pallas kernels for 0%

profile of v6, /device:TPU:1, one launch (start us, length us, event | category | flops | bytes accessed | tf_op | source)
XLA Modules:
  0.0 64.5 jit_solution(7879346736068858186)
XLA Ops:
  0.7 1.0 %fusion.112 = (f32[1,256]{1,0:T(1,128)S(1)}, f32[1,256]{1,0:T(1,128)S(1)}, f32[1,256]{1,0:T(1,128)S(1)}, f32[1,256]{1,0:T(1,128)S(1)}, f32[1,256]{1,0:T(1,128)S(...) fusion(f32[15,256]{1,0:T(8,128)} %param.26), kind=kLoop, calls=%fused_computation.288 | loop fusion | flops 2816 | bytes 24576 | tf_op jit(solution)/shard_map/slice | solution.py:61
  1.7 0.9 %fusion.113 = (f32[1,256]{1,0:T(1,128)S(1)}, f32[1,256]{1,0:T(1,128)S(1)}, f32[1,256]{1,0:T(1,128)S(1)}, f32[1,256]{1,0:T(1,128)S(1)}, f32[1,256]{1,0:T(1,128)S(...) fusion(f32[15,256]{1,0:T(8,128)} %param.26), kind=kLoop, calls=%fused_computation.289 | loop fusion | bytes 14336 | tf_op jit(solution)/shard_map/slice | solution.py:61
  2.6 1.0 %broadcast_add_fusion.1 = (f32[1,256]{1,0:T(1,128)S(1)}, f32[1,256]{1,0:T(1,128)S(1)}, f32[1,256]{1,0:T(1,128)S(1)}, f32[1,256]{1,0:T(1,128)S(1)}, f32[1,256]{1,...) fusion(f32[15,256]{1,0:T(8,128)} %param.26), kind=kLoop, calls=%fused_computation.273 | loop fusion | flops 4608 | bytes 20480 | tf_op jit(solution)/shard_map/add;add | solution.py:62
  3.6 1.2 %fusion.111 = (f32[3,1,256]{2,1,0:T(1,128)S(1)}, f32[3,1,256]{2,1,0:T(1,128)S(1)}, f32[3,1,256]{2,1,0:T(1,128)S(1)}, f32[3,1,256]{2,1,0:T(1,128)S(1)}, f32[3,1,2...) fusion(f32[3,16,256]{2,1,0:T(8,128)} %param.24), kind=kLoop, calls=%fused_computation.287 | loop fusion | bytes 98304 | tf_op jit(solution)/shard_map/slice | solution.py:65
  5.1 0.9 %mul.1905 = f32[128,128]{1,0:T(8,128)S(1)} multiply(f32[128,128]{1,0:T(8,128)} %param.15, f32[128,128]{1,0:T(8,128)} %param.15) | non-fusion elementwise | flops 16384 | bytes 196608 | tf_op jit(solution)/shard_map/mul | solution.py:24
  6.1 0.9 %add_sqrt_fusion = f32[128,128]{1,0:T(8,128)S(1)} fusion(f32[128,128]{1,0:T(8,128)} %param.16), kind=kLoop, calls=%fused_computation.69 | loop fusion | flops 32768 | bytes 131072 | tf_op jit(solution)/shard_map/sqrt | solution.py:14
  6.9 0.9 %add_select_fusion.1 = (s32[16384]{0:T(1024)S(1)}, s32[16384]{0:T(1024)S(1)}) fusion(s32[128,128]{1,0:T(8,128)} %param.18), kind=kLoop, calls=%fused_computation.58 | loop fusion | flops 311296 | bytes 196608 | tf_op jit(solution)/shard_map/jit(remainder)/select_n | solution.py:35
  7.8 0.9 %reduce-precision_convert_fusion.1 = (bf16[256,128]{1,0:T(8,128)(2,1)S(1)}, bf16[256,128]{1,0:T(8,128)(2,1)S(1)}, bf16[256,128]{1,0:T(8,128)(2,1)S(1)}) fusion(f32[32768]{0:T(1024)} %param.19), kind=kLoop, calls=%fused_computation.51 | loop fusion | flops 229376 | bytes 327680 | tf_op jit(solution)/shard_map/convert.6
  8.8 0.9 %fusion.30 = f32[4,128,128]{2,0,1:T(4,128)S(1)} fusion(s32[128,128]{1,0:T(8,128)} %param.17), kind=kLoop, calls=%fused_computation.46 | loop fusion | flops 131072 | bytes 327680 | tf_op jit(solution)/shard_map/convert_element_type | solution.py:16
  9.7 5.4 %fusion.15 = f32[8192]{0:T(1024)S(1)} fusion(s32[8192]{0:T(1024)S(1)} %get-tuple-element.136, s32[768]{0:T(1024)S(1)} %get-tuple-element.138, s32[768]{0:T(1024)S(1)} %get-tuple-element.139, pred[768]{0:T(1024)(128)(4,1)S(1)} %fusion.91, s32[8192]{0:T(1024)S(1)} %get-tuple-element.84, bf16[256,128]{1,0:T(8,128)(2,1)S(1)} %get-tuple-element.81, ...), kind=kOutput, calls=%fused_computation.23 | convolution fusion | flops 1626923008 | bytes 301824 | tf_op jit(solution)/shard_map/dot_general | solution.py:46
  15.2 5.4 %fusion.14 = f32[8192]{0:T(1024)S(1)} fusion(s32[8192]{0:T(1024)S(1)} %get-tuple-element.137, s32[768]{0:T(1024)S(1)} %get-tuple-element.138, s32[768]{0:T(1024)S(1)} %get-tuple-element.139, pred[768]{0:T(1024)(128)(4,1)S(1)} %fusion.91, s32[8192]{0:T(1024)S(1)} %get-tuple-element.83, bf16[256,128]{1,0:T(8,128)(2,1)S(1)} %get-tuple-element.81, ...), kind=kOutput, calls=%fused_computation.22 | convolution fusion | flops 1626923008 | bytes 301824 | tf_op jit(solution)/shard_map/dot_general | solution.py:46
  20.7 0.8 %fusion.21 = f32[12,128,128,1]{2,0,3,1:T(8,128)S(1)} fusion(f32[128,128]{1,0:T(8,128)S(1)} %mul.1905, f32[128,128]{1,0:T(8,128)S(1)} %add_sqrt_fusion, f32[12]{0:T(128)S(1)} %multiply_sqrt_fusion, f32[128,128]{1,0:T(8,128)S(1)} %copy-done.1, f32[128,128]{1,0:T(8,128)S(1)} %maximum_multiply_fusion, s32[128,128]{1,0:T(8,128)S(1)} %copy-done.4, ...), kind=kOutput, calls=%fused_computation.32 | convolution fusion | flops 11075584 | bytes 1114352 | tf_op jit(solution)/shard_map/tb,tnl->bnl/dot_general | solution.py:17
  21.5 2.1 %fusion.13 = bf16[8,128,128]{2,0,1:T(8,128)(2,1)S(1)} fusion(f32[12,128,128,1]{2,0,3,1:T(8,128)S(1)} %fusion.21, f32[4,128,128]{2,0,1:T(4,128)S(1)} %fusion.30, f32[4,8,12]{2,1,0:T(8,128)S(1)} %copy-done), kind=kOutput, calls=%fused_computation.19 | convolution fusion | flops 76414976 | bytes 1312256 | tf_op jit(solution)/shard_map/tkb,bnl->tknl/dot_general | solution.py:26
  23.6 1.2 %fusion.26 = f32[128,8,256]{2,1,0:T(8,128)S(1)} fusion(bf16[128,128,256]{2,1,0:T(8,128)(2,1)S(1)} %bitcast.240, bf16[8,128,128]{2,0,1:T(8,128)(2,1)S(1)} %fusion.13), kind=kOutput, calls=%fused_computation.41 | convolution fusion | flops 67108864 | bytes 9699328 | tf_op jit(solution)/shard_map/gkl,gla->gka/dot_general | solution.py:110
  25.3 1.3 %fusion.12 = bf16[128,1,2560]{2,0,1:T(8,128)(2,1)S(1)} fusion(f32[128,2048]{1,0:T(8,128)S(1)} %bitcast.244, f32[1,2560]{1,0:T(1,128)S(1)} %pad_convert_fusion, f32[128,128]{1,0:T(8,128)S(1)} %fusion.37), kind=kOutput, calls=%fused_computation.17 | convolution fusion | flops 508567040 | bytes 1779712 | tf_op jit(solution)/shard_map/dot_general | solution.py:124
  26.6 0.5 broadcast.18967
  27.1 1.1 %reduce.2 = bf16[128,2560]{1,0:T(8,128)(2,1)S(1)} reduce(bf16[128,1,2560]{2,0,1:T(8,128)(2,1)S(1)} %fusion.12, bf16[]{:T(256)} %broadcast.18967), dimensions={1}, to_apply=%copy.106.reduce_sub_computation | reduce | bytes 1310722 | tf_op jit(solution)/shard_map/all_to_all | solution.py:125
  28.2 1.0 %reshape.27167 = bf16[128,2,1280]{2,1,0:T(2,128)(2,1)} reshape(bf16[128,2560]{1,0:T(8,128)(2,1)S(1)} %reduce.2) | data formatting | bytes 1310720
  29.2 11.5 %all-to-all-start = ((bf16[128,2,1280]{2,1,0:T(2,128)(2,1)}), bf16[128,2,1280]{2,1,0:T(2,128)(2,1)S(1)}, u32[]{:S(2)}, u32[]{:S(2)}) async-start(bf16[128,2,1280]{2,1,0:T(2,128)(2,1)} %reshape.27167), calls=%async_computation | async-start | bytes 1310720 | tf_op jit(solution)/shard_map/all_to_all | solution.py:125
  40.8 14.0 %all-to-all-done = bf16[128,2,1280]{2,1,0:T(2,128)(2,1)S(1)} async-done(((bf16[128,2,1280]{2,1,0:T(2,128)(2,1)}), bf16[128,2,1280]{2,1,0:T(2,128)(2,1)S(1)}, u32[]{:S(2)}, u32[]{:S(2)}) %all-to-all-start) | async-done | bytes 655392 | tf_op jit(solution)/shard_map/all_to_all | solution.py:125
  54.9 0.5 reshape.27168
  55.9 5.7 %convolution_bitcast_fusion = f32[3,128,128]{2,0,1:T(4,128)S(1)} fusion(bf16[128,128,256]{2,1,0:T(8,128)(2,1)} %param.23, bf16[128,2,256]{2,1,0:T(2,128)(2,1)S(1)} %reshape.27163), kind=kOutput, calls=%fused_computation.33 | convolution fusion | flops 25165824 | bytes 8716288 | tf_op jit(solution)/shard_map/gla,gka->kgl/dot_general | solution.py:134
  63.1 0.7 %copy.126 = f32[8,16,256]{2,1,0:T(8,128)} copy(f32[8,16,256]{2,0,1:T(8,128)S(1)} %constant_dynamic-update-slice_fusion) | data formatting | bytes 262144
  63.8 0.7 %pad_maximum_fusion.1 = f32[2,128,128]{2,1,0:T(8,128)} fusion(f32[1,128,128]{2,1,0:T(8,128)S(1)} %add_bitcast_fusion, f32[1,128,128]{2,1,0:T(8,128)S(1)} %div.1527), kind=kLoop, calls=%fused_computation.54 | loop fusion | flops 32768 | bytes 262144 | tf_op jit(solution)/shard_map/stack | solution.py:136
  (62 shorter events, 2.7 us)
Async XLA Ops:
  0.6 20.9 %copy-start = (f32[4,8,12]{2,1,0:T(8,128)S(1)}, f32[4,8,12]{2,1,0:T(8,128)}, u32[]{:S(2)}) copy-start(f32[4,8,12]{2,1,0:T(8,128)} %param.21) | copy-start | bytes 4612
  15.1 8.5 %slice-start = ((s8[8388608]{0:T(1024)(128)(4,1)}), s8[4194304]{0:T(1024)(128)(4,1)S(1)}, s32[]{:S(2)}) async-start(s8[8388608]{0:T(1024)(128)(4,1)} %bitcast.239), calls=%async_computation.1 | async-start | bytes 8388608
  15.1 5.5 %copy-start.1 = (f32[128,128]{1,0:T(8,128)S(1)}, f32[128,128]{1,0:T(8,128)}, u32[]{:S(2)}) copy-start(f32[128,128]{1,0:T(8,128)} %param.15) | copy-start | bytes 196612
  15.2 5.5 %copy-start.4 = (s32[128,128]{1,0:T(8,128)S(1)}, s32[128,128]{1,0:T(8,128)}, u32[]{:S(2)}) copy-start(s32[128,128]{1,0:T(8,128)} %param.17) | copy-start | bytes 196612
  15.2 5.5 %copy-start.7 = (f32[4,12]{1,0:T(4,128)S(1)}, f32[4,12]{1,0:T(4,128)}, u32[]{:S(2)}) copy-start(f32[4,12]{1,0:T(4,128)} %param.20) | copy-start | bytes 580
  15.2 8.4 %slice-start.1 = ((s8[8388608]{0:T(1024)(128)(4,1)}), s8[4194304]{0:T(1024)(128)(4,1)S(1)}, s32[]{:S(2)}) async-start(s8[8388608]{0:T(1024)(128)(4,1)} %bitcast.239), calls=%async_computation.2 | async-start | bytes 8388608
  23.6 1.6 %copy-start.6 = (s32[128,1]{0,1:T(1,128)S(1)}, s32[128,1]{0,1:T(1,128)}, u32[]{:S(2)}) copy-start(s32[128,1]{0,1:T(1,128)} %param.22) | copy-start | bytes 1540
  24.8 15.9 %copy-start.3 = (f32[8,16,256]{2,1,0:T(8,128)S(1)}, f32[8,16,256]{2,1,0:T(8,128)}, u32[]{:S(2)}) copy-start(f32[8,16,256]{2,1,0:T(8,128)} %param.25) | copy-start | bytes 393220
  29.2 25.6 %all-to-all-start = ((bf16[128,2,1280]{2,1,0:T(2,128)(2,1)}), bf16[128,2,1280]{2,1,0:T(2,128)(2,1)S(1)}, u32[]{:S(2)}, u32[]{:S(2)}) async-start(bf16[128,2,1280]{2,1,0:T(2,128)(2,1)} %reshape.27167), calls=%async_computation | async-start | bytes 1310720 | tf_op jit(solution)/shard_map/all_to_all | solution.py:125
  55.9 5.9 %copy-start.2 = (f32[128,128]{1,0:T(8,128)S(1)}, f32[128,128]{1,0:T(8,128)}, u32[]{:S(2)}) copy-start(f32[128,128]{1,0:T(8,128)} %param.16) | copy-start | bytes 196612
  55.9 5.9 %copy-start.5 = (f32[8]{0:T(128)S(1)}, f32[8]{0:T(128)}, u32[]{:S(2)}) copy-start(f32[8]{0:T(128)} %param.27) | copy-start | bytes 100

commit v7 on v1

--- a/solution.py
+++ b/solution.py
@@ -116,10 +116,10 @@
     dims = (((0,), (0,)), ((), ()))
     outgoing = lax.dot_general(onehot, flat_flux, dims, precision=high)
     spread = jnp.broadcast_to(surface, (devices, 2 * columns))
-    payload = jnp.concatenate([outgoing.astype(jnp.bfloat16), spread], axis=1)
+    payload = jnp.concatenate([outgoing, spread.astype(jnp.float32)], axis=1)
     incoming = lax.all_to_all(payload, ("sec", "tile"), split_axis=0, concat_axis=0, tiled=True)
     flux = jnp.sum(incoming[:, : nbins * columns].astype(jnp.float32), axis=0).reshape(nbins, columns)
-    gathered = incoming[:, nbins * columns :]
+    gathered = incoming[:, nbins * columns :].astype(jnp.bfloat16)
     flux = flux * (float(columns) / float(ncells * nblocks))
     loaded = dust_mix.at[:, 0, :].add(flux)
     dust_out = solve(loaded, mixing, settle)

time: 63.5 us -> 69 us (1.087)
  waiting for transfers between devices: 14 us -> 20.3 us
  other arithmetic: 6.6 us -> 5.5 us
    all_to_all x1, waiting for transfers between devices: 14 us -> 20.3 us  [on_device(): lax.all_to_all(payload, ('sec', 'tile'), split_axis=0, concat_axis=0, til...]
    all_to_all x1, local copies, waits for them, and re-layouts: 0.51 us -> 2.42 us  [on_device(): lax.all_to_all(payload, ('sec', 'tile'), split_axis=0, concat_axis=0, til...]
    unnamed x35 -> x33, local copies, waits for them, and re-layouts: 2.76 us -> 1.23 us
    all_to_all x2 -> x1, other arithmetic: 1.2 us -> 0.12 us  [on_device(): lax.all_to_all(payload, ('sec', 'tile'), split_axis=0, concat_axis=0, til...]
where the time goes in v7:
time: 69 us; the launch traced here: 68.5 us
  matrix products  24.2 us (35%)
  waiting for transfers between devices  20.3 us (29%)
  starting transfers between devices  11.5 us (17%)
  local copies, waits for them, and re-layouts  5.91 us (9%)
  other arithmetic  5.5 us (8%)
  between operations  1.16 us (2%)
    all_to_all x1, waiting for transfers between devices, on_device(): lax.all_to_all(payload, ('sec', 'tile'), split_axis=0, concat_axis=0, til...  20.3 us
    dot_general x3, matrix products, lookup(): lax.dot_general(p, pick_row, dims, preferred_element_type=jnp.float32)  13.7 us
    all_to_all x1, starting transfers between devices, on_device(): lax.all_to_all(payload, ('sec', 'tile'), split_axis=0, concat_axis=0, til...  11.5 us
    dot_general x1, matrix products, on_device(): jnp.einsum('gla,gka->kgl', regrid_w, picked, preferred_element_type=jnp.f...  5.63 us
    all_to_all x1, local copies, waits for them, and re-layouts, on_device(): lax.all_to_all(payload, ('sec', 'tile'), split_axis=0, concat_axis=0, til...  2.42 us
    dot_general x1, matrix products, emit(): blasted = jnp.einsum('tkb,bnl->tknl', blast_table, salt, precision=high)  1.88 us
  transfers between devices with their start and end apart: 1, of which 1 were waited for; matrix products, arithmetic and copies ran while one was open for 0% of the time, Pallas kernels for 0%

profile of v7, /device:TPU:1, one launch (start us, length us, event | category | flops | bytes accessed | tf_op | source)
XLA Modules:
  0.0 68.5 jit_solution(10598154204039391235)
XLA Ops:
  0.7 1.0 %fusion.85 = (f32[1,256]{1,0:T(1,128)S(1)}, f32[1,256]{1,0:T(1,128)S(1)}, f32[1,256]{1,0:T(1,128)S(1)}, f32[1,256]{1,0:T(1,128)S(1)}, f32[1,256]{1,0:T(1,128)S(1...) fusion(f32[15,256]{1,0:T(8,128)} %param.26), kind=kLoop, calls=%fused_computation.259 | loop fusion | flops 2816 | bytes 24576 | tf_op jit(solution)/shard_map/slice | solution.py:61
  1.6 1.0 %broadcast_add_fusion.1 = (f32[1,256]{1,0:T(1,128)S(1)}, f32[1,256]{1,0:T(1,128)S(1)}, f32[1,256]{1,0:T(1,128)S(1)}, f32[1,256]{1,0:T(1,128)S(1)}, f32[1,256]{1,...) fusion(f32[15,256]{1,0:T(8,128)} %param.26), kind=kLoop, calls=%fused_computation.252 | loop fusion | flops 4608 | bytes 20480 | tf_op jit(solution)/shard_map/add;add | solution.py:62
  2.6 0.9 %fusion.86 = (f32[1,256]{1,0:T(1,128)S(1)}, f32[1,256]{1,0:T(1,128)S(1)}, f32[1,256]{1,0:T(1,128)S(1)}, f32[1,256]{1,0:T(1,128)S(1)}, f32[1,256]{1,0:T(1,128)S(1...) fusion(f32[15,256]{1,0:T(8,128)} %param.26), kind=kLoop, calls=%fused_computation.260 | loop fusion | bytes 14336 | tf_op jit(solution)/shard_map/slice | solution.py:61
  3.5 1.2 %fusion.84 = (f32[3,1,256]{2,1,0:T(1,128)S(1)}, f32[3,1,256]{2,1,0:T(1,128)S(1)}, f32[3,1,256]{2,1,0:T(1,128)S(1)}, f32[3,1,256]{2,1,0:T(1,128)S(1)}, f32[3,1,25...) fusion(f32[3,16,256]{2,1,0:T(8,128)} %param.24), kind=kLoop, calls=%fused_computation.258 | loop fusion | bytes 98304 | tf_op jit(solution)/shard_map/slice | solution.py:65
  4.8 0.1 multiply_add_fusion.15
  5.1 0.9 %add_select_fusion.1 = (s32[16384]{0:T(1024)S(1)}, s32[16384]{0:T(1024)S(1)}) fusion(s32[128,128]{1,0:T(8,128)} %param.18), kind=kLoop, calls=%fused_computation.42 | loop fusion | flops 311296 | bytes 196608 | tf_op jit(solution)/shard_map/jit(remainder)/select_n | solution.py:35
  6.1 4.4 %convolution_bitcast_fusion = f32[128,16384]{1,0:T(8,128)S(1)} fusion(s32[16384]{0:T(1024)S(1)} %get-tuple-element.81, f32[32768]{0:T(1024)} %param.19), kind=kOutput, calls=%fused_computation | convolution fusion | flops 1078001664 | bytes 8585216 | tf_op jit(solution)/shard_map/dot_general | solution.py:45
  10.5 4.0 %convolution_add_fusion.1 = f32[128,16384]{1,0:T(8,128)S(1)} fusion(f32[128,16384]{1,0:T(8,128)S(1)} %convolution_bitcast_fusion, s32[16384]{0:T(1024)S(1)} %get-tuple-element.81, f32[32768]{0:T(1024)S(1)} %copy-done.1), kind=kOutput, calls=%fused_computation.3 | convolution fusion | flops 1080164352 | bytes 16973824 | tf_op jit(solution)/shard_map/dot_general | solution.py:45
  14.6 5.2 %fusion.5 = f32[16384]{0:T(1024)S(1)} fusion(f32[128,16384]{1,0:T(8,128)S(1)} %convolution_add_fusion.1, s32[16384]{0:T(1024)S(1)} %get-tuple-element.81, s32[16384]{0:T(1024)S(1)} %get-tuple-element.80, f32[32768]{0:T(1024)S(1)} %copy-done.1), kind=kOutput, calls=%fused_computation.11 | convolution fusion | flops 1086472192 | bytes 8716288 | tf_op jit(solution)/shard_map/dot_general | solution.py:45
  20.0 0.8 %fusion.9 = f32[12,128,128,1]{2,0,3,1:T(8,128)S(1)} fusion(f32[128,128]{1,0:T(8,128)S(1)} %mul.1908, f32[128,128]{1,0:T(8,128)S(1)} %add_sqrt_fusion, f32[12]{0:T(128)S(1)} %multiply_sqrt_fusion, f32[128,128]{1,0:T(8,128)S(1)} %copy-done.2, f32[128,128]{1,0:T(8,128)S(1)} %multiply_bitcast_fusion, s32[128,128]{1,0:T(8,128)S(1)} %copy-done.5, ...), kind=kOutput, calls=%fused_computation.18 | convolution fusion | flops 11075584 | bytes 1114352 | tf_op jit(solution)/shard_map/tb,tnl->bnl/dot_general | solution.py:17
  20.9 1.9 %fusion.4 = bf16[8,128,128]{2,0,1:T(8,128)(2,1)S(1)} fusion(f32[12,128,128,1]{2,0,3,1:T(8,128)S(1)} %fusion.9, f32[4,128,128]{2,0,1:T(4,128)S(1)} %fusion.16, f32[4,8,12]{2,1,0:T(8,128)S(1)} %copy-done), kind=kOutput, calls=%fused_computation.10 | convolution fusion | flops 76414976 | bytes 1312256 | tf_op jit(solution)/shard_map/tkb,bnl->tknl/dot_general | solution.py:26
  22.8 1.2 %fusion.12 = f32[128,8,256]{2,1,0:T(8,128)S(1)} fusion(bf16[128,128,256]{2,1,0:T(8,128)(2,1)S(1)} %bitcast.245, bf16[8,128,128]{2,0,1:T(8,128)(2,1)S(1)} %fusion.4), kind=kOutput, calls=%fused_computation.27 | convolution fusion | flops 67108864 | bytes 9699328 | tf_op jit(solution)/shard_map/gkl,gla->gka/dot_general | solution.py:110
  24.0 0.3 copy.144
  24.4 0.7 %fusion.22 = f32[128,2048]{1,0:T(8,128)S(1)} fusion(f32[128,2048]{1,0:T(8,128)S(1)} %bitcast.249, s32[128]{0:T(128)S(1)} %bitcast.420), kind=kOutput, calls=%fused_computation.55 | convolution fusion | flops 402669568 | bytes 2097664 | tf_op jit(solution)/shard_map/dot_general | solution.py:117
  25.2 2.4 %copy.87 = f32[128,1,2560]{2,1,0:T(1,128)} copy(f32[128,1,2560]{2,0,1:T(8,128)S(1)} %maximum_bitcast_fusion) | data formatting | bytes 2621440 | tf_op jit(solution)/shard_map/all_to_all | solution.py:120
  27.6 11.5 %all-to-all-start = ((f32[128,1,2560]{2,1,0:T(1,128)}), f32[128,1,2560]{2,1,0:T(1,128)S(1)}, u32[]{:S(2)}, u32[]{:S(2)}) async-start(f32[128,1,2560]{2,1,0:T(1,128)} %copy.87), calls=%async_computation | async-start | bytes 2621440 | tf_op jit(solution)/shard_map/all_to_all | solution.py:120
  39.2 20.3 %all-to-all-done = f32[128,1,2560]{2,1,0:T(1,128)S(1)} async-done(((f32[128,1,2560]{2,1,0:T(1,128)}), f32[128,1,2560]{2,1,0:T(1,128)S(1)}, u32[]{:S(2)}, u32[]{:S(2)}) %all-to-all-start) | async-done | bytes 1310752 | tf_op jit(solution)/shard_map/all_to_all | solution.py:120
  59.7 0.2 convolution_convert_fusion
  59.9 0.2 fusion.34
  60.1 0.2 constant_dynamic-update-slice_fusion.15
  61.2 0.7 %copy.107 = f32[8,16,256]{2,1,0:T(8,128)} copy(f32[8,16,256]{2,0,1:T(8,128)S(1)} %constant_dynamic-update-slice_fusion) | data formatting | bytes 262144
  61.9 5.6 %convolution_bitcast_fusion.1 = f32[3,128,128]{2,0,1:T(4,128)S(1)} fusion(bf16[128,128,256]{2,1,0:T(8,128)(2,1)} %param.23, bf16[128,2,256]{2,1,0:T(2,128)(2,1)S(1)} %reshape.27197), kind=kOutput, calls=%fused_computation.21 | convolution fusion | flops 25165824 | bytes 8716288 | tf_op jit(solution)/shard_map/gla,gka->kgl/dot_general | solution.py:129
  67.6 0.2 fusion.82
  67.8 0.7 pad_maximum_fusion
  (58 shorter events, 1.6 us)
Async XLA Ops:
  0.6 20.2 %copy-start = (f32[4,8,12]{2,1,0:T(8,128)S(1)}, f32[4,8,12]{2,1,0:T(8,128)}, u32[]{:S(2)}) copy-start(f32[4,8,12]{2,1,0:T(8,128)} %param.21) | copy-start | bytes 4612
  0.6 9.8 %copy-start.1 = (f32[32768]{0:T(1024)S(1)}, f32[32768]{0:T(1024)}, u32[]{:S(2)}) copy-start(f32[32768]{0:T(1024)} %param.19) | copy-start | bytes 393220
  10.5 12.2 %slice-start = ((s8[8388608]{0:T(1024)(128)(4,1)}), s8[4194304]{0:T(1024)(128)(4,1)S(1)}, s32[]{:S(2)}) async-start(s8[8388608]{0:T(1024)(128)(4,1)} %bitcast.244), calls=%async_computation.1 | async-start | bytes 8388608
  14.6 5.3 %copy-start.3 = (f32[128,128]{1,0:T(8,128)S(1)}, f32[128,128]{1,0:T(8,128)}, u32[]{:S(2)}) copy-start(f32[128,128]{1,0:T(8,128)} %param.16) | copy-start | bytes 196612
  14.6 5.3 %copy-start.2 = (f32[128,128]{1,0:T(8,128)S(1)}, f32[128,128]{1,0:T(8,128)}, u32[]{:S(2)}) copy-start(f32[128,128]{1,0:T(8,128)} %param.15) | copy-start | bytes 196612
  14.6 5.3 %copy-start.5 = (s32[128,128]{1,0:T(8,128)S(1)}, s32[128,128]{1,0:T(8,128)}, u32[]{:S(2)}) copy-start(s32[128,128]{1,0:T(8,128)} %param.17) | copy-start | bytes 196612
  14.6 5.4 %copy-start.8 = (f32[4,12]{1,0:T(4,128)S(1)}, f32[4,12]{1,0:T(4,128)}, u32[]{:S(2)}) copy-start(f32[4,12]{1,0:T(4,128)} %param.20) | copy-start | bytes 580
  14.6 8.1 %slice-start.1 = ((s8[8388608]{0:T(1024)(128)(4,1)}), s8[4194304]{0:T(1024)(128)(4,1)S(1)}, s32[]{:S(2)}) async-start(s8[8388608]{0:T(1024)(128)(4,1)} %bitcast.244), calls=%async_computation.2 | async-start | bytes 8388608
  22.8 1.6 %copy-start.7 = (s32[128,1]{0,1:T(1,128)S(1)}, s32[128,1]{0,1:T(1,128)}, u32[]{:S(2)}) copy-start(s32[128,1]{0,1:T(1,128)} %param.22) | copy-start | bytes 1540
  24.0 15.1 %copy-start.4 = (f32[8,16,256]{2,1,0:T(8,128)S(1)}, f32[8,16,256]{2,1,0:T(8,128)}, u32[]{:S(2)}) copy-start(f32[8,16,256]{2,1,0:T(8,128)} %param.25) | copy-start | bytes 393220
  24.0 35.9 %copy-start.6 = (f32[8]{0:T(128)S(1)}, f32[8]{0:T(128)}, u32[]{:S(2)}) copy-start(f32[8]{0:T(128)} %param.27) | copy-start | bytes 100
  27.6 31.9 %all-to-all-start = ((f32[128,1,2560]{2,1,0:T(1,128)}), f32[128,1,2560]{2,1,0:T(1,128)S(1)}, u32[]{:S(2)}, u32[]{:S(2)}) async-start(f32[128,1,2560]{2,1,0:T(1,128)} %copy.87), calls=%async_computation | async-start | bytes 2621440 | tf_op jit(solution)/shard_map/all_to_all | solution.py:120

commit v8 on v7

--- a/solution.py
+++ b/solution.py
@@ -116,10 +116,13 @@
     dims = (((0,), (0,)), ((), ()))
     outgoing = lax.dot_general(onehot, flat_flux, dims, precision=high)
     spread = jnp.broadcast_to(surface, (devices, 2 * columns))
-    payload = jnp.concatenate([outgoing, spread.astype(jnp.float32)], axis=1)
+    half = nbins * columns // 2
+    payload = jnp.concatenate(
+        [outgoing.astype(jnp.bfloat16).reshape(devices, 2, half), spread.reshape(devices, 2, columns)], axis=2
+    )
     incoming = lax.all_to_all(payload, ("sec", "tile"), split_axis=0, concat_axis=0, tiled=True)
-    flux = jnp.sum(incoming[:, : nbins * columns].astype(jnp.float32), axis=0).reshape(nbins, columns)
-    gathered = incoming[:, nbins * columns :].astype(jnp.bfloat16)
+    flux = jnp.sum(incoming[:, :, :half].astype(jnp.float32), axis=0).reshape(nbins, columns)
+    gathered = incoming[:, :, half:].reshape(devices, 2 * columns)
     flux = flux * (float(columns) / float(ncells * nblocks))
     loaded = dust_mix.at[:, 0, :].add(flux)
     dust_out = solve(loaded, mixing, settle)

time: 69 us -> 62.6 us (0.907)
  waiting for transfers between devices: 20.3 us -> 14 us
  local copies, waits for them, and re-layouts: 5.91 us -> 4.01 us
  other arithmetic: 5.5 us -> 7.23 us
    all_to_all x1, waiting for transfers between devices: 20.3 us -> 14 us  [on_device(): lax.all_to_all(payload, ('sec', 'tile'), split_axis=0, concat_axis=0, til...]
    all_to_all x1 -> x0, local copies, waits for them, and re-layouts: 2.42 us -> none  [on_device(): lax.all_to_all(payload, ('sec', 'tile'), split_axis=0, concat_axis=0, til...]
    concatenate x0 -> x1, other arithmetic: none -> 1.44 us  [on_device(): jnp.concatenate([outgoing.astype(jnp.bfloat16).reshape(devices, 2, half),...]
where the time goes in v8:
time: 62.6 us; the launch traced here: 62.1 us
  matrix products  24.2 us (39%)
  waiting for transfers between devices  14 us (22%)
  starting transfers between devices  11.5 us (18%)
  other arithmetic  7.23 us (12%)
  local copies, waits for them, and re-layouts  4.01 us (6%)
  between operations  1.16 us (2%)
    all_to_all x1, waiting for transfers between devices, on_device(): lax.all_to_all(payload, ('sec', 'tile'), split_axis=0, concat_axis=0, til...  14 us
    dot_general x3, matrix products, lookup(): lax.dot_general(p, pick_row, dims, preferred_element_type=jnp.float32)  13.7 us
    all_to_all x1, starting transfers between devices, on_device(): lax.all_to_all(payload, ('sec', 'tile'), split_axis=0, concat_axis=0, til...  11.5 us
    dot_general x1, matrix products, on_device(): jnp.einsum('gla,gka->kgl', regrid_w, picked, preferred_element_type=jnp.f...  5.63 us
    dot_general x1, matrix products, emit(): blasted = jnp.einsum('tkb,bnl->tknl', blast_table, salt, precision=high)  1.88 us
    concatenate x1, other arithmetic, on_device(): jnp.concatenate([outgoing.astype(jnp.bfloat16).reshape(devices, 2, half),...  1.44 us
  transfers between devices with their start and end apart: 1, of which 1 were waited for; matrix products, arithmetic and copies ran while one was open for 0% of the time, Pallas kernels for 0%

profile of v8, /device:TPU:1, one launch (start us, length us, event | category | flops | bytes accessed | tf_op | source)
XLA Modules:
  0.0 62.1 jit_solution(1516558947973759956)
XLA Ops:
  0.7 1.0 %fusion.84 = (f32[1,256]{1,0:T(1,128)S(1)}, f32[1,256]{1,0:T(1,128)S(1)}, f32[1,256]{1,0:T(1,128)S(1)}, f32[1,256]{1,0:T(1,128)S(1)}, f32[1,256]{1,0:T(1,128)S(1...) fusion(f32[15,256]{1,0:T(8,128)} %param.26), kind=kLoop, calls=%fused_computation.258 | loop fusion | flops 2816 | bytes 24576 | tf_op jit(solution)/shard_map/slice | solution.py:61
  1.6 1.0 %broadcast_add_fusion.1 = (f32[1,256]{1,0:T(1,128)S(1)}, f32[1,256]{1,0:T(1,128)S(1)}, f32[1,256]{1,0:T(1,128)S(1)}, f32[1,256]{1,0:T(1,128)S(1)}, f32[1,256]{1,...) fusion(f32[15,256]{1,0:T(8,128)} %param.26), kind=kLoop, calls=%fused_computation.251 | loop fusion | flops 4608 | bytes 20480 | tf_op jit(solution)/shard_map/add;add | solution.py:62
  2.6 0.9 %fusion.85 = (f32[1,256]{1,0:T(1,128)S(1)}, f32[1,256]{1,0:T(1,128)S(1)}, f32[1,256]{1,0:T(1,128)S(1)}, f32[1,256]{1,0:T(1,128)S(1)}, f32[1,256]{1,0:T(1,128)S(1...) fusion(f32[15,256]{1,0:T(8,128)} %param.26), kind=kLoop, calls=%fused_computation.259 | loop fusion | bytes 14336 | tf_op jit(solution)/shard_map/slice | solution.py:61
  3.5 1.2 %fusion.83 = (f32[3,1,256]{2,1,0:T(1,128)S(1)}, f32[3,1,256]{2,1,0:T(1,128)S(1)}, f32[3,1,256]{2,1,0:T(1,128)S(1)}, f32[3,1,256]{2,1,0:T(1,128)S(1)}, f32[3,1,25...) fusion(f32[3,16,256]{2,1,0:T(8,128)} %param.24), kind=kLoop, calls=%fused_computation.257 | loop fusion | bytes 98304 | tf_op jit(solution)/shard_map/slice | solution.py:65
  5.1 0.9 %add_select_fusion.1 = (s32[16384]{0:T(1024)S(1)}, s32[16384]{0:T(1024)S(1)}) fusion(s32[128,128]{1,0:T(8,128)} %param.18), kind=kLoop, calls=%fused_computation.42 | loop fusion | flops 311296 | bytes 196608 | tf_op jit(solution)/shard_map/jit(remainder)/select_n | solution.py:35
  6.0 4.4 %convolution_bitcast_fusion = f32[128,16384]{1,0:T(8,128)S(1)} fusion(s32[16384]{0:T(1024)S(1)} %get-tuple-element.83, f32[32768]{0:T(1024)} %param.19), kind=kOutput, calls=%fused_computation | convolution fusion | flops 1078001664 | bytes 8585216 | tf_op jit(solution)/shard_map/dot_general | solution.py:45
  10.5 4.0 %convolution_add_fusion.1 = f32[128,16384]{1,0:T(8,128)S(1)} fusion(f32[128,16384]{1,0:T(8,128)S(1)} %convolution_bitcast_fusion, s32[16384]{0:T(1024)S(1)} %get-tuple-element.83, f32[32768]{0:T(1024)S(1)} %copy-done.1), kind=kOutput, calls=%fused_computation.3 | convolution fusion | flops 1080164352 | bytes 16973824 | tf_op jit(solution)/shard_map/dot_general | solution.py:45
  14.6 5.2 %fusion.5 = f32[16384]{0:T(1024)S(1)} fusion(f32[128,16384]{1,0:T(8,128)S(1)} %convolution_add_fusion.1, s32[16384]{0:T(1024)S(1)} %get-tuple-element.83, s32[16384]{0:T(1024)S(1)} %get-tuple-element.82, f32[32768]{0:T(1024)S(1)} %copy-done.1), kind=kOutput, calls=%fused_computation.12 | convolution fusion | flops 1086472192 | bytes 8716288 | tf_op jit(solution)/shard_map/dot_general | solution.py:45
  20.0 0.8 %fusion.9 = f32[12,128,128,1]{2,0,3,1:T(8,128)S(1)} fusion(f32[128,128]{1,0:T(8,128)S(1)} %mul.1908, f32[128,128]{1,0:T(8,128)S(1)} %add_sqrt_fusion, f32[12]{0:T(128)S(1)} %multiply_sqrt_fusion, f32[128,128]{1,0:T(8,128)S(1)} %copy-done.2, f32[128,128]{1,0:T(8,128)S(1)} %multiply_bitcast_fusion, s32[128,128]{1,0:T(8,128)S(1)} %copy-done.5, ...), kind=kOutput, calls=%fused_computation.19 | convolution fusion | flops 11075584 | bytes 1114352 | tf_op jit(solution)/shard_map/tb,tnl->bnl/dot_general | solution.py:17
  20.8 1.9 %fusion.4 = bf16[8,128,128]{2,0,1:T(8,128)(2,1)S(1)} fusion(f32[12,128,128,1]{2,0,3,1:T(8,128)S(1)} %fusion.9, f32[4,128,128]{2,0,1:T(4,128)S(1)} %fusion.16, f32[4,8,12]{2,1,0:T(8,128)S(1)} %copy-done), kind=kOutput, calls=%fused_computation.11 | convolution fusion | flops 76414976 | bytes 1312256 | tf_op jit(solution)/shard_map/tkb,bnl->tknl/dot_general | solution.py:26
  22.8 1.2 %fusion.13 = f32[128,8,256]{2,1,0:T(8,128)S(1)} fusion(bf16[128,128,256]{2,1,0:T(8,128)(2,1)S(1)} %bitcast.240, bf16[128,8,128]{2,0,1:T(8,128)(2,1)S(1)} %bitcast.243), kind=kOutput, calls=%fused_computation.28 | convolution fusion | flops 67108864 | bytes 9699328 | tf_op jit(solution)/shard_map/gkl,gla->gka/dot_general | solution.py:110
  24.0 0.3 copy.143
  24.4 0.7 %convolution_convert_fusion = bf16[128,2048]{1,0:T(8,128)(2,1)S(1)} fusion(f32[128,2048]{1,0:T(8,128)S(1)} %bitcast.242, s32[128]{0:T(128)S(1)} %bitcast.415), kind=kOutput, calls=%fused_computation.9 | convolution fusion | flops 402931712 | bytes 1573376 | tf_op jit(solution)/shard_map/dot_general | solution.py:117
  25.1 0.4 reshape.27203
  25.6 1.4 %pad_maximum_fusion = bf16[128,2,1280]{2,1,0:T(2,128)(2,1)} fusion(bf16[128,2,256]{2,1,0:T(2,128)(2,1)S(1)} %broadcast_in_dim.7, bf16[128,2,1024]{2,1,0:T(2,128)(2,1)S(1)} %reshape.27203), kind=kLoop, calls=%fused_computation.25 | loop fusion | flops 1310720 | bytes 1310720 | tf_op jit(solution)/shard_map/concatenate | solution.py:120
  27.0 11.5 %all-to-all-start = ((bf16[128,2,1280]{2,1,0:T(2,128)(2,1)}), bf16[128,2,1280]{2,1,0:T(2,128)(2,1)S(1)}, u32[]{:S(2)}, u32[]{:S(2)}) async-start(bf16[128,2,1280]{2,1,0:T(2,128)(2,1)} %pad_maximum_fusion), calls=%async_computation | async-start | bytes 1310720 | tf_op jit(solution)/shard_map/all_to_all | solution.py:123
  38.7 14.0 %all-to-all-done = bf16[128,2,1280]{2,1,0:T(2,128)(2,1)S(1)} async-done(((bf16[128,2,1280]{2,1,0:T(2,128)(2,1)}), bf16[128,2,1280]{2,1,0:T(2,128)(2,1)S(1)}, u32[]{:S(2)}, u32[]{:S(2)}) %all-to-all-start) | async-done | bytes 655392 | tf_op jit(solution)/shard_map/all_to_all | solution.py:123
  52.7 0.5 convert_reduce_fusion
  53.4 0.2 constant_dynamic-update-slice_fusion.15
  54.5 0.7 %copy.106 = f32[8,16,256]{2,1,0:T(8,128)} copy(f32[8,16,256]{2,0,1:T(8,128)S(1)} %constant_dynamic-update-slice_fusion) | data formatting | bytes 262144
  55.3 0.2 convolution_convert_fusion.1
  55.6 5.6 %convolution_bitcast_fusion.1 = f32[3,128,128]{2,0,1:T(4,128)S(1)} fusion(bf16[128,128,256]{2,1,0:T(8,128)(2,1)} %param.23, bf16[128,2,256]{2,1,0:T(2,128)(2,1)S(1)} %reshape.27205), kind=kOutput, calls=%fused_computation.20 | convolution fusion | flops 25165824 | bytes 8716288 | tf_op jit(solution)/shard_map/gla,gka->kgl/dot_general | solution.py:132
  61.2 0.2 fusion.81
  61.4 0.7 %pad_maximum_fusion.1 = f32[2,128,128]{2,1,0:T(8,128)} fusion(f32[1,128,128]{2,1,0:T(8,128)S(1)} %add_bitcast_fusion, f32[1,128,128]{2,1,0:T(8,128)S(1)} %div.1527), kind=kLoop, calls=%fused_computation.38 | loop fusion | flops 32768 | bytes 262144 | tf_op jit(solution)/shard_map/stack | solution.py:134
  (59 shorter events, 1.8 us)
Async XLA Ops:
  0.6 20.2 %copy-start = (f32[4,8,12]{2,1,0:T(8,128)S(1)}, f32[4,8,12]{2,1,0:T(8,128)}, u32[]{:S(2)}) copy-start(f32[4,8,12]{2,1,0:T(8,128)} %param.21) | copy-start | bytes 4612
  0.6 9.8 %copy-start.1 = (f32[32768]{0:T(1024)S(1)}, f32[32768]{0:T(1024)}, u32[]{:S(2)}) copy-start(f32[32768]{0:T(1024)} %param.19) | copy-start | bytes 393220
  10.5 12.3 %slice-start = ((s8[8388608]{0:T(1024)(128)(4,1)}), s8[4194304]{0:T(1024)(128)(4,1)S(1)}, s32[]{:S(2)}) async-start(s8[8388608]{0:T(1024)(128)(4,1)} %bitcast.239), calls=%async_computation.1 | async-start | bytes 8388608
  14.5 5.3 %copy-start.3 = (f32[128,128]{1,0:T(8,128)S(1)}, f32[128,128]{1,0:T(8,128)}, u32[]{:S(2)}) copy-start(f32[128,128]{1,0:T(8,128)} %param.16) | copy-start | bytes 196612
  14.5 5.3 %copy-start.2 = (f32[128,128]{1,0:T(8,128)S(1)}, f32[128,128]{1,0:T(8,128)}, u32[]{:S(2)}) copy-start(f32[128,128]{1,0:T(8,128)} %param.15) | copy-start | bytes 196612
  14.6 5.3 %copy-start.5 = (s32[128,128]{1,0:T(8,128)S(1)}, s32[128,128]{1,0:T(8,128)}, u32[]{:S(2)}) copy-start(s32[128,128]{1,0:T(8,128)} %param.17) | copy-start | bytes 196612
  14.6 5.4 %copy-start.8 = (f32[4,12]{1,0:T(4,128)S(1)}, f32[4,12]{1,0:T(4,128)}, u32[]{:S(2)}) copy-start(f32[4,12]{1,0:T(4,128)} %param.20) | copy-start | bytes 580
  14.6 8.2 %slice-start.1 = ((s8[8388608]{0:T(1024)(128)(4,1)}), s8[4194304]{0:T(1024)(128)(4,1)S(1)}, s32[]{:S(2)}) async-start(s8[8388608]{0:T(1024)(128)(4,1)} %bitcast.239), calls=%async_computation.2 | async-start | bytes 8388608
  22.8 1.6 %copy-start.7 = (s32[128,1]{0,1:T(1,128)S(1)}, s32[128,1]{0,1:T(1,128)}, u32[]{:S(2)}) copy-start(s32[128,1]{0,1:T(1,128)} %param.22) | copy-start | bytes 1540
  22.8 15.8 %copy-start.4 = (f32[8,16,256]{2,1,0:T(8,128)S(1)}, f32[8,16,256]{2,1,0:T(8,128)}, u32[]{:S(2)}) copy-start(f32[8,16,256]{2,1,0:T(8,128)} %param.25) | copy-start | bytes 393220
  22.8 30.4 %copy-start.6 = (f32[8]{0:T(128)S(1)}, f32[8]{0:T(128)}, u32[]{:S(2)}) copy-start(f32[8]{0:T(128)} %param.27) | copy-start | bytes 100
  27.0 25.7 %all-to-all-start = ((bf16[128,2,1280]{2,1,0:T(2,128)(2,1)}), bf16[128,2,1280]{2,1,0:T(2,128)(2,1)S(1)}, u32[]{:S(2)}, u32[]{:S(2)}) async-start(bf16[128,2,1280]{2,1,0:T(2,128)(2,1)} %pad_maximum_fusion), calls=%async_computation | async-start | bytes 1310720 | tf_op jit(solution)/shard_map/all_to_all | solution.py:123

commit v9 on v2

--- a/solution.py
+++ b/solution.py
@@ -2,6 +2,7 @@
 import jax.numpy as jnp
 from jax import lax
 from jax.experimental import pallas as pl
+from jax.experimental.pallas import tpu as pltpu
 from jax.sharding import PartitionSpec as P
 
 
@@ -31,16 +32,19 @@
 
 def lookup_kernel(index_ref, parts_ref, out_ref):
     rows_per_step, lanes = index_ref.shape
-    segments = parts_ref.shape[1]
+    segments = parts_ref.shape[1] // 3
+    levels = lax.broadcasted_iota(jnp.int32, (segments, lanes), 0).astype(jnp.bfloat16)
+    lane_rows = lax.broadcasted_iota(jnp.int32, (128, lanes), 0)
+    one = jnp.ones((segments, lanes), jnp.bfloat16)
+    zero = jnp.zeros((segments, lanes), jnp.bfloat16)
     for r in range(rows_per_step):
         cell = index_ref[r : r + 1, :]
-        high_part = cell // 128
+        high_part = (cell // 128).astype(jnp.bfloat16)
         low_part = cell % 128
-        pick_row = lax.broadcasted_iota(jnp.int32, (segments, lanes), 0) == high_part
-        pick_row = jnp.where(pick_row, 1.0, 0.0).astype(jnp.bfloat16)
-        products = jnp.dot(parts_ref[...], pick_row, preferred_element_type=jnp.float32)
-        row_values = (products[0:128] + products[128:256]) + products[256:384]
-        pick_lane = lax.broadcasted_iota(jnp.int32, (128, lanes), 0) == low_part
+        pick_row = jnp.where(levels == high_part, one, zero)
+        stacked = jnp.concatenate([pick_row, pick_row, pick_row], axis=0)
+        row_values = jnp.dot(parts_ref[...], stacked, preferred_element_type=jnp.float32)
+        pick_lane = lane_rows == low_part
         out_ref[r : r + 1, :] = jnp.sum(jnp.where(pick_lane, row_values, 0.0), axis=0, keepdims=True)
 
 
@@ -50,9 +54,7 @@
     first_wide = lax.reduce_precision(grid, exponent_bits=8, mantissa_bits=7)
     rest = grid - first_wide
     second_wide = lax.reduce_precision(rest, exponent_bits=8, mantissa_bits=7)
-    parts = jnp.concatenate(
-        [first_wide.T, second_wide.T, (rest - second_wide).T], axis=0
-    ).astype(jnp.bfloat16)
+    parts = jnp.concatenate([first_wide, second_wide, rest - second_wide], axis=0).T.astype(jnp.bfloat16)
     rows, lanes = index.shape
     step = 8
     return pl.pallas_call(
@@ -61,12 +63,13 @@
         grid=(rows // step,),
         in_specs=[
             pl.BlockSpec((step, lanes), lambda i: (i, 0)),
-            pl.BlockSpec((3 * 128, segments), lambda i: (0, 0)),
+            pl.BlockSpec((128, 3 * segments), lambda i: (0, 0)),
         ],
         out_specs=pl.BlockSpec((step, lanes), lambda i: (i, 0)),
+        compiler_params=pltpu.CompilerParams(vmem_limit_bytes=8 * 1024 * 1024),
         cost_estimate=pl.CostEstimate(
             flops=2 * 384 * segments * rows * lanes, transcendentals=0,
-            bytes_accessed=8 * rows * lanes + 2 * 384 * segments,
+            bytes_accessed=8 * rows * lanes + 768 * segments,
         ),
     )(index, parts)
 
@@ -138,10 +141,13 @@
     dims = (((0,), (0,)), ((), ()))
     outgoing = lax.dot_general(onehot, flat_flux, dims, precision=high)
     spread = jnp.broadcast_to(surface, (devices, 2 * columns))
-    payload = jnp.concatenate([outgoing.astype(jnp.bfloat16), spread], axis=1)
+    half = nbins * columns // 2
+    payload = jnp.concatenate(
+        [outgoing.astype(jnp.bfloat16).reshape(devices, 2, half), spread.reshape(devices, 2, columns)], axis=2
+    )
     incoming = lax.all_to_all(payload, ("sec", "tile"), split_axis=0, concat_axis=0, tiled=True)
-    flux = jnp.sum(incoming[:, : nbins * columns].astype(jnp.float32), axis=0).reshape(nbins, columns)
-    gathered = incoming[:, nbins * columns :]
+    flux = jnp.sum(incoming[:, :, :half].astype(jnp.float32), axis=0).reshape(nbins, columns)
+    gathered = incoming[:, :, half:].reshape(devices, 2 * columns)
     flux = flux * (float(columns) / float(ncells * nblocks))
     loaded = dust_mix.at[:, 0, :].add(flux)
     dust_out = solve(loaded, mixing, settle)

time: 69 us -> 61 us (0.88)
  matrix products: 13.8 us -> 10.5 us
  Pallas kernels: 11.8 us -> 9.36 us
  other arithmetic: 9.01 us -> 8.12 us
    dot_general x1, matrix products: 4.57 us -> 1.19 us  [on_device(): jnp.einsum('gkl,gla->gka', emission, regrid_w, preferred_element_type=jnp...]
    pallas_call x1, Pallas kernels: 11.8 us -> 9.36 us  [lookup(): pl.pallas_call(lookup_kernel, out_shape=jax.ShapeDtypeStruct((rows, lanes...]
    all_to_all x2 -> x0, other arithmetic: 1.2 us -> none  [on_device(): lax.all_to_all(payload, ('sec', 'tile'), split_axis=0, concat_axis=0, til...]
    sqrt x1, other arithmetic: 0.87 us -> 0.03 us  [emit(): jnp.sqrt(1.0 + 12.1 * moist_rows)[None]]
    concatenate x1, other arithmetic: 0.69 us -> 1.43 us  [on_device(): jnp.concatenate([outgoing.astype(jnp.bfloat16).reshape(devices, 2, half),...]
    unnamed x29 -> x31, local copies, waits for them, and re-layouts: 2.73 us -> 2.01 us
where the time goes in v9:
time: 61 us; the launch traced here: 60.4 us
  waiting for transfers between devices  14 us (23%)
  starting transfers between devices  11.5 us (19%)
  matrix products  10.5 us (17%)
  Pallas kernels  9.36 us (15%)
  other arithmetic  8.12 us (13%)
  local copies, waits for them, and re-layouts  5.83 us (10%)
  between operations  1.1 us (2%)
    all_to_all x1, waiting for transfers between devices, on_device(): lax.all_to_all(payload, ('sec', 'tile'), split_axis=0, concat_axis=0, til...  14 us
    all_to_all x1, starting transfers between devices, on_device(): lax.all_to_all(payload, ('sec', 'tile'), split_axis=0, concat_axis=0, til...  11.5 us
    pallas_call x1, Pallas kernels, lookup(): pl.pallas_call(lookup_kernel, out_shape=jax.ShapeDtypeStruct((rows, lanes...  9.36 us
    dot_general x1, matrix products, on_device(): jnp.einsum('gla,gka->kgl', regrid_w, picked, preferred_element_type=jnp.f...  5.63 us
    unnamed x31, local copies, waits for them, and re-layouts  2.01 us
    dot_general x1, matrix products, emit(): blasted = jnp.einsum('tkb,bnl->tknl', blast_table, salt, precision=high)  1.88 us
    concatenate x1, other arithmetic, on_device(): jnp.concatenate([outgoing.astype(jnp.bfloat16).reshape(devices, 2, half),...  1.43 us
    slice x1, local copies, waits for them, and re-layouts, solve(): part_now = right_side[:, level] / pivot  1.24 us
  transfers between devices with their start and end apart: 1, of which 1 were waited for; matrix products, arithmetic and copies ran while one was open for 0% of the time, Pallas kernels for 0%

profile of v9, /device:TPU:1, one launch (start us, length us, event | category | flops | bytes accessed | tf_op | source)
XLA Modules:
  0.0 60.4 jit_solution(4365315246822860615)
XLA Ops:
  0.7 1.0 %fusion.75 = (f32[1,256]{1,0:T(1,128)S(1)}, f32[1,256]{1,0:T(1,128)S(1)}, f32[1,256]{1,0:T(1,128)S(1)}, f32[1,256]{1,0:T(1,128)S(1)}, f32[1,256]{1,0:T(1,128)S(1...) fusion(f32[15,256]{1,0:T(8,128)} %param.26), kind=kLoop, calls=%fused_computation.239 | loop fusion | flops 2816 | bytes 24576 | tf_op jit(solution)/shard_map/slice | solution.py:86
  1.7 1.0 %broadcast_add_fusion.1 = (f32[1,256]{1,0:T(1,128)S(1)}, f32[1,256]{1,0:T(1,128)S(1)}, f32[1,256]{1,0:T(1,128)S(1)}, f32[1,256]{1,0:T(1,128)S(1)}, f32[1,256]{1,...) fusion(f32[15,256]{1,0:T(8,128)} %param.26), kind=kLoop, calls=%fused_computation.232 | loop fusion | flops 4608 | bytes 20480 | tf_op jit(solution)/shard_map/add;add | solution.py:87
  2.7 0.9 %fusion.76 = (f32[1,256]{1,0:T(1,128)S(1)}, f32[1,256]{1,0:T(1,128)S(1)}, f32[1,256]{1,0:T(1,128)S(1)}, f32[1,256]{1,0:T(1,128)S(1)}, f32[1,256]{1,0:T(1,128)S(1...) fusion(f32[15,256]{1,0:T(8,128)} %param.26), kind=kLoop, calls=%fused_computation.240 | loop fusion | bytes 14336 | tf_op jit(solution)/shard_map/slice | solution.py:86
  3.6 1.2 %fusion.74 = (f32[3,1,256]{2,1,0:T(1,128)S(1)}, f32[3,1,256]{2,1,0:T(1,128)S(1)}, f32[3,1,256]{2,1,0:T(1,128)S(1)}, f32[3,1,256]{2,1,0:T(1,128)S(1)}, f32[3,1,25...) fusion(f32[3,16,256]{2,1,0:T(8,128)} %param.24), kind=kLoop, calls=%fused_computation.238 | loop fusion | bytes 98304 | tf_op jit(solution)/shard_map/slice | solution.py:90
  5.2 1.0 %copy.72 = f32[256,128]{0,1:T(8,128)S(1)} copy(f32[256,128]{1,0:T(8,128)} %bitcast.210) | data formatting | bytes 262144 | tf_op jit(solution)/shard_map/reshape | solution.py:53
  6.2 0.9 %mul.1905 = f32[128,128]{1,0:T(8,128)S(1)} multiply(f32[128,128]{1,0:T(8,128)} %param.15, f32[128,128]{1,0:T(8,128)} %param.15) | non-fusion elementwise | flops 16384 | bytes 196608 | tf_op jit(solution)/shard_map/mul | solution.py:26
  7.1 0.9 %fusion.11 = f32[4,128,128]{2,0,1:T(4,128)S(1)} fusion(s32[128,128]{1,0:T(8,128)} %param.17), kind=kLoop, calls=%fused_computation.22 | loop fusion | flops 131072 | bytes 327680 | tf_op jit(solution)/shard_map/convert_element_type | solution.py:18
  8.1 0.8 %copy-done.1 = s32[128,128]{1,0:T(8,128)S(1)} copy-done((s32[128,128]{1,0:T(8,128)S(1)}, s32[128,128]{1,0:T(8,128)}, u32[]{:S(2)}) %copy-start.1) | copy-done | bytes 65560
  8.9 9.4 %shard_map.140 = f32[128,128]{1,0:T(8,128)S(1)} custom-call(s32[128,128]{1,0:T(8,128)S(1)} %copy-done.1, bf16[128,768]{1,0:T(8,128)(2,1)S(1)} %maximum_bitcast_fusion.parts_ref), custom_call_target="tpu_custom_call" | custom-call | flops 3221225472 | bytes 327680 | tf_op jit(solution)/shard_map/pallas_call | solution.py:60
  18.4 0.8 %fusion.4 = f32[12,128,128,1]{2,0,3,1:T(8,128)S(1)} fusion(f32[128,128]{1,0:T(8,128)S(1)} %mul.1905, f32[128,128]{1,0:T(8,128)S(1)} %get-tuple-element.132, f32[12]{0:T(128)S(1)} %multiply_sqrt_fusion, f32[128,128]{1,0:T(8,128)S(1)} %copy-done.3, f32[128,128]{1,0:T(8,128)S(1)} %get-tuple-element.133, s32[128,128]{1,0:T(8,128)S(1)} %copy-done.6, ...), kind=kOutput, calls=%fused_computation.9 | convolution fusion | flops 11075584 | bytes 1114352 | tf_op jit(solution)/shard_map/tb,tnl->bnl/dot_general | solution.py:19
  19.2 1.9 %fusion = bf16[8,128,128]{2,0,1:T(8,128)(2,1)S(1)} fusion(f32[12,128,128,1]{2,0,3,1:T(8,128)S(1)} %fusion.4, f32[4,128,128]{2,0,1:T(4,128)S(1)} %fusion.11, f32[4,8,12]{2,1,0:T(8,128)S(1)} %copy-done), kind=kOutput, calls=%fused_computation.2 | convolution fusion | flops 76414976 | bytes 1312256 | tf_op jit(solution)/shard_map/tkb,bnl->tknl/dot_general | solution.py:28
  21.2 1.2 %fusion.8 = f32[128,8,256]{2,1,0:T(8,128)S(1)} fusion(bf16[128,128,256]{2,1,0:T(8,128)(2,1)S(1)} %copy-done.2, bf16[128,8,128]{2,0,1:T(8,128)(2,1)S(1)} %bitcast.204), kind=kOutput, calls=%fused_computation.18 | convolution fusion | flops 67108864 | bytes 9699328 | tf_op jit(solution)/shard_map/gkl,gla->gka/dot_general | solution.py:135
  22.4 0.3 copy.147
  22.7 0.7 %convolution_convert_fusion = bf16[128,2048]{1,0:T(8,128)(2,1)S(1)} fusion(f32[128,2048]{1,0:T(8,128)S(1)} %bitcast.203, s32[128]{0:T(128)S(1)} %bitcast.377), kind=kOutput, calls=%fused_computation | convolution fusion | flops 402931712 | bytes 1573376 | tf_op jit(solution)/shard_map/dot_general | solution.py:142
  23.5 0.4 reshape.27148
  23.9 1.4 %pad_maximum_fusion = bf16[128,2,1280]{2,1,0:T(2,128)(2,1)} fusion(bf16[128,2,256]{2,1,0:T(2,128)(2,1)S(1)} %broadcast_in_dim.2, bf16[128,2,1024]{2,1,0:T(2,128)(2,1)S(1)} %reshape.27148), kind=kLoop, calls=%fused_computation.15 | loop fusion | flops 1310720 | bytes 1310720 | tf_op jit(solution)/shard_map/concatenate | solution.py:145
  25.4 11.5 %all-to-all-start = ((bf16[128,2,1280]{2,1,0:T(2,128)(2,1)}), bf16[128,2,1280]{2,1,0:T(2,128)(2,1)S(1)}, u32[]{:S(2)}, u32[]{:S(2)}) async-start(bf16[128,2,1280]{2,1,0:T(2,128)(2,1)} %pad_maximum_fusion), calls=%async_computation | async-start | bytes 1310720 | tf_op jit(solution)/shard_map/all_to_all | solution.py:148
  37.0 14.0 %all-to-all-done = bf16[128,2,1280]{2,1,0:T(2,128)(2,1)S(1)} async-done(((bf16[128,2,1280]{2,1,0:T(2,128)(2,1)}), bf16[128,2,1280]{2,1,0:T(2,128)(2,1)S(1)}, u32[]{:S(2)}, u32[]{:S(2)}) %all-to-all-start) | async-done | bytes 655392 | tf_op jit(solution)/shard_map/all_to_all | solution.py:148
  51.0 0.5 convert_reduce_fusion
  51.7 0.2 constant_dynamic-update-slice_fusion.15
  52.8 0.7 %copy.110 = f32[8,16,256]{2,1,0:T(8,128)} copy(f32[8,16,256]{2,0,1:T(8,128)S(1)} %constant_dynamic-update-slice_fusion) | data formatting | bytes 262144
  53.6 0.2 convolution_convert_fusion.1
  53.9 5.6 %convolution_bitcast_fusion = f32[3,128,128]{2,0,1:T(4,128)S(1)} fusion(bf16[128,128,256]{2,1,0:T(8,128)(2,1)} %param.23, bf16[128,2,256]{2,1,0:T(2,128)(2,1)S(1)} %reshape.27150), kind=kOutput, calls=%fused_computation.10 | convolution fusion | flops 25165824 | bytes 8716288 | tf_op jit(solution)/shard_map/gla,gka->kgl/dot_general | solution.py:157
  59.7 0.7 %pad_maximum_fusion.1 = f32[2,128,128]{2,1,0:T(8,128)} fusion(f32[1,128,128]{2,1,0:T(8,128)S(1)} %add_bitcast_fusion, f32[1,128,128]{2,1,0:T(8,128)S(1)} %div.1511), kind=kLoop, calls=%fused_computation.29 | loop fusion | flops 32768 | bytes 262144 | tf_op jit(solution)/shard_map/stack | solution.py:159
  (55 shorter events, 2.0 us)
Async XLA Ops:
  0.6 18.6 %copy-start = (f32[4,8,12]{2,1,0:T(8,128)S(1)}, f32[4,8,12]{2,1,0:T(8,128)}, u32[]{:S(2)}) copy-start(f32[4,8,12]{2,1,0:T(8,128)} %param.21) | copy-start | bytes 4612
  0.6 17.7 %copy-start.3 = (f32[128,128]{1,0:T(8,128)S(1)}, f32[128,128]{1,0:T(8,128)}, u32[]{:S(2)}) copy-start(f32[128,128]{1,0:T(8,128)} %param.15) | copy-start | bytes 196612
  0.7 17.7 %copy-start.6 = (s32[128,128]{1,0:T(8,128)S(1)}, s32[128,128]{1,0:T(8,128)}, u32[]{:S(2)}) copy-start(s32[128,128]{1,0:T(8,128)} %param.17) | copy-start | bytes 196612
  0.7 17.6 %copy-start.4 = (f32[128,128]{1,0:T(8,128)S(1)}, f32[128,128]{1,0:T(8,128)}, u32[]{:S(2)}) copy-start(f32[128,128]{1,0:T(8,128)} %param.16) | copy-start | bytes 196612
  0.7 17.7 %copy-start.9 = (f32[4,12]{1,0:T(4,128)S(1)}, f32[4,12]{1,0:T(4,128)}, u32[]{:S(2)}) copy-start(f32[4,12]{1,0:T(4,128)} %param.20) | copy-start | bytes 580
  8.1 0.8 %copy-start.1 = (s32[128,128]{1,0:T(8,128)S(1)}, s32[128,128]{1,0:T(8,128)}, u32[]{:S(2)}) copy-start(s32[128,128]{1,0:T(8,128)} %index_ref.1) | copy-start | bytes 196612
  8.9 12.2 %copy-start.2 = (bf16[128,128,256]{2,1,0:T(8,128)(2,1)S(1)}, bf16[128,128,256]{2,1,0:T(8,128)(2,1)}, u32[]{:S(2)}) copy-start(bf16[128,128,256]{2,1,0:T(8,128)(2,1)} %param.23) | copy-start | bytes 25165828
  21.1 1.6 %copy-start.8 = (s32[128,1]{0,1:T(1,128)S(1)}, s32[128,1]{0,1:T(1,128)}, u32[]{:S(2)}) copy-start(s32[128,1]{0,1:T(1,128)} %param.22) | copy-start | bytes 1540
  21.2 15.7 %copy-start.5 = (f32[8,16,256]{2,1,0:T(8,128)S(1)}, f32[8,16,256]{2,1,0:T(8,128)}, u32[]{:S(2)}) copy-start(f32[8,16,256]{2,1,0:T(8,128)} %param.25) | copy-start | bytes 393220
  21.2 30.3 %copy-start.7 = (f32[8]{0:T(128)S(1)}, f32[8]{0:T(128)}, u32[]{:S(2)}) copy-start(f32[8]{0:T(128)} %param.27) | copy-start | bytes 100
  25.4 25.6 %all-to-all-start = ((bf16[128,2,1280]{2,1,0:T(2,128)(2,1)}), bf16[128,2,1280]{2,1,0:T(2,128)(2,1)S(1)}, u32[]{:S(2)}, u32[]{:S(2)}) async-start(bf16[128,2,1280]{2,1,0:T(2,128)(2,1)} %pad_maximum_fusion), calls=%async_computation | async-start | bytes 1310720 | tf_op jit(solution)/shard_map/all_to_all | solution.py:148

commit v10 on v9

--- a/solution.py
+++ b/solution.py
@@ -106,6 +106,45 @@
     return jnp.stack(result, axis=1)
 
 
+def surface_kernel(state_ref, coupling_ref, out_ref):
+    fields, levels, columns = state_ref.shape
+    zero_row = jnp.zeros((1, columns), jnp.float32)
+    ratios = []
+    partial_value = [[] for _ in range(fields)]
+    ratio_prev = None
+    for level in range(levels):
+        lower_c = coupling_ref[level - 1 : level, :] if level > 0 else zero_row
+        upper_c = coupling_ref[level : level + 1, :] if level < levels - 1 else zero_row
+        diagonal = 1.0 + lower_c + upper_c
+        pivot = diagonal if level == 0 else diagonal + lower_c * ratio_prev
+        for f in range(fields):
+            rhs = state_ref[f, level : level + 1, :]
+            if level == 0:
+                partial_value[f].append(rhs / pivot)
+            else:
+                partial_value[f].append((rhs + lower_c * partial_value[f][-1]) / pivot)
+        ratio_now = -upper_c / pivot if level < levels - 1 else zero_row
+        ratios.append(ratio_now)
+        ratio_prev = ratio_now
+    lowest = []
+    for f in range(fields):
+        result = partial_value[f][levels - 1]
+        for level in range(levels - 2, -1, -1):
+            result = partial_value[f][level] - ratios[level] * result
+        lowest.append(result)
+    out_ref[0:1, :] = jnp.sqrt(lowest[0] * lowest[0] + lowest[1] * lowest[1] + 0.25)
+    out_ref[1:2, :] = lowest[2]
+
+
+def surface_of(atm_state, mixing):
+    columns = atm_state.shape[2]
+    return pl.pallas_call(
+        surface_kernel,
+        out_shape=jax.ShapeDtypeStruct((2, columns), jnp.float32),
+        compiler_params=pltpu.CompilerParams(vmem_limit_bytes=8 * 1024 * 1024),
+    )(atm_state, mixing)
+
+
 def on_device(
     land_wind,
     land_moist,
@@ -126,9 +165,7 @@
     columns = atm_state.shape[2]
     nbins = blast_table.shape[1]
     devices = lax.axis_size(("sec", "tile"))
-    state = solve(atm_state, mixing, jnp.zeros((3,), jnp.float32))
-    speed = jnp.sqrt(state[0, 0] ** 2 + state[1, 0] ** 2 + 0.25)
-    surface = jnp.stack([speed, state[2, 0]]).astype(jnp.bfloat16).reshape(1, 2 * columns)
+    surface = surface_of(atm_state, mixing).astype(jnp.bfloat16).reshape(1, 2 * columns)
     base_thresh = threshold_table(mass_frac.shape[1])
     erodible = lookup(erod_map, land_index)
     emission = emit(land_wind, land_moist, texture, erodible, mass_frac, blast_table, base_thresh)

time: 61 us -> 56.6 us (0.928)
  other arithmetic: 8.12 us -> 5.88 us
  local copies, waits for them, and re-layouts: 5.83 us -> 3.75 us
    slice x2 -> x0, local copies, waits for them, and re-layouts: 1.24 us -> none  [the longest x1 1.24 us: solve(): part_now = right_side[:, level] / pivot]
    another operation x4 -> x1, other arithmetic: 1.06 us -> 0.03 us  [the longest x1 1.01 us: solve(): diagonal = 1.0 + lower_c[None] + upper_c[None] + sink_col]
    slice x1, other arithmetic: 0.97 us -> 0.02 us  [solve(): upper_c = coupling[level] if level < levels - 1 else zero_row]
    slice x1, local copies, waits for them, and re-layouts: 0.89 us -> 0.01 us  [solve(): upper_c = coupling[level] if level < levels - 1 else zero_row]
    unnamed x31 -> x35, local copies, waits for them, and re-layouts: 2.01 us -> 2.02 us
where the time goes in v10:
time: 56.6 us; the launch traced here: 56.2 us
  waiting for transfers between devices  14 us (25%)
  starting transfers between devices  11.5 us (20%)
  matrix products  10.5 us (19%)
  Pallas kernels  9.53 us (17%)
  other arithmetic  5.88 us (10%)
  local copies, waits for them, and re-layouts  3.75 us (7%)
  between operations  1.12 us (2%)
    all_to_all x1, waiting for transfers between devices, on_device(): lax.all_to_all(payload, ('sec', 'tile'), split_axis=0, concat_axis=0, til...  14 us
    all_to_all x1, starting transfers between devices, on_device(): lax.all_to_all(payload, ('sec', 'tile'), split_axis=0, concat_axis=0, til...  11.5 us
    pallas_call x1, Pallas kernels, lookup(): pl.pallas_call(lookup_kernel, out_shape=jax.ShapeDtypeStruct((rows, lanes...  9.36 us
    dot_general x1, matrix products, on_device(): jnp.einsum('gla,gka->kgl', regrid_w, picked, preferred_element_type=jnp.f...  5.63 us
    unnamed x35, local copies, waits for them, and re-layouts  2.02 us
    dot_general x1, matrix products, emit(): blasted = jnp.einsum('tkb,bnl->tknl', blast_table, salt, precision=high)  1.88 us
    concatenate x1, other arithmetic, on_device(): jnp.concatenate([outgoing.astype(jnp.bfloat16).reshape(devices, 2, half),...  1.43 us
    dot_general x1, matrix products, on_device(): jnp.einsum('gkl,gla->gka', emission, regrid_w, preferred_element_type=jnp...  1.19 us
  transfers between devices with their start and end apart: 1, of which 1 were waited for; matrix products, arithmetic and copies ran while one was open for 0% of the time, Pallas kernels for 0%

profile of v10, /device:TPU:1, one launch (start us, length us, event | category | flops | bytes accessed | tf_op | source)
XLA Modules:
  0.0 56.2 jit_solution(69046886882832710)
XLA Ops:
  0.7 1.0 %copy.42 = f32[256,128]{0,1:T(8,128)S(1)} copy(f32[256,128]{1,0:T(8,128)} %bitcast.86) | data formatting | bytes 262144 | tf_op jit(solution)/shard_map/reshape | solution.py:53
  1.8 0.9 %mul.1665 = f32[128,128]{1,0:T(8,128)S(1)} multiply(f32[128,128]{1,0:T(8,128)} %param.15, f32[128,128]{1,0:T(8,128)} %param.15) | non-fusion elementwise | flops 16384 | bytes 196608 | tf_op jit(solution)/shard_map/mul | solution.py:26
  2.7 0.9 %fusion.11 = f32[4,128,128]{2,0,1:T(4,128)S(1)} fusion(s32[128,128]{1,0:T(8,128)} %param.17), kind=kLoop, calls=%fused_computation.22 | loop fusion | flops 131072 | bytes 327680 | tf_op jit(solution)/shard_map/convert_element_type | solution.py:18
  3.7 0.8 %copy-done.3 = s32[128,128]{1,0:T(8,128)S(1)} copy-done((s32[128,128]{1,0:T(8,128)S(1)}, s32[128,128]{1,0:T(8,128)}, u32[]{:S(2)}) %copy-start.3) | copy-done | bytes 65560
  4.5 9.4 %shard_map.140 = f32[128,128]{1,0:T(8,128)S(1)} custom-call(s32[128,128]{1,0:T(8,128)S(1)} %copy-done.3, bf16[128,768]{1,0:T(8,128)(2,1)S(1)} %maximum_bitcast_fusion.parts_ref), custom_call_target="tpu_custom_call" | custom-call | flops 3221225472 | bytes 327680 | tf_op jit(solution)/shard_map/pallas_call | solution.py:60
  13.9 0.8 %fusion.4 = f32[12,128,128,1]{2,0,3,1:T(8,128)S(1)} fusion(f32[128,128]{1,0:T(8,128)S(1)} %mul.1665, f32[128,128]{1,0:T(8,128)S(1)} %get-tuple-element.86, f32[12]{0:T(128)S(1)} %multiply_sqrt_fusion, f32[128,128]{1,0:T(8,128)S(1)} %copy-done.5, f32[128,128]{1,0:T(8,128)S(1)} %get-tuple-element.87, s32[128,128]{1,0:T(8,128)S(1)} %copy-done.8, ...), kind=kOutput, calls=%fused_computation.9 | convolution fusion | flops 11075584 | bytes 1114352 | tf_op jit(solution)/shard_map/tb,tnl->bnl/dot_general | solution.py:19
  14.8 1.9 %fusion = bf16[8,128,128]{2,0,1:T(8,128)(2,1)S(1)} fusion(f32[12,128,128,1]{2,0,3,1:T(8,128)S(1)} %fusion.4, f32[4,128,128]{2,0,1:T(4,128)S(1)} %fusion.11, f32[4,8,12]{2,1,0:T(8,128)S(1)} %copy-done), kind=kOutput, calls=%fused_computation.2 | convolution fusion | flops 76414976 | bytes 1312256 | tf_op jit(solution)/shard_map/tkb,bnl->tknl/dot_general | solution.py:28
  16.8 1.2 %fusion.8 = f32[128,8,256]{2,1,0:T(8,128)S(1)} fusion(bf16[128,128,256]{2,1,0:T(8,128)(2,1)S(1)} %copy-done.4, bf16[128,8,128]{2,0,1:T(8,128)(2,1)S(1)} %bitcast.80), kind=kOutput, calls=%fused_computation.18 | convolution fusion | flops 67108864 | bytes 9699328 | tf_op jit(solution)/shard_map/gkl,gla->gka/dot_general | solution.py:172
  18.0 0.3 copy.86
  18.3 0.7 %convolution_convert_fusion = bf16[128,2048]{1,0:T(8,128)(2,1)S(1)} fusion(f32[128,2048]{1,0:T(8,128)S(1)} %bitcast.79, s32[128]{0:T(128)S(1)} %bitcast.206), kind=kOutput, calls=%fused_computation | convolution fusion | flops 402931712 | bytes 1573376 | tf_op jit(solution)/shard_map/dot_general | solution.py:179
  19.1 0.4 reshape.27137
  19.5 0.2 shard_map.141
  19.7 1.4 %pad_maximum_fusion = bf16[128,2,1280]{2,1,0:T(2,128)(2,1)} fusion(bf16[128,2,256]{2,1,0:T(2,128)(2,1)S(1)} %broadcast_in_dim.2, bf16[128,2,1024]{2,1,0:T(2,128)(2,1)S(1)} %reshape.27137), kind=kLoop, calls=%fused_computation.15 | loop fusion | flops 1310720 | bytes 1310720 | tf_op jit(solution)/shard_map/concatenate | solution.py:182
  21.2 11.5 %all-to-all-start = ((bf16[128,2,1280]{2,1,0:T(2,128)(2,1)}), bf16[128,2,1280]{2,1,0:T(2,128)(2,1)S(1)}, u32[]{:S(2)}, u32[]{:S(2)}) async-start(bf16[128,2,1280]{2,1,0:T(2,128)(2,1)} %pad_maximum_fusion), calls=%async_computation | async-start | bytes 1310720 | tf_op jit(solution)/shard_map/all_to_all | solution.py:185
  32.8 14.0 %all-to-all-done = bf16[128,2,1280]{2,1,0:T(2,128)(2,1)S(1)} async-done(((bf16[128,2,1280]{2,1,0:T(2,128)(2,1)}), bf16[128,2,1280]{2,1,0:T(2,128)(2,1)S(1)}, u32[]{:S(2)}, u32[]{:S(2)}) %all-to-all-start) | async-done | bytes 655392 | tf_op jit(solution)/shard_map/all_to_all | solution.py:185
  46.8 0.5 convert_reduce_fusion
  47.3 0.2 fusion.24
  47.5 0.2 constant_dynamic-update-slice_fusion.15
  48.3 0.1 constant_dynamic-update-slice_fusion.1
  48.6 0.7 %copy.65 = f32[8,16,256]{2,1,0:T(8,128)} copy(f32[8,16,256]{2,0,1:T(8,128)S(1)} %constant_dynamic-update-slice_fusion) | data formatting | bytes 262144
  49.4 0.2 convolution_convert_fusion.1
  49.7 5.6 %convolution_bitcast_fusion = f32[3,128,128]{2,0,1:T(4,128)S(1)} fusion(bf16[128,128,256]{2,1,0:T(8,128)(2,1)} %param.23, bf16[128,2,256]{2,1,0:T(2,128)(2,1)S(1)} %reshape.27139), kind=kOutput, calls=%fused_computation.10 | convolution fusion | flops 25165824 | bytes 8716288 | tf_op jit(solution)/shard_map/gla,gka->kgl/dot_general | solution.py:194
  55.3 0.2 fusion.41
  55.5 0.7 %pad_maximum_fusion.1 = f32[2,128,128]{2,1,0:T(8,128)} fusion(f32[1,128,128]{2,1,0:T(8,128)S(1)} %add_bitcast_fusion, f32[1,128,128]{2,1,0:T(8,128)S(1)} %div.1372), kind=kLoop, calls=%fused_computation.29 | loop fusion | flops 32768 | bytes 262144 | tf_op jit(solution)/shard_map/stack | solution.py:196
  (55 shorter events, 1.3 us)
Async XLA Ops:
  0.6 14.1 %copy-start = (f32[4,8,12]{2,1,0:T(8,128)S(1)}, f32[4,8,12]{2,1,0:T(8,128)}, u32[]{:S(2)}) copy-start(f32[4,8,12]{2,1,0:T(8,128)} %param.21) | copy-start | bytes 4612
  0.6 13.3 %copy-start.5 = (f32[128,128]{1,0:T(8,128)S(1)}, f32[128,128]{1,0:T(8,128)}, u32[]{:S(2)}) copy-start(f32[128,128]{1,0:T(8,128)} %param.15) | copy-start | bytes 196612
  0.7 13.3 %copy-start.8 = (s32[128,128]{1,0:T(8,128)S(1)}, s32[128,128]{1,0:T(8,128)}, u32[]{:S(2)}) copy-start(s32[128,128]{1,0:T(8,128)} %param.17) | copy-start | bytes 196612
  0.7 13.2 %copy-start.6 = (f32[128,128]{1,0:T(8,128)S(1)}, f32[128,128]{1,0:T(8,128)}, u32[]{:S(2)}) copy-start(f32[128,128]{1,0:T(8,128)} %param.16) | copy-start | bytes 196612
  0.7 13.3 %copy-start.11 = (f32[4,12]{1,0:T(4,128)S(1)}, f32[4,12]{1,0:T(4,128)}, u32[]{:S(2)}) copy-start(f32[4,12]{1,0:T(4,128)} %param.20) | copy-start | bytes 580
  3.6 0.8 %copy-start.3 = (s32[128,128]{1,0:T(8,128)S(1)}, s32[128,128]{1,0:T(8,128)}, u32[]{:S(2)}) copy-start(s32[128,128]{1,0:T(8,128)} %index_ref.1) | copy-start | bytes 196612
  4.5 12.2 %copy-start.4 = (bf16[128,128,256]{2,1,0:T(8,128)(2,1)S(1)}, bf16[128,128,256]{2,1,0:T(8,128)(2,1)}, u32[]{:S(2)}) copy-start(bf16[128,128,256]{2,1,0:T(8,128)(2,1)} %param.23) | copy-start | bytes 25165828
  16.7 1.6 %copy-start.10 = (s32[128,1]{0,1:T(1,128)S(1)}, s32[128,1]{0,1:T(1,128)}, u32[]{:S(2)}) copy-start(s32[128,1]{0,1:T(1,128)} %param.22) | copy-start | bytes 1540
  16.7 2.7 %copy-start.1 = (f32[15,256]{1,0:T(8,128)S(1)}, f32[15,256]{1,0:T(8,128)}, u32[]{:S(2)}) copy-start(f32[15,256]{1,0:T(8,128)} %coupling_ref.1) | copy-start | bytes 46084
  16.8 2.7 %copy-start.2 = (f32[3,16,256]{2,1,0:T(8,128)S(1)}, f32[3,16,256]{2,1,0:T(8,128)}, u32[]{:S(2)}) copy-start(f32[3,16,256]{2,1,0:T(8,128)} %state_ref.1) | copy-start | bytes 147460
  16.8 16.0 %copy-start.7 = (f32[8,16,256]{2,1,0:T(8,128)S(1)}, f32[8,16,256]{2,1,0:T(8,128)}, u32[]{:S(2)}) copy-start(f32[8,16,256]{2,1,0:T(8,128)} %param.25) | copy-start | bytes 393220
  18.0 29.3 %copy-start.9 = (f32[8]{0:T(128)S(1)}, f32[8]{0:T(128)}, u32[]{:S(2)}) copy-start(f32[8]{0:T(128)} %param.27) | copy-start | bytes 100
  21.2 25.6 %all-to-all-start = ((bf16[128,2,1280]{2,1,0:T(2,128)(2,1)}), bf16[128,2,1280]{2,1,0:T(2,128)(2,1)S(1)}, u32[]{:S(2)}, u32[]{:S(2)}) async-start(bf16[128,2,1280]{2,1,0:T(2,128)(2,1)} %pad_maximum_fusion), calls=%async_computation | async-start | bytes 1310720 | tf_op jit(solution)/shard_map/all_to_all | solution.py:185

commit v11 on v10

--- a/solution.py
+++ b/solution.py
@@ -16,7 +16,9 @@
     thresh = base_thresh[:, None, None] * jnp.sqrt(1.0 + 12.1 * moist_rows)[None]
     classes = jnp.arange(mass_frac.shape[0])
     onehot = (texture_rows[None] == classes[:, None, None]).astype(jnp.float32)
-    fraction = jnp.einsum("tb,tnl->bnl", mass_frac, onehot, precision=high)
+    fraction = jnp.zeros((mass_frac.shape[1],) + texture_rows.shape, jnp.float32)
+    for t in range(mass_frac.shape[0]):
+        fraction = jnp.where(texture_rows[None] == t, mass_frac[t][:, None, None], fraction)
     speed = wind_rows[None]
     salt = (
         40.0
@@ -30,9 +32,20 @@
     return jnp.transpose(emission, (1, 0, 2)).astype(jnp.bfloat16)
 
 
-def lookup_kernel(index_ref, parts_ref, out_ref):
+def lookup_kernel(index_ref, table_ref, out_ref, parts_ref):
     rows_per_step, lanes = index_ref.shape
-    segments = parts_ref.shape[1] // 3
+    segments = table_ref.shape[0]
+
+    @pl.when(pl.program_id(0) == 0)
+    def _():
+        grid = table_ref[...]
+        first = grid.astype(jnp.bfloat16)
+        rest = grid - first.astype(jnp.float32)
+        second = rest.astype(jnp.bfloat16)
+        third = rest - second.astype(jnp.float32)
+        for p, part in enumerate((first.astype(jnp.float32), second.astype(jnp.float32), third)):
+            parts_ref[:, p * segments : (p + 1) * segments] = part.T.astype(jnp.bfloat16)
+
     levels = lax.broadcasted_iota(jnp.int32, (segments, lanes), 0).astype(jnp.bfloat16)
     lane_rows = lax.broadcasted_iota(jnp.int32, (128, lanes), 0)
     one = jnp.ones((segments, lanes), jnp.bfloat16)
@@ -50,11 +63,6 @@
 
 def lookup(table, index):
     segments = table.shape[0] // 128
-    grid = table.reshape(segments, 128)
-    first_wide = lax.reduce_precision(grid, exponent_bits=8, mantissa_bits=7)
-    rest = grid - first_wide
-    second_wide = lax.reduce_precision(rest, exponent_bits=8, mantissa_bits=7)
-    parts = jnp.concatenate([first_wide, second_wide, rest - second_wide], axis=0).T.astype(jnp.bfloat16)
     rows, lanes = index.shape
     step = 8
     return pl.pallas_call(
@@ -63,15 +71,16 @@
         grid=(rows // step,),
         in_specs=[
             pl.BlockSpec((step, lanes), lambda i: (i, 0)),
-            pl.BlockSpec((128, 3 * segments), lambda i: (0, 0)),
+            pl.BlockSpec((segments, 128), lambda i: (0, 0)),
         ],
         out_specs=pl.BlockSpec((step, lanes), lambda i: (i, 0)),
+        scratch_shapes=[pltpu.VMEM((128, 3 * segments), jnp.bfloat16)],
         compiler_params=pltpu.CompilerParams(vmem_limit_bytes=8 * 1024 * 1024),
         cost_estimate=pl.CostEstimate(
             flops=2 * 384 * segments * rows * lanes, transcendentals=0,
-            bytes_accessed=8 * rows * lanes + 768 * segments,
+            bytes_accessed=8 * rows * lanes + 512 * segments,
         ),
-    )(index, parts)
+    )(index, table.reshape(segments, 128))
 
 def solve(right_side, coupling, sinking):
     levels = right_side.shape[1]

time: 56.6 us -> 58.4 us (1.032)
  other arithmetic: 5.88 us -> 6.76 us
  local copies, waits for them, and re-layouts: 3.75 us -> 4.45 us
    reshape x1 -> x0, local copies, waits for them, and re-layouts: 1.04 us -> none  [lookup(): grid = table.reshape(segments, 128)]
    eq x0 -> x1, other arithmetic: none -> 0.93 us  [emit(): texture_rows[None] == t]
    unnamed x35 -> x33, local copies, waits for them, and re-layouts: 2.02 us -> 2.91 us
    broadcast_in_dim x0 -> x1, local copies, waits for them, and re-layouts: none -> 0.84 us  [emit(): jnp.where(texture_rows[None] == t, mass_frac[t][:, None, None], fraction)]
    dot_general x1 -> x0, matrix products: 0.83 us -> none  [emit(): fraction = jnp.einsum('tb,tnl->bnl', mass_frac, onehot, precision=high)]
    dot_general x1, matrix products: 1.88 us -> 2.66 us  [emit(): blasted = jnp.einsum('tkb,bnl->tknl', blast_table, salt, precision=high)]
where the time goes in v11:
time: 58.4 us; the launch traced here: 58 us
  waiting for transfers between devices  14 us (24%)
  starting transfers between devices  11.4 us (20%)
  matrix products  10.4 us (18%)
  Pallas kernels  9.97 us (17%)
  other arithmetic  6.76 us (12%)
  local copies, waits for them, and re-layouts  4.45 us (8%)
  between operations  1.06 us (2%)
    all_to_all x1, waiting for transfers between devices, on_device(): lax.all_to_all(payload, ('sec', 'tile'), split_axis=0, concat_axis=0, til...  14 us
    all_to_all x1, starting transfers between devices, on_device(): lax.all_to_all(payload, ('sec', 'tile'), split_axis=0, concat_axis=0, til...  11.4 us
    pallas_call x1, Pallas kernels, lookup(): pl.pallas_call(lookup_kernel, out_shape=jax.ShapeDtypeStruct((rows, lanes...  9.8 us
    dot_general x1, matrix products, on_device(): jnp.einsum('gla,gka->kgl', regrid_w, picked, preferred_element_type=jnp.f...  5.63 us
    unnamed x33, local copies, waits for them, and re-layouts  2.91 us
    dot_general x1, matrix products, emit(): blasted = jnp.einsum('tkb,bnl->tknl', blast_table, salt, precision=high)  2.66 us
    concatenate x1, other arithmetic, on_device(): jnp.concatenate([outgoing.astype(jnp.bfloat16).reshape(devices, 2, half),...  1.43 us
    dot_general x1, matrix products, on_device(): jnp.einsum('gkl,gla->gka', emission, regrid_w, preferred_element_type=jnp...  1.19 us
  transfers between devices with their start and end apart: 1, of which 1 were waited for; matrix products, arithmetic and copies ran while one was open for 0% of the time, Pallas kernels for 0%

profile of v11, /device:TPU:1, one launch (start us, length us, event | category | flops | bytes accessed | tf_op | source)
XLA Modules:
  0.0 58.0 jit_solution(1008312360862367282)
XLA Ops:
  0.7 0.9 %broadcast_compare_fusion.3 = (pred[128,128]{1,0:T(8,128)(4,1)S(1)}, pred[128,128]{1,0:T(8,128)(4,1)S(1)}, pred[128,128]{1,0:T(8,128)(4,1)S(1)}, pred[128,128]{1,0:T(8,128)(4,1)S(1)}) fusion(s32[128,128]{1,0:T(8,128)} %param.17), kind=kLoop, calls=%fused_computation.67 | loop fusion | flops 65536 | bytes 131072 | tf_op jit(solution)/shard_map/eq | solution.py:21
  1.6 0.9 %fusion.31 = f32[4,128,128]{2,0,1:T(4,128)S(1)} fusion(s32[128,128]{1,0:T(8,128)} %param.17), kind=kLoop, calls=%fused_computation.39 | loop fusion | flops 131072 | bytes 327680 | tf_op jit(solution)/shard_map/convert_element_type | solution.py:18
  2.5 0.8 %slice_bitcast_fusion.3 = (f32[12]{0:T(128)S(1)}, f32[12]{0:T(128)S(1)}, f32[12]{0:T(128)S(1)}, f32[12]{0:T(128)S(1)}) fusion(f32[4,12]{1,0:T(4,128)} %param.20), kind=kLoop, calls=%fused_computation.167 | loop fusion | bytes 384 | tf_op jit(solution)/shard_map/jit(_where)/broadcast_in_dim | solution.py:21
  3.4 0.9 %mul.1661 = f32[128,128]{1,0:T(8,128)S(1)} multiply(f32[128,128]{1,0:T(8,128)} %param.15, f32[128,128]{1,0:T(8,128)} %param.15) | non-fusion elementwise | flops 16384 | bytes 196608 | tf_op jit(solution)/shard_map/mul | solution.py:28
  4.3 0.9 %copy-done.3 = f32[32768]{0:T(1024)S(1)} copy-done((f32[32768]{0:T(1024)S(1)}, f32[32768]{0:T(1024)}, u32[]{:S(2)}) %copy-start.3) | copy-done | bytes 131096
  5.2 0.8 %copy-done.4 = s32[128,128]{1,0:T(8,128)S(1)} copy-done((s32[128,128]{1,0:T(8,128)S(1)}, s32[128,128]{1,0:T(8,128)}, u32[]{:S(2)}) %copy-start.4) | copy-done | bytes 65560
  6.0 9.8 %shard_map.140 = f32[128,128]{1,0:T(8,128)S(1)} custom-call(s32[128,128]{1,0:T(8,128)S(1)} %copy-done.4, f32[256,128]{1,0:T(8,128)S(1)} %bitcast.73), custom_call_target="tpu_custom_call" | custom-call | flops 3221225472 | bytes 262144 | tf_op jit(solution)/shard_map/pallas_call | solution.py:68
  15.9 2.7 %fusion = bf16[8,128,128]{2,0,1:T(8,128)(2,1)S(1)} fusion(f32[4,128,128]{2,0,1:T(4,128)S(1)} %fusion.31, f32[128,128]{1,0:T(8,128)S(1)} %mul.1661, f32[128,128]{1,0:T(8,128)S(1)} %get-tuple-element.91, f32[12]{0:T(128)S(1)} %multiply_sqrt_fusion, f32[128,128]{1,0:T(8,128)S(1)} %copy-done.6, f32[128,128]{1,0:T(8,128)S(1)} %get-tuple-element.92, ...), kind=kOutput, calls=%fused_computation.2 | convolution fusion | flops 78774272 | bytes 853744 | tf_op jit(solution)/shard_map/tkb,bnl->tknl/dot_general | solution.py:30
  18.7 1.2 %fusion.28 = f32[128,8,256]{2,1,0:T(8,128)S(1)} fusion(bf16[128,128,256]{2,1,0:T(8,128)(2,1)S(1)} %copy-done.5, bf16[128,8,128]{2,0,1:T(8,128)(2,1)S(1)} %bitcast.76), kind=kOutput, calls=%fused_computation.35 | convolution fusion | flops 67108864 | bytes 9699328 | tf_op jit(solution)/shard_map/gkl,gla->gka/dot_general | solution.py:181
  19.9 0.3 copy.80
  20.2 0.7 %convolution_convert_fusion = bf16[128,2048]{1,0:T(8,128)(2,1)S(1)} fusion(f32[128,2048]{1,0:T(8,128)S(1)} %bitcast.75, s32[128]{0:T(128)S(1)} %bitcast.201), kind=kOutput, calls=%fused_computation | convolution fusion | flops 402931712 | bytes 1573376 | tf_op jit(solution)/shard_map/dot_general | solution.py:188
  21.0 0.4 reshape.27149
  21.4 0.2 shard_map.141
  21.6 1.4 %pad_maximum_fusion = bf16[128,2,1280]{2,1,0:T(2,128)(2,1)} fusion(bf16[128,2,256]{2,1,0:T(2,128)(2,1)S(1)} %broadcast_in_dim.85, bf16[128,2,1024]{2,1,0:T(2,128)(2,1)S(1)} %reshape.27149), kind=kLoop, calls=%fused_computation.18 | loop fusion | flops 1310720 | bytes 1310720 | tf_op jit(solution)/shard_map/concatenate | solution.py:191
  23.1 11.4 %all-to-all-start = ((bf16[128,2,1280]{2,1,0:T(2,128)(2,1)}), bf16[128,2,1280]{2,1,0:T(2,128)(2,1)S(1)}, u32[]{:S(2)}, u32[]{:S(2)}) async-start(bf16[128,2,1280]{2,1,0:T(2,128)(2,1)} %pad_maximum_fusion), calls=%async_computation | async-start | bytes 1310720 | tf_op jit(solution)/shard_map/all_to_all | solution.py:194
  34.6 14.0 %all-to-all-done = bf16[128,2,1280]{2,1,0:T(2,128)(2,1)S(1)} async-done(((bf16[128,2,1280]{2,1,0:T(2,128)(2,1)}), bf16[128,2,1280]{2,1,0:T(2,128)(2,1)S(1)}, u32[]{:S(2)}, u32[]{:S(2)}) %all-to-all-start) | async-done | bytes 655392 | tf_op jit(solution)/shard_map/all_to_all | solution.py:194
  48.6 0.5 convert_reduce_fusion
  49.1 0.2 fusion.42
  49.3 0.2 constant_dynamic-update-slice_fusion.15
  50.4 0.7 %copy.59 = f32[8,16,256]{2,1,0:T(8,128)} copy(f32[8,16,256]{2,0,1:T(8,128)S(1)} %constant_dynamic-update-slice_fusion) | data formatting | bytes 262144
  51.2 0.2 convolution_convert_fusion.1
  51.5 5.6 %convolution_bitcast_fusion = f32[3,128,128]{2,0,1:T(4,128)S(1)} fusion(bf16[128,128,256]{2,1,0:T(8,128)(2,1)} %param.23, bf16[128,2,256]{2,1,0:T(2,128)(2,1)S(1)} %reshape.27151), kind=kOutput, calls=%fused_computation.5 | convolution fusion | flops 25165824 | bytes 8716288 | tf_op jit(solution)/shard_map/gla,gka->kgl/dot_general | solution.py:203
  57.1 0.2 fusion.59
  57.3 0.7 %pad_maximum_fusion.1 = f32[2,128,128]{2,1,0:T(8,128)} fusion(f32[1,128,128]{2,1,0:T(8,128)S(1)} %add_bitcast_fusion, f32[1,128,128]{2,1,0:T(8,128)S(1)} %div.1372), kind=kLoop, calls=%fused_computation.40 | loop fusion | flops 32768 | bytes 262144 | tf_op jit(solution)/shard_map/stack | solution.py:205
  (51 shorter events, 1.3 us)
Async XLA Ops:
  0.6 15.3 %copy-start = (f32[4,8,12]{2,1,0:T(8,128)S(1)}, f32[4,8,12]{2,1,0:T(8,128)}, u32[]{:S(2)}) copy-start(f32[4,8,12]{2,1,0:T(8,128)} %param.21) | copy-start | bytes 4612
  0.6 15.3 %copy-start.6 = (f32[128,128]{1,0:T(8,128)S(1)}, f32[128,128]{1,0:T(8,128)}, u32[]{:S(2)}) copy-start(f32[128,128]{1,0:T(8,128)} %param.15) | copy-start | bytes 196612
  0.7 15.2 %copy-start.7 = (f32[128,128]{1,0:T(8,128)S(1)}, f32[128,128]{1,0:T(8,128)}, u32[]{:S(2)}) copy-start(f32[128,128]{1,0:T(8,128)} %param.16) | copy-start | bytes 196612
  4.3 0.9 %copy-start.3 = (f32[32768]{0:T(1024)S(1)}, f32[32768]{0:T(1024)}, u32[]{:S(2)}) copy-start(f32[32768]{0:T(1024)} %param.19) | copy-start | bytes 393220
  5.2 0.8 %copy-start.4 = (s32[128,128]{1,0:T(8,128)S(1)}, s32[128,128]{1,0:T(8,128)}, u32[]{:S(2)}) copy-start(s32[128,128]{1,0:T(8,128)} %index_ref.1) | copy-start | bytes 196612
  6.0 12.6 %copy-start.5 = (bf16[128,128,256]{2,1,0:T(8,128)(2,1)S(1)}, bf16[128,128,256]{2,1,0:T(8,128)(2,1)}, u32[]{:S(2)}) copy-start(bf16[128,128,256]{2,1,0:T(8,128)(2,1)} %param.23) | copy-start | bytes 25165828
  18.6 1.6 %copy-start.10 = (s32[128,1]{0,1:T(1,128)S(1)}, s32[128,1]{0,1:T(1,128)}, u32[]{:S(2)}) copy-start(s32[128,1]{0,1:T(1,128)} %param.22) | copy-start | bytes 1540
  18.6 2.7 %copy-start.1 = (f32[15,256]{1,0:T(8,128)S(1)}, f32[15,256]{1,0:T(8,128)}, u32[]{:S(2)}) copy-start(f32[15,256]{1,0:T(8,128)} %coupling_ref.1) | copy-start | bytes 46084
  18.7 2.7 %copy-start.2 = (f32[3,16,256]{2,1,0:T(8,128)S(1)}, f32[3,16,256]{2,1,0:T(8,128)}, u32[]{:S(2)}) copy-start(f32[3,16,256]{2,1,0:T(8,128)} %state_ref.1) | copy-start | bytes 147460
  18.7 15.9 %copy-start.8 = (f32[8,16,256]{2,1,0:T(8,128)S(1)}, f32[8,16,256]{2,1,0:T(8,128)}, u32[]{:S(2)}) copy-start(f32[8,16,256]{2,1,0:T(8,128)} %param.25) | copy-start | bytes 393220
  19.9 29.2 %copy-start.9 = (f32[8]{0:T(128)S(1)}, f32[8]{0:T(128)}, u32[]{:S(2)}) copy-start(f32[8]{0:T(128)} %param.27) | copy-start | bytes 100
  23.1 25.5 %all-to-all-start = ((bf16[128,2,1280]{2,1,0:T(2,128)(2,1)}), bf16[128,2,1280]{2,1,0:T(2,128)(2,1)S(1)}, u32[]{:S(2)}, u32[]{:S(2)}) async-start(bf16[128,2,1280]{2,1,0:T(2,128)(2,1)} %pad_maximum_fusion), calls=%async_computation | async-start | bytes 1310720 | tf_op jit(solution)/shard_map/all_to_all | solution.py:194

commit v12 on v11

--- a/solution.py
+++ b/solution.py
@@ -16,9 +16,7 @@
     thresh = base_thresh[:, None, None] * jnp.sqrt(1.0 + 12.1 * moist_rows)[None]
     classes = jnp.arange(mass_frac.shape[0])
     onehot = (texture_rows[None] == classes[:, None, None]).astype(jnp.float32)
-    fraction = jnp.zeros((mass_frac.shape[1],) + texture_rows.shape, jnp.float32)
-    for t in range(mass_frac.shape[0]):
-        fraction = jnp.where(texture_rows[None] == t, mass_frac[t][:, None, None], fraction)
+    fraction = jnp.einsum("tb,tnl->bnl", mass_frac, onehot, precision=high)
     speed = wind_rows[None]
     salt = (
         40.0

time: 58.4 us -> 58.4 us (level)
  other arithmetic: 6.76 us -> 5.83 us
  local copies, waits for them, and re-layouts: 4.45 us -> 5.12 us
    unnamed x33 -> x39, local copies, waits for them, and re-layouts: 2.91 us -> 4.43 us
    eq x1 -> x0, other arithmetic: 0.93 us -> none  [emit(): texture_rows[None] == t]
    broadcast_in_dim x1 -> x0, local copies, waits for them, and re-layouts: 0.84 us -> none  [emit(): jnp.where(texture_rows[None] == t, mass_frac[t][:, None, None], fraction)]
    dot_general x0 -> x1, matrix products: none -> 0.82 us  [emit(): fraction = jnp.einsum('tb,tnl->bnl', mass_frac, onehot, precision=high)]
    dot_general x1, matrix products: 2.66 us -> 1.88 us  [emit(): blasted = jnp.einsum('tkb,bnl->tknl', blast_table, salt, precision=high)]
where the time goes in v12:
time: 58.4 us; the launch traced here: 57.9 us
  waiting for transfers between devices  14 us (24%)
  starting transfers between devices  11.8 us (20%)
  matrix products  10.5 us (18%)
  Pallas kernels  9.68 us (17%)
  other arithmetic  5.83 us (10%)
  local copies, waits for them, and re-layouts  5.12 us (9%)
  between operations  1.06 us (2%)
    all_to_all x1, waiting for transfers between devices, on_device(): lax.all_to_all(payload, ('sec', 'tile'), split_axis=0, concat_axis=0, til...  14 us
    all_to_all x1, starting transfers between devices, on_device(): lax.all_to_all(payload, ('sec', 'tile'), split_axis=0, concat_axis=0, til...  11.8 us
    pallas_call x1, Pallas kernels, lookup(): pl.pallas_call(lookup_kernel, out_shape=jax.ShapeDtypeStruct((rows, lanes...  9.51 us
    dot_general x1, matrix products, on_device(): jnp.einsum('gla,gka->kgl', regrid_w, picked, preferred_element_type=jnp.f...  5.63 us
    unnamed x39, local copies, waits for them, and re-layouts  4.43 us
    dot_general x1, matrix products, emit(): blasted = jnp.einsum('tkb,bnl->tknl', blast_table, salt, precision=high)  1.88 us
    concatenate x1, other arithmetic, on_device(): jnp.concatenate([outgoing.astype(jnp.bfloat16).reshape(devices, 2, half),...  1.43 us
    dot_general x1, matrix products, on_device(): jnp.einsum('gkl,gla->gka', emission, regrid_w, preferred_element_type=jnp...  1.19 us
  transfers between devices with their start and end apart: 1, of which 1 were waited for; matrix products, arithmetic and copies ran while one was open for 0% of the time, Pallas kernels for 0%

profile of v12, /device:TPU:1, one launch (start us, length us, event | category | flops | bytes accessed | tf_op | source)
XLA Modules:
  0.0 57.9 jit_solution(7002850757248686154)
XLA Ops:
  0.7 0.7 %copy-done.1 = f32[15,256]{1,0:T(8,128)S(1)} copy-done((f32[15,256]{1,0:T(8,128)S(1)}, f32[15,256]{1,0:T(8,128)}, u32[]{:S(2)}) %copy-start.1) | copy-done | bytes 15384
  1.4 0.8 %copy-done.3 = f32[3,16,256]{2,1,0:T(8,128)S(1)} copy-done((f32[3,16,256]{2,1,0:T(8,128)S(1)}, f32[3,16,256]{2,1,0:T(8,128)}, u32[]{:S(2)}) %copy-start.3) | copy-done | bytes 49176
  2.2 0.2 shard_map.141
  2.4 0.9 %mul.1665 = f32[128,128]{1,0:T(8,128)S(1)} multiply(f32[128,128]{1,0:T(8,128)} %param.15, f32[128,128]{1,0:T(8,128)} %param.15) | non-fusion elementwise | flops 16384 | bytes 196608 | tf_op jit(solution)/shard_map/mul | solution.py:26
  3.3 0.9 %fusion.11 = f32[4,128,128]{2,0,1:T(4,128)S(1)} fusion(s32[128,128]{1,0:T(8,128)} %param.17), kind=kLoop, calls=%fused_computation.22 | loop fusion | flops 131072 | bytes 327680 | tf_op jit(solution)/shard_map/convert_element_type | solution.py:18
  4.2 0.9 %copy-done.4 = f32[32768]{0:T(1024)S(1)} copy-done((f32[32768]{0:T(1024)S(1)}, f32[32768]{0:T(1024)}, u32[]{:S(2)}) %copy-start.4) | copy-done | bytes 131096
  5.1 0.8 %copy-done.5 = s32[128,128]{1,0:T(8,128)S(1)} copy-done((s32[128,128]{1,0:T(8,128)S(1)}, s32[128,128]{1,0:T(8,128)}, u32[]{:S(2)}) %copy-start.5) | copy-done | bytes 65560
  6.0 9.5 %shard_map.140 = f32[128,128]{1,0:T(8,128)S(1)} custom-call(s32[128,128]{1,0:T(8,128)S(1)} %copy-done.5, f32[256,128]{1,0:T(8,128)S(1)} %bitcast.76), custom_call_target="tpu_custom_call" | custom-call | flops 3221225472 | bytes 262144 | tf_op jit(solution)/shard_map/pallas_call | solution.py:66
  15.6 0.8 %fusion.4 = f32[12,128,128,1]{2,0,3,1:T(8,128)S(1)} fusion(f32[128,128]{1,0:T(8,128)S(1)} %mul.1665, f32[128,128]{1,0:T(8,128)S(1)} %get-tuple-element.83, f32[12]{0:T(128)S(1)} %multiply_sqrt_fusion, f32[128,128]{1,0:T(8,128)S(1)} %copy-done.7, f32[128,128]{1,0:T(8,128)S(1)} %get-tuple-element.84, s32[128,128]{1,0:T(8,128)S(1)} %copy-done.10, ...), kind=kOutput, calls=%fused_computation.9 | convolution fusion | flops 11075584 | bytes 1114352 | tf_op jit(solution)/shard_map/tb,tnl->bnl/dot_general | solution.py:19
  16.4 1.9 %fusion = bf16[8,128,128]{2,0,1:T(8,128)(2,1)S(1)} fusion(f32[12,128,128,1]{2,0,3,1:T(8,128)S(1)} %fusion.4, f32[4,128,128]{2,0,1:T(4,128)S(1)} %fusion.11, f32[4,8,12]{2,1,0:T(8,128)S(1)} %copy-done), kind=kOutput, calls=%fused_computation.2 | convolution fusion | flops 76414976 | bytes 1312256 | tf_op jit(solution)/shard_map/tkb,bnl->tknl/dot_general | solution.py:28
  18.4 1.2 %fusion.8 = f32[128,8,256]{2,1,0:T(8,128)S(1)} fusion(bf16[128,128,256]{2,1,0:T(8,128)(2,1)S(1)} %copy-done.6, bf16[128,8,128]{2,0,1:T(8,128)(2,1)S(1)} %bitcast.79), kind=kOutput, calls=%fused_computation.18 | convolution fusion | flops 67108864 | bytes 9699328 | tf_op jit(solution)/shard_map/gkl,gla->gka/dot_general | solution.py:179
  19.6 0.3 copy.82
  19.9 0.7 %convolution_convert_fusion = bf16[128,2048]{1,0:T(8,128)(2,1)S(1)} fusion(f32[128,2048]{1,0:T(8,128)S(1)} %bitcast.78, s32[128]{0:T(128)S(1)} %bitcast.204), kind=kOutput, calls=%fused_computation | convolution fusion | flops 402931712 | bytes 1573376 | tf_op jit(solution)/shard_map/dot_general | solution.py:186
  20.7 0.4 reshape.27137
  21.1 1.4 %pad_maximum_fusion = bf16[128,2,1280]{2,1,0:T(2,128)(2,1)} fusion(bf16[128,2,256]{2,1,0:T(2,128)(2,1)S(1)} %broadcast_in_dim.2, bf16[128,2,1024]{2,1,0:T(2,128)(2,1)S(1)} %reshape.27137), kind=kLoop, calls=%fused_computation.15 | loop fusion | flops 1310720 | bytes 1310720 | tf_op jit(solution)/shard_map/concatenate | solution.py:189
  22.6 11.8 %all-to-all-start = ((bf16[128,2,1280]{2,1,0:T(2,128)(2,1)}), bf16[128,2,1280]{2,1,0:T(2,128)(2,1)S(1)}, u32[]{:S(2)}, u32[]{:S(2)}) async-start(bf16[128,2,1280]{2,1,0:T(2,128)(2,1)} %pad_maximum_fusion), calls=%async_computation | async-start | bytes 1310720 | tf_op jit(solution)/shard_map/all_to_all | solution.py:192
  34.5 14.0 %all-to-all-done = bf16[128,2,1280]{2,1,0:T(2,128)(2,1)S(1)} async-done(((bf16[128,2,1280]{2,1,0:T(2,128)(2,1)}), bf16[128,2,1280]{2,1,0:T(2,128)(2,1)S(1)}, u32[]{:S(2)}, u32[]{:S(2)}) %all-to-all-start) | async-done | bytes 655392 | tf_op jit(solution)/shard_map/all_to_all | solution.py:192
  48.6 0.2 convolution_convert_fusion.1
  48.9 5.6 %convolution_bitcast_fusion = f32[3,128,128]{2,0,1:T(4,128)S(1)} fusion(bf16[128,128,256]{2,1,0:T(8,128)(2,1)} %param.23, bf16[128,2,256]{2,1,0:T(2,128)(2,1)S(1)} %reshape.27139), kind=kOutput, calls=%fused_computation.10 | convolution fusion | flops 25165824 | bytes 8716288 | tf_op jit(solution)/shard_map/gla,gka->kgl/dot_general | solution.py:201
  54.5 0.2 fusion.40
  54.7 0.5 convert_reduce_fusion
  55.4 0.2 constant_dynamic-update-slice_fusion.15
  56.5 0.7 %copy.61 = f32[8,16,256]{2,1,0:T(8,128)} copy(f32[8,16,256]{2,0,1:T(8,128)S(1)} %constant_dynamic-update-slice_fusion) | data formatting | bytes 262144
  57.2 0.7 %pad_maximum_fusion.1 = f32[2,128,128]{2,1,0:T(8,128)} fusion(f32[1,128,128]{2,1,0:T(8,128)S(1)} %add_bitcast_fusion, f32[1,128,128]{2,1,0:T(8,128)S(1)} %div.1372), kind=kLoop, calls=%fused_computation.23 | loop fusion | flops 32768 | bytes 262144 | tf_op jit(solution)/shard_map/stack | solution.py:203
  (56 shorter events, 1.5 us)
Async XLA Ops:
  0.6 15.8 %copy-start = (f32[4,8,12]{2,1,0:T(8,128)S(1)}, f32[4,8,12]{2,1,0:T(8,128)}, u32[]{:S(2)}) copy-start(f32[4,8,12]{2,1,0:T(8,128)} %param.21) | copy-start | bytes 4612
  0.7 0.7 %copy-start.1 = (f32[15,256]{1,0:T(8,128)S(1)}, f32[15,256]{1,0:T(8,128)}, u32[]{:S(2)}) copy-start(f32[15,256]{1,0:T(8,128)} %coupling_ref.1) | copy-start | bytes 46084
  1.4 0.8 %copy-start.3 = (f32[3,16,256]{2,1,0:T(8,128)S(1)}, f32[3,16,256]{2,1,0:T(8,128)}, u32[]{:S(2)}) copy-start(f32[3,16,256]{2,1,0:T(8,128)} %state_ref.1) | copy-start | bytes 147460
  2.2 13.3 %copy-start.8 = (f32[128,128]{1,0:T(8,128)S(1)}, f32[128,128]{1,0:T(8,128)}, u32[]{:S(2)}) copy-start(f32[128,128]{1,0:T(8,128)} %param.16) | copy-start | bytes 196612
  2.2 13.3 %copy-start.7 = (f32[128,128]{1,0:T(8,128)S(1)}, f32[128,128]{1,0:T(8,128)}, u32[]{:S(2)}) copy-start(f32[128,128]{1,0:T(8,128)} %param.15) | copy-start | bytes 196612
  2.2 13.4 %copy-start.10 = (s32[128,128]{1,0:T(8,128)S(1)}, s32[128,128]{1,0:T(8,128)}, u32[]{:S(2)}) copy-start(s32[128,128]{1,0:T(8,128)} %param.17) | copy-start | bytes 196612
  2.2 13.4 %copy-start.13 = (f32[4,12]{1,0:T(4,128)S(1)}, f32[4,12]{1,0:T(4,128)}, u32[]{:S(2)}) copy-start(f32[4,12]{1,0:T(4,128)} %param.20) | copy-start | bytes 580
  4.2 0.9 %copy-start.4 = (f32[32768]{0:T(1024)S(1)}, f32[32768]{0:T(1024)}, u32[]{:S(2)}) copy-start(f32[32768]{0:T(1024)} %param.19) | copy-start | bytes 393220
  5.1 0.8 %copy-start.5 = (s32[128,128]{1,0:T(8,128)S(1)}, s32[128,128]{1,0:T(8,128)}, u32[]{:S(2)}) copy-start(s32[128,128]{1,0:T(8,128)} %index_ref.1) | copy-start | bytes 196612
  6.0 12.4 %copy-start.6 = (bf16[128,128,256]{2,1,0:T(8,128)(2,1)S(1)}, bf16[128,128,256]{2,1,0:T(8,128)(2,1)}, u32[]{:S(2)}) copy-start(bf16[128,128,256]{2,1,0:T(8,128)(2,1)} %param.23) | copy-start | bytes 25165828
  18.3 1.6 %copy-start.12 = (s32[128,1]{0,1:T(1,128)S(1)}, s32[128,1]{0,1:T(1,128)}, u32[]{:S(2)}) copy-start(s32[128,1]{0,1:T(1,128)} %param.22) | copy-start | bytes 1540
  18.4 16.0 %copy-start.2 = (f32[15,256]{1,0:T(8,128)S(1)}, f32[15,256]{1,0:T(8,128)}, u32[]{:S(2)}) copy-start(f32[15,256]{1,0:T(8,128)} %coupling_ref.1) | copy-start | bytes 46084
  18.4 16.1 %copy-start.9 = (f32[8,16,256]{2,1,0:T(8,128)S(1)}, f32[8,16,256]{2,1,0:T(8,128)}, u32[]{:S(2)}) copy-start(f32[8,16,256]{2,1,0:T(8,128)} %param.25) | copy-start | bytes 393220
  19.9 35.3 %copy-start.11 = (f32[8]{0:T(128)S(1)}, f32[8]{0:T(128)}, u32[]{:S(2)}) copy-start(f32[8]{0:T(128)} %param.27) | copy-start | bytes 100
  22.6 25.9 %all-to-all-start = ((bf16[128,2,1280]{2,1,0:T(2,128)(2,1)}), bf16[128,2,1280]{2,1,0:T(2,128)(2,1)S(1)}, u32[]{:S(2)}, u32[]{:S(2)}) async-start(bf16[128,2,1280]{2,1,0:T(2,128)(2,1)} %pad_maximum_fusion), calls=%async_computation | async-start | bytes 1310720 | tf_op jit(solution)/shard_map/all_to_all | solution.py:192

commit v13 on v10

--- a/solution.py
+++ b/solution.py
@@ -56,7 +56,7 @@
     second_wide = lax.reduce_precision(rest, exponent_bits=8, mantissa_bits=7)
     parts = jnp.concatenate([first_wide, second_wide, rest - second_wide], axis=0).T.astype(jnp.bfloat16)
     rows, lanes = index.shape
-    step = 8
+    step = 32
     return pl.pallas_call(
         lookup_kernel,
         out_shape=jax.ShapeDtypeStruct((rows, lanes), jnp.float32),

time: 56.6 us -> 54.5 us (0.963)
  Pallas kernels: 9.53 us -> 7.46 us
    pallas_call x1, Pallas kernels: 9.36 us -> 7.29 us  [lookup(): pl.pallas_call(lookup_kernel, out_shape=jax.ShapeDtypeStruct((rows, lanes...]
where the time goes in v13:
time: 54.5 us; the launch traced here: 54.1 us
  waiting for transfers between devices  14 us (26%)
  starting transfers between devices  11.5 us (21%)
  matrix products  10.5 us (19%)
  Pallas kernels  7.46 us (14%)
  other arithmetic  5.88 us (11%)
  local copies, waits for them, and re-layouts  3.75 us (7%)
  between operations  1.12 us (2%)
    all_to_all x1, waiting for transfers between devices, on_device(): lax.all_to_all(payload, ('sec', 'tile'), split_axis=0, concat_axis=0, til...  14 us
    all_to_all x1, starting transfers between devices, on_device(): lax.all_to_all(payload, ('sec', 'tile'), split_axis=0, concat_axis=0, til...  11.5 us
    pallas_call x1, Pallas kernels, lookup(): pl.pallas_call(lookup_kernel, out_shape=jax.ShapeDtypeStruct((rows, lanes...  7.29 us
    dot_general x1, matrix products, on_device(): jnp.einsum('gla,gka->kgl', regrid_w, picked, preferred_element_type=jnp.f...  5.63 us
    unnamed x35, local copies, waits for them, and re-layouts  2.02 us
    dot_general x1, matrix products, emit(): blasted = jnp.einsum('tkb,bnl->tknl', blast_table, salt, precision=high)  1.88 us
    concatenate x1, other arithmetic, on_device(): jnp.concatenate([outgoing.astype(jnp.bfloat16).reshape(devices, 2, half),...  1.43 us
    dot_general x1, matrix products, on_device(): jnp.einsum('gkl,gla->gka', emission, regrid_w, preferred_element_type=jnp...  1.19 us
  transfers between devices with their start and end apart: 1, of which 1 were waited for; matrix products, arithmetic and copies ran while one was open for 0% of the time, Pallas kernels for 0%

profile of v13, /device:TPU:1, one launch (start us, length us, event | category | flops | bytes accessed | tf_op | source)
XLA Modules:
  0.0 54.1 jit_solution(16413070026608060926)
XLA Ops:
  0.7 1.0 %copy.42 = f32[256,128]{0,1:T(8,128)S(1)} copy(f32[256,128]{1,0:T(8,128)} %bitcast.86) | data formatting | bytes 262144 | tf_op jit(solution)/shard_map/reshape | solution.py:53
  1.8 0.9 %mul.1665 = f32[128,128]{1,0:T(8,128)S(1)} multiply(f32[128,128]{1,0:T(8,128)} %param.15, f32[128,128]{1,0:T(8,128)} %param.15) | non-fusion elementwise | flops 16384 | bytes 196608 | tf_op jit(solution)/shard_map/mul | solution.py:26
  2.7 0.9 %fusion.11 = f32[4,128,128]{2,0,1:T(4,128)S(1)} fusion(s32[128,128]{1,0:T(8,128)} %param.17), kind=kLoop, calls=%fused_computation.22 | loop fusion | flops 131072 | bytes 327680 | tf_op jit(solution)/shard_map/convert_element_type | solution.py:18
  3.7 0.8 %copy-done.3 = s32[128,128]{1,0:T(8,128)S(1)} copy-done((s32[128,128]{1,0:T(8,128)S(1)}, s32[128,128]{1,0:T(8,128)}, u32[]{:S(2)}) %copy-start.3) | copy-done | bytes 65560
  4.5 7.3 %shard_map.140 = f32[128,128]{1,0:T(8,128)S(1)} custom-call(s32[128,128]{1,0:T(8,128)S(1)} %copy-done.3, bf16[128,768]{1,0:T(8,128)(2,1)S(1)} %maximum_bitcast_fusion.parts_ref), custom_call_target="tpu_custom_call" | custom-call | flops 3221225472 | bytes 327680 | tf_op jit(solution)/shard_map/pallas_call | solution.py:60
  11.9 0.8 %fusion.4 = f32[12,128,128,1]{2,0,3,1:T(8,128)S(1)} fusion(f32[128,128]{1,0:T(8,128)S(1)} %mul.1665, f32[128,128]{1,0:T(8,128)S(1)} %get-tuple-element.86, f32[12]{0:T(128)S(1)} %multiply_sqrt_fusion, f32[128,128]{1,0:T(8,128)S(1)} %copy-done.5, f32[128,128]{1,0:T(8,128)S(1)} %get-tuple-element.87, s32[128,128]{1,0:T(8,128)S(1)} %copy-done.8, ...), kind=kOutput, calls=%fused_computation.9 | convolution fusion | flops 11075584 | bytes 1114352 | tf_op jit(solution)/shard_map/tb,tnl->bnl/dot_general | solution.py:19
  12.7 1.9 %fusion = bf16[8,128,128]{2,0,1:T(8,128)(2,1)S(1)} fusion(f32[12,128,128,1]{2,0,3,1:T(8,128)S(1)} %fusion.4, f32[4,128,128]{2,0,1:T(4,128)S(1)} %fusion.11, f32[4,8,12]{2,1,0:T(8,128)S(1)} %copy-done), kind=kOutput, calls=%fused_computation.2 | convolution fusion | flops 76414976 | bytes 1312256 | tf_op jit(solution)/shard_map/tkb,bnl->tknl/dot_general | solution.py:28
  14.7 1.2 %fusion.8 = f32[128,8,256]{2,1,0:T(8,128)S(1)} fusion(bf16[128,128,256]{2,1,0:T(8,128)(2,1)S(1)} %copy-done.4, bf16[128,8,128]{2,0,1:T(8,128)(2,1)S(1)} %bitcast.80), kind=kOutput, calls=%fused_computation.18 | convolution fusion | flops 67108864 | bytes 9699328 | tf_op jit(solution)/shard_map/gkl,gla->gka/dot_general | solution.py:172
  15.9 0.3 copy.86
  16.3 0.7 %convolution_convert_fusion = bf16[128,2048]{1,0:T(8,128)(2,1)S(1)} fusion(f32[128,2048]{1,0:T(8,128)S(1)} %bitcast.79, s32[128]{0:T(128)S(1)} %bitcast.206), kind=kOutput, calls=%fused_computation | convolution fusion | flops 402931712 | bytes 1573376 | tf_op jit(solution)/shard_map/dot_general | solution.py:179
  17.0 0.4 reshape.27137
  17.4 0.2 shard_map.141
  17.7 1.4 %pad_maximum_fusion = bf16[128,2,1280]{2,1,0:T(2,128)(2,1)} fusion(bf16[128,2,256]{2,1,0:T(2,128)(2,1)S(1)} %broadcast_in_dim.2, bf16[128,2,1024]{2,1,0:T(2,128)(2,1)S(1)} %reshape.27137), kind=kLoop, calls=%fused_computation.15 | loop fusion | flops 1310720 | bytes 1310720 | tf_op jit(solution)/shard_map/concatenate | solution.py:182
  19.1 11.5 %all-to-all-start = ((bf16[128,2,1280]{2,1,0:T(2,128)(2,1)}), bf16[128,2,1280]{2,1,0:T(2,128)(2,1)S(1)}, u32[]{:S(2)}, u32[]{:S(2)}) async-start(bf16[128,2,1280]{2,1,0:T(2,128)(2,1)} %pad_maximum_fusion), calls=%async_computation | async-start | bytes 1310720 | tf_op jit(solution)/shard_map/all_to_all | solution.py:185
  30.8 14.0 %all-to-all-done = bf16[128,2,1280]{2,1,0:T(2,128)(2,1)S(1)} async-done(((bf16[128,2,1280]{2,1,0:T(2,128)(2,1)}), bf16[128,2,1280]{2,1,0:T(2,128)(2,1)S(1)}, u32[]{:S(2)}, u32[]{:S(2)}) %all-to-all-start) | async-done | bytes 655392 | tf_op jit(solution)/shard_map/all_to_all | solution.py:185
  44.7 0.5 convert_reduce_fusion
  45.2 0.2 fusion.24
  45.4 0.2 constant_dynamic-update-slice_fusion.15
  46.2 0.1 constant_dynamic-update-slice_fusion.1
  46.5 0.7 %copy.65 = f32[8,16,256]{2,1,0:T(8,128)} copy(f32[8,16,256]{2,0,1:T(8,128)S(1)} %constant_dynamic-update-slice_fusion) | data formatting | bytes 262144
  47.3 0.2 convolution_convert_fusion.1
  47.6 5.6 %convolution_bitcast_fusion = f32[3,128,128]{2,0,1:T(4,128)S(1)} fusion(bf16[128,128,256]{2,1,0:T(8,128)(2,1)} %param.23, bf16[128,2,256]{2,1,0:T(2,128)(2,1)S(1)} %reshape.27139), kind=kOutput, calls=%fused_computation.10 | convolution fusion | flops 25165824 | bytes 8716288 | tf_op jit(solution)/shard_map/gla,gka->kgl/dot_general | solution.py:194
  53.2 0.2 fusion.41
  53.5 0.7 %pad_maximum_fusion.1 = f32[2,128,128]{2,1,0:T(8,128)} fusion(f32[1,128,128]{2,1,0:T(8,128)S(1)} %add_bitcast_fusion, f32[1,128,128]{2,1,0:T(8,128)S(1)} %div.1372), kind=kLoop, calls=%fused_computation.29 | loop fusion | flops 32768 | bytes 262144 | tf_op jit(solution)/shard_map/stack | solution.py:196
  (55 shorter events, 1.3 us)
Async XLA Ops:
  0.6 12.1 %copy-start = (f32[4,8,12]{2,1,0:T(8,128)S(1)}, f32[4,8,12]{2,1,0:T(8,128)}, u32[]{:S(2)}) copy-start(f32[4,8,12]{2,1,0:T(8,128)} %param.21) | copy-start | bytes 4612
  0.6 11.2 %copy-start.5 = (f32[128,128]{1,0:T(8,128)S(1)}, f32[128,128]{1,0:T(8,128)}, u32[]{:S(2)}) copy-start(f32[128,128]{1,0:T(8,128)} %param.15) | copy-start | bytes 196612
  0.7 11.2 %copy-start.8 = (s32[128,128]{1,0:T(8,128)S(1)}, s32[128,128]{1,0:T(8,128)}, u32[]{:S(2)}) copy-start(s32[128,128]{1,0:T(8,128)} %param.17) | copy-start | bytes 196612
  0.7 11.1 %copy-start.6 = (f32[128,128]{1,0:T(8,128)S(1)}, f32[128,128]{1,0:T(8,128)}, u32[]{:S(2)}) copy-start(f32[128,128]{1,0:T(8,128)} %param.16) | copy-start | bytes 196612
  0.7 11.2 %copy-start.11 = (f32[4,12]{1,0:T(4,128)S(1)}, f32[4,12]{1,0:T(4,128)}, u32[]{:S(2)}) copy-start(f32[4,12]{1,0:T(4,128)} %param.20) | copy-start | bytes 580
  3.6 0.8 %copy-start.3 = (s32[128,128]{1,0:T(8,128)S(1)}, s32[128,128]{1,0:T(8,128)}, u32[]{:S(2)}) copy-start(s32[128,128]{1,0:T(8,128)} %index_ref.1) | copy-start | bytes 196612
  4.5 10.2 %copy-start.4 = (bf16[128,128,256]{2,1,0:T(8,128)(2,1)S(1)}, bf16[128,128,256]{2,1,0:T(8,128)(2,1)}, u32[]{:S(2)}) copy-start(bf16[128,128,256]{2,1,0:T(8,128)(2,1)} %param.23) | copy-start | bytes 25165828
  14.7 1.6 %copy-start.10 = (s32[128,1]{0,1:T(1,128)S(1)}, s32[128,1]{0,1:T(1,128)}, u32[]{:S(2)}) copy-start(s32[128,1]{0,1:T(1,128)} %param.22) | copy-start | bytes 1540
  14.7 2.7 %copy-start.1 = (f32[15,256]{1,0:T(8,128)S(1)}, f32[15,256]{1,0:T(8,128)}, u32[]{:S(2)}) copy-start(f32[15,256]{1,0:T(8,128)} %coupling_ref.1) | copy-start | bytes 46084
  14.7 2.7 %copy-start.2 = (f32[3,16,256]{2,1,0:T(8,128)S(1)}, f32[3,16,256]{2,1,0:T(8,128)}, u32[]{:S(2)}) copy-start(f32[3,16,256]{2,1,0:T(8,128)} %state_ref.1) | copy-start | bytes 147460
  14.7 16.0 %copy-start.7 = (f32[8,16,256]{2,1,0:T(8,128)S(1)}, f32[8,16,256]{2,1,0:T(8,128)}, u32[]{:S(2)}) copy-start(f32[8,16,256]{2,1,0:T(8,128)} %param.25) | copy-start | bytes 393220
  15.9 29.3 %copy-start.9 = (f32[8]{0:T(128)S(1)}, f32[8]{0:T(128)}, u32[]{:S(2)}) copy-start(f32[8]{0:T(128)} %param.27) | copy-start | bytes 100
  19.1 25.6 %all-to-all-start = ((bf16[128,2,1280]{2,1,0:T(2,128)(2,1)}), bf16[128,2,1280]{2,1,0:T(2,128)(2,1)S(1)}, u32[]{:S(2)}, u32[]{:S(2)}) async-start(bf16[128,2,1280]{2,1,0:T(2,128)(2,1)} %pad_maximum_fusion), calls=%async_computation | async-start | bytes 1310720 | tf_op jit(solution)/shard_map/all_to_all | solution.py:185

commit v14 on v13

--- a/solution.py
+++ b/solution.py
@@ -56,7 +56,7 @@
     second_wide = lax.reduce_precision(rest, exponent_bits=8, mantissa_bits=7)
     parts = jnp.concatenate([first_wide, second_wide, rest - second_wide], axis=0).T.astype(jnp.bfloat16)
     rows, lanes = index.shape
-    step = 32
+    step = 128
     return pl.pallas_call(
         lookup_kernel,
         out_shape=jax.ShapeDtypeStruct((rows, lanes), jnp.float32),

time: 54.5 us -> 54.1 us (level)
  no operation moved by 1% of the time
where the time goes in v14:
time: 54.1 us; the launch traced here: 53.8 us
  waiting for transfers between devices  14 us (26%)
  starting transfers between devices  11.5 us (21%)
  matrix products  10.5 us (19%)
  Pallas kernels  6.92 us (13%)
  other arithmetic  5.88 us (11%)
  local copies, waits for them, and re-layouts  3.93 us (7%)
  between operations  1.11 us (2%)
    all_to_all x1, waiting for transfers between devices, on_device(): lax.all_to_all(payload, ('sec', 'tile'), split_axis=0, concat_axis=0, til...  14 us
    all_to_all x1, starting transfers between devices, on_device(): lax.all_to_all(payload, ('sec', 'tile'), split_axis=0, concat_axis=0, til...  11.5 us
    pallas_call x1, Pallas kernels, lookup(): pl.pallas_call(lookup_kernel, out_shape=jax.ShapeDtypeStruct((rows, lanes...  6.75 us
    dot_general x1, matrix products, on_device(): jnp.einsum('gla,gka->kgl', regrid_w, picked, preferred_element_type=jnp.f...  5.63 us
    unnamed x35, local copies, waits for them, and re-layouts  2.02 us
    dot_general x1, matrix products, emit(): blasted = jnp.einsum('tkb,bnl->tknl', blast_table, salt, precision=high)  1.88 us
    concatenate x1, other arithmetic, on_device(): jnp.concatenate([outgoing.astype(jnp.bfloat16).reshape(devices, 2, half),...  1.43 us
    dot_general x1, matrix products, on_device(): jnp.einsum('gkl,gla->gka', emission, regrid_w, preferred_element_type=jnp...  1.19 us
  transfers between devices with their start and end apart: 1, of which 1 were waited for; matrix products, arithmetic and copies ran while one was open for 0% of the time, Pallas kernels for 0%

profile of v14, /device:TPU:1, one launch (start us, length us, event | category | flops | bytes accessed | tf_op | source)
XLA Modules:
  0.0 53.8 jit_solution(15113284752963159442)
XLA Ops:
  0.7 1.0 %copy.42 = f32[256,128]{0,1:T(8,128)S(1)} copy(f32[256,128]{1,0:T(8,128)} %bitcast.86) | data formatting | bytes 262144 | tf_op jit(solution)/shard_map/reshape | solution.py:53
  1.8 0.9 %mul.1665 = f32[128,128]{1,0:T(8,128)S(1)} multiply(f32[128,128]{1,0:T(8,128)} %param.15, f32[128,128]{1,0:T(8,128)} %param.15) | non-fusion elementwise | flops 16384 | bytes 196608 | tf_op jit(solution)/shard_map/mul | solution.py:26
  2.7 0.9 %fusion.11 = f32[4,128,128]{2,0,1:T(4,128)S(1)} fusion(s32[128,128]{1,0:T(8,128)} %param.17), kind=kLoop, calls=%fused_computation.22 | loop fusion | flops 131072 | bytes 327680 | tf_op jit(solution)/shard_map/convert_element_type | solution.py:18
  3.7 0.8 %copy-done.3 = s32[128,128]{1,0:T(8,128)S(1)} copy-done((s32[128,128]{1,0:T(8,128)S(1)}, s32[128,128]{1,0:T(8,128)}, u32[]{:S(2)}) %copy-start.3) | copy-done | bytes 65560
  4.5 6.7 %shard_map.140 = f32[128,128]{1,0:T(8,128)S(1)} custom-call(s32[128,128]{1,0:T(8,128)S(1)} %copy-done.3, bf16[128,768]{1,0:T(8,128)(2,1)S(1)} %maximum_bitcast_fusion.parts_ref), custom_call_target="tpu_custom_call" | custom-call | flops 3221225472 | bytes 327680 | tf_op jit(solution)/shard_map/pallas_call | solution.py:60
  11.3 0.8 %fusion.4 = f32[12,128,128,1]{2,0,3,1:T(8,128)S(1)} fusion(f32[128,128]{1,0:T(8,128)S(1)} %mul.1665, f32[128,128]{1,0:T(8,128)S(1)} %get-tuple-element.86, f32[12]{0:T(128)S(1)} %multiply_sqrt_fusion, f32[128,128]{1,0:T(8,128)S(1)} %copy-done.5, f32[128,128]{1,0:T(8,128)S(1)} %get-tuple-element.87, s32[128,128]{1,0:T(8,128)S(1)} %copy-done.8, ...), kind=kOutput, calls=%fused_computation.9 | convolution fusion | flops 11075584 | bytes 1114352 | tf_op jit(solution)/shard_map/tb,tnl->bnl/dot_general | solution.py:19
  12.2 1.9 %fusion = bf16[8,128,128]{2,0,1:T(8,128)(2,1)S(1)} fusion(f32[12,128,128,1]{2,0,3,1:T(8,128)S(1)} %fusion.4, f32[4,128,128]{2,0,1:T(4,128)S(1)} %fusion.11, f32[4,8,12]{2,1,0:T(8,128)S(1)} %copy-done), kind=kOutput, calls=%fused_computation.2 | convolution fusion | flops 76414976 | bytes 1312256 | tf_op jit(solution)/shard_map/tkb,bnl->tknl/dot_general | solution.py:28
  14.2 1.2 %fusion.8 = f32[128,8,256]{2,1,0:T(8,128)S(1)} fusion(bf16[128,128,256]{2,1,0:T(8,128)(2,1)S(1)} %copy-done.4, bf16[128,8,128]{2,0,1:T(8,128)(2,1)S(1)} %bitcast.80), kind=kOutput, calls=%fused_computation.18 | convolution fusion | flops 67108864 | bytes 9699328 | tf_op jit(solution)/shard_map/gkl,gla->gka/dot_general | solution.py:172
  15.3 0.3 copy.86
  15.7 0.7 %convolution_convert_fusion = bf16[128,2048]{1,0:T(8,128)(2,1)S(1)} fusion(f32[128,2048]{1,0:T(8,128)S(1)} %bitcast.79, s32[128]{0:T(128)S(1)} %bitcast.206), kind=kOutput, calls=%fused_computation | convolution fusion | flops 402931712 | bytes 1573376 | tf_op jit(solution)/shard_map/dot_general | solution.py:179
  16.4 0.6 %reshape.27137 = bf16[128,2,1024]{2,1,0:T(2,128)(2,1)S(1)} reshape(bf16[128,2048]{1,0:T(8,128)(2,1)S(1)} %convolution_convert_fusion) | data formatting | bytes 1048576 | tf_op jit(solution)/shard_map/reshape | solution.py:183
  17.0 0.2 shard_map.141
  17.3 1.4 %pad_maximum_fusion = bf16[128,2,1280]{2,1,0:T(2,128)(2,1)} fusion(bf16[128,2,256]{2,1,0:T(2,128)(2,1)S(1)} %broadcast_in_dim.2, bf16[128,2,1024]{2,1,0:T(2,128)(2,1)S(1)} %reshape.27137), kind=kLoop, calls=%fused_computation.15 | loop fusion | flops 1310720 | bytes 1310720 | tf_op jit(solution)/shard_map/concatenate | solution.py:182
  18.7 11.5 %all-to-all-start = ((bf16[128,2,1280]{2,1,0:T(2,128)(2,1)}), bf16[128,2,1280]{2,1,0:T(2,128)(2,1)S(1)}, u32[]{:S(2)}, u32[]{:S(2)}) async-start(bf16[128,2,1280]{2,1,0:T(2,128)(2,1)} %pad_maximum_fusion), calls=%async_computation | async-start | bytes 1310720 | tf_op jit(solution)/shard_map/all_to_all | solution.py:185
  30.4 14.0 %all-to-all-done = bf16[128,2,1280]{2,1,0:T(2,128)(2,1)S(1)} async-done(((bf16[128,2,1280]{2,1,0:T(2,128)(2,1)}), bf16[128,2,1280]{2,1,0:T(2,128)(2,1)S(1)}, u32[]{:S(2)}, u32[]{:S(2)}) %all-to-all-start) | async-done | bytes 655392 | tf_op jit(solution)/shard_map/all_to_all | solution.py:185
  44.4 0.5 convert_reduce_fusion
  44.9 0.2 fusion.24
  45.0 0.2 constant_dynamic-update-slice_fusion.15
  45.9 0.1 constant_dynamic-update-slice_fusion.1
  46.1 0.7 %copy.65 = f32[8,16,256]{2,1,0:T(8,128)} copy(f32[8,16,256]{2,0,1:T(8,128)S(1)} %constant_dynamic-update-slice_fusion) | data formatting | bytes 262144
  47.0 0.2 convolution_convert_fusion.1
  47.2 5.6 %convolution_bitcast_fusion = f32[3,128,128]{2,0,1:T(4,128)S(1)} fusion(bf16[128,128,256]{2,1,0:T(8,128)(2,1)} %param.23, bf16[128,2,256]{2,1,0:T(2,128)(2,1)S(1)} %reshape.27139), kind=kOutput, calls=%fused_computation.10 | convolution fusion | flops 25165824 | bytes 8716288 | tf_op jit(solution)/shard_map/gla,gka->kgl/dot_general | solution.py:194
  52.9 0.2 fusion.41
  53.1 0.7 %pad_maximum_fusion.1 = f32[2,128,128]{2,1,0:T(8,128)} fusion(f32[1,128,128]{2,1,0:T(8,128)S(1)} %add_bitcast_fusion, f32[1,128,128]{2,1,0:T(8,128)S(1)} %div.1372), kind=kLoop, calls=%fused_computation.29 | loop fusion | flops 32768 | bytes 262144 | tf_op jit(solution)/shard_map/stack | solution.py:196
  (55 shorter events, 1.3 us)
Async XLA Ops:
  0.6 11.5 %copy-start = (f32[4,8,12]{2,1,0:T(8,128)S(1)}, f32[4,8,12]{2,1,0:T(8,128)}, u32[]{:S(2)}) copy-start(f32[4,8,12]{2,1,0:T(8,128)} %param.21) | copy-start | bytes 4612
  0.6 10.6 %copy-start.5 = (f32[128,128]{1,0:T(8,128)S(1)}, f32[128,128]{1,0:T(8,128)}, u32[]{:S(2)}) copy-start(f32[128,128]{1,0:T(8,128)} %param.15) | copy-start | bytes 196612
  0.7 10.6 %copy-start.8 = (s32[128,128]{1,0:T(8,128)S(1)}, s32[128,128]{1,0:T(8,128)}, u32[]{:S(2)}) copy-start(s32[128,128]{1,0:T(8,128)} %param.17) | copy-start | bytes 196612
  0.7 10.6 %copy-start.6 = (f32[128,128]{1,0:T(8,128)S(1)}, f32[128,128]{1,0:T(8,128)}, u32[]{:S(2)}) copy-start(f32[128,128]{1,0:T(8,128)} %param.16) | copy-start | bytes 196612
  0.7 10.6 %copy-start.11 = (f32[4,12]{1,0:T(4,128)S(1)}, f32[4,12]{1,0:T(4,128)}, u32[]{:S(2)}) copy-start(f32[4,12]{1,0:T(4,128)} %param.20) | copy-start | bytes 580
  3.6 0.8 %copy-start.3 = (s32[128,128]{1,0:T(8,128)S(1)}, s32[128,128]{1,0:T(8,128)}, u32[]{:S(2)}) copy-start(s32[128,128]{1,0:T(8,128)} %index_ref.1) | copy-start | bytes 196612
  4.5 9.6 %copy-start.4 = (bf16[128,128,256]{2,1,0:T(8,128)(2,1)S(1)}, bf16[128,128,256]{2,1,0:T(8,128)(2,1)}, u32[]{:S(2)}) copy-start(bf16[128,128,256]{2,1,0:T(8,128)(2,1)} %param.23) | copy-start | bytes 25165828
  14.1 1.6 %copy-start.10 = (s32[128,1]{0,1:T(1,128)S(1)}, s32[128,1]{0,1:T(1,128)}, u32[]{:S(2)}) copy-start(s32[128,1]{0,1:T(1,128)} %param.22) | copy-start | bytes 1540
  14.1 2.9 %copy-start.1 = (f32[15,256]{1,0:T(8,128)S(1)}, f32[15,256]{1,0:T(8,128)}, u32[]{:S(2)}) copy-start(f32[15,256]{1,0:T(8,128)} %coupling_ref.1) | copy-start | bytes 46084
  14.1 2.9 %copy-start.2 = (f32[3,16,256]{2,1,0:T(8,128)S(1)}, f32[3,16,256]{2,1,0:T(8,128)}, u32[]{:S(2)}) copy-start(f32[3,16,256]{2,1,0:T(8,128)} %state_ref.1) | copy-start | bytes 147460
  14.1 16.2 %copy-start.7 = (f32[8,16,256]{2,1,0:T(8,128)S(1)}, f32[8,16,256]{2,1,0:T(8,128)}, u32[]{:S(2)}) copy-start(f32[8,16,256]{2,1,0:T(8,128)} %param.25) | copy-start | bytes 393220
  15.3 29.5 %copy-start.9 = (f32[8]{0:T(128)S(1)}, f32[8]{0:T(128)}, u32[]{:S(2)}) copy-start(f32[8]{0:T(128)} %param.27) | copy-start | bytes 100
  18.7 25.6 %all-to-all-start = ((bf16[128,2,1280]{2,1,0:T(2,128)(2,1)}), bf16[128,2,1280]{2,1,0:T(2,128)(2,1)S(1)}, u32[]{:S(2)}, u32[]{:S(2)}) async-start(bf16[128,2,1280]{2,1,0:T(2,128)(2,1)} %pad_maximum_fusion), calls=%async_computation | async-start | bytes 1310720 | tf_op jit(solution)/shard_map/all_to_all | solution.py:185

commit v15 on v14

--- a/solution.py
+++ b/solution.py
@@ -11,7 +11,7 @@
     return jnp.sqrt(0.0123 * (2160.0 * 9.81 * diameter + 0.0003 / (1.227 * diameter)))
 
 
-def emit(wind_rows, moist_rows, texture_rows, erodible, mass_frac, blast_table, base_thresh):
+def emit(wind_rows, wind_square, moist_rows, texture_rows, erodible, mass_frac, blast_table, base_thresh):
     high = lax.Precision.HIGHEST
     thresh = base_thresh[:, None, None] * jnp.sqrt(1.0 + 12.1 * moist_rows)[None]
     classes = jnp.arange(mass_frac.shape[0])
@@ -23,20 +23,21 @@
         * fraction
         * erodible[None]
         * (speed + thresh)
-        * jnp.maximum(speed * speed - thresh * thresh, 0.0)
+        * jnp.maximum(wind_square[None] - thresh * thresh, 0.0)
     )
     blasted = jnp.einsum("tkb,bnl->tknl", blast_table, salt, precision=high)
     emission = jnp.sum(blasted * onehot[:, None], axis=0)
     return jnp.transpose(emission, (1, 0, 2)).astype(jnp.bfloat16)
 
 
-def lookup_kernel(index_ref, parts_ref, out_ref):
+def lookup_kernel(index_ref, parts_ref, wind_ref, out_ref, square_ref):
     rows_per_step, lanes = index_ref.shape
     segments = parts_ref.shape[1] // 3
     levels = lax.broadcasted_iota(jnp.int32, (segments, lanes), 0).astype(jnp.bfloat16)
     lane_rows = lax.broadcasted_iota(jnp.int32, (128, lanes), 0)
     one = jnp.ones((segments, lanes), jnp.bfloat16)
     zero = jnp.zeros((segments, lanes), jnp.bfloat16)
+    square_ref[...] = wind_ref[...] * wind_ref[...]
     for r in range(rows_per_step):
         cell = index_ref[r : r + 1, :]
         high_part = (cell // 128).astype(jnp.bfloat16)
@@ -48,7 +49,7 @@
         out_ref[r : r + 1, :] = jnp.sum(jnp.where(pick_lane, row_values, 0.0), axis=0, keepdims=True)
 
 
-def lookup(table, index):
+def lookup(table, index, wind):
     segments = table.shape[0] // 128
     grid = table.reshape(segments, 128)
     first_wide = lax.reduce_precision(grid, exponent_bits=8, mantissa_bits=7)
@@ -59,19 +60,20 @@
     step = 128
     return pl.pallas_call(
         lookup_kernel,
-        out_shape=jax.ShapeDtypeStruct((rows, lanes), jnp.float32),
+        out_shape=(jax.ShapeDtypeStruct((rows, lanes), jnp.float32),) * 2,
         grid=(rows // step,),
         in_specs=[
             pl.BlockSpec((step, lanes), lambda i: (i, 0)),
             pl.BlockSpec((128, 3 * segments), lambda i: (0, 0)),
+            pl.BlockSpec((step, lanes), lambda i: (i, 0)),
         ],
-        out_specs=pl.BlockSpec((step, lanes), lambda i: (i, 0)),
+        out_specs=(pl.BlockSpec((step, lanes), lambda i: (i, 0)),) * 2,
         compiler_params=pltpu.CompilerParams(vmem_limit_bytes=8 * 1024 * 1024),
         cost_estimate=pl.CostEstimate(
             flops=2 * 384 * segments * rows * lanes, transcendentals=0,
             bytes_accessed=8 * rows * lanes + 768 * segments,
         ),
-    )(index, parts)
+    )(index, parts, wind)
 
 def solve(right_side, coupling, sinking):
     levels = right_side.shape[1]
@@ -167,8 +169,8 @@
     devices = lax.axis_size(("sec", "tile"))
     surface = surface_of(atm_state, mixing).astype(jnp.bfloat16).reshape(1, 2 * columns)
     base_thresh = threshold_table(mass_frac.shape[1])
-    erodible = lookup(erod_map, land_index)
-    emission = emit(land_wind, land_moist, texture, erodible, mass_frac, blast_table, base_thresh)
+    erodible, wind_square = lookup(erod_map, land_index, land_wind)
+    emission = emit(land_wind, wind_square, land_moist, texture, erodible, mass_frac, blast_table, base_thresh)
     partial_flux = jnp.einsum(
         "gkl,gla->gka", emission, regrid_w, preferred_element_type=jnp.float32
     )

time: 54.1 us -> 54 us (level)
  other arithmetic: 5.88 us -> 4.96 us
  local copies, waits for them, and re-layouts: 3.93 us -> 4.77 us
    mul x1 -> x0, other arithmetic: 0.93 us -> none  [emit(): speed * speed - thresh * thresh]
    unnamed x35 -> x37, local copies, waits for them, and re-layouts: 2.02 us -> 2.86 us
where the time goes in v15:
time: 54 us; the launch traced here: 53.7 us
  waiting for transfers between devices  14 us (26%)
  starting transfers between devices  11.5 us (21%)
  matrix products  10.5 us (19%)
  Pallas kernels  6.92 us (13%)
  other arithmetic  4.96 us (9%)
  local copies, waits for them, and re-layouts  4.77 us (9%)
  between operations  1.11 us (2%)
    all_to_all x1, waiting for transfers between devices, on_device(): lax.all_to_all(payload, ('sec', 'tile'), split_axis=0, concat_axis=0, til...  14 us
    all_to_all x1, starting transfers between devices, on_device(): lax.all_to_all(payload, ('sec', 'tile'), split_axis=0, concat_axis=0, til...  11.5 us
    pallas_call x1, Pallas kernels, lookup(): pl.pallas_call(lookup_kernel, out_shape=(jax.ShapeDtypeStruct((rows, lane...  6.75 us
    dot_general x1, matrix products, on_device(): jnp.einsum('gla,gka->kgl', regrid_w, picked, preferred_element_type=jnp.f...  5.63 us
    unnamed x37, local copies, waits for them, and re-layouts  2.86 us
    dot_general x1, matrix products, emit(): blasted = jnp.einsum('tkb,bnl->tknl', blast_table, salt, precision=high)  1.88 us
    concatenate x1, other arithmetic, on_device(): jnp.concatenate([outgoing.astype(jnp.bfloat16).reshape(devices, 2, half),...  1.44 us
    dot_general x1, matrix products, on_device(): jnp.einsum('gkl,gla->gka', emission, regrid_w, preferred_element_type=jnp...  1.19 us
  transfers between devices with their start and end apart: 1, of which 1 were waited for; matrix products, arithmetic and copies ran while one was open for 0% of the time, Pallas kernels for 0%

profile of v15, /device:TPU:1, one launch (start us, length us, event | category | flops | bytes accessed | tf_op | source)
XLA Modules:
  0.0 53.7 jit_solution(12859414924004432522)
XLA Ops:
  0.7 1.0 %copy.42 = f32[256,128]{0,1:T(8,128)S(1)} copy(f32[256,128]{1,0:T(8,128)} %bitcast.86) | data formatting | bytes 262144 | tf_op jit(solution)/shard_map/reshape | solution.py:54
  1.8 0.9 %fusion.11 = f32[4,128,128]{2,0,1:T(4,128)S(1)} fusion(s32[128,128]{1,0:T(8,128)} %param.17), kind=kLoop, calls=%fused_computation.22 | loop fusion | flops 131072 | bytes 327680 | tf_op jit(solution)/shard_map/convert_element_type | solution.py:18
  2.7 0.8 %copy-done.3 = s32[128,128]{1,0:T(8,128)S(1)} copy-done((s32[128,128]{1,0:T(8,128)S(1)}, s32[128,128]{1,0:T(8,128)}, u32[]{:S(2)}) %copy-start.3) | copy-done | bytes 65560
  3.6 0.8 %copy-done.4 = f32[128,128]{1,0:T(8,128)S(1)} copy-done((f32[128,128]{1,0:T(8,128)S(1)}, f32[128,128]{1,0:T(8,128)}, u32[]{:S(2)}) %copy-start.4) | copy-done | bytes 65560
  4.4 6.7 %shard_map.140 = (f32[128,128]{1,0:T(8,128)S(1)}, f32[128,128]{1,0:T(8,128)S(1)}) custom-call(s32[128,128]{1,0:T(8,128)S(1)} %copy-done.3, bf16[128,768]{1,0:T(8,128)(2,1)S(1)} %maximum_bitcast_fusion.parts_ref, f32[128,128]{1,0:T(8,128)S(1)} %copy-done.4), custom_call_target="tpu_custom_call" | custom-call | flops 3221225472 | bytes 327680 | tf_op jit(solution)/shard_map/pallas_call | solution.py:61
  11.2 0.8 %fusion.4 = f32[12,128,128,1]{2,0,3,1:T(8,128)S(1)} fusion(f32[128,128]{1,0:T(8,128)S(1)} %get-tuple-element.17, f32[128,128]{1,0:T(8,128)S(1)} %get-tuple-element.90, f32[12]{0:T(128)S(1)} %multiply_sqrt_fusion, f32[128,128]{1,0:T(8,128)S(1)} %copy-done.5, f32[128,128]{1,0:T(8,128)S(1)} %get-tuple-element.91, s32[128,128]{1,0:T(8,128)S(1)} %copy-done.9, ...), kind=kOutput, calls=%fused_computation.9 | convolution fusion | flops 11075584 | bytes 1114352 | tf_op jit(solution)/shard_map/tb,tnl->bnl/dot_general | solution.py:19
  12.1 1.9 %fusion = bf16[8,128,128]{2,0,1:T(8,128)(2,1)S(1)} fusion(f32[12,128,128,1]{2,0,3,1:T(8,128)S(1)} %fusion.4, f32[4,128,128]{2,0,1:T(4,128)S(1)} %fusion.11, f32[4,8,12]{2,1,0:T(8,128)S(1)} %copy-done), kind=kOutput, calls=%fused_computation.2 | convolution fusion | flops 76414976 | bytes 1312256 | tf_op jit(solution)/shard_map/tkb,bnl->tknl/dot_general | solution.py:28
  14.1 1.2 %fusion.8 = f32[128,8,256]{2,1,0:T(8,128)S(1)} fusion(bf16[128,128,256]{2,1,0:T(8,128)(2,1)S(1)} %copy-done.6, bf16[128,8,128]{2,0,1:T(8,128)(2,1)S(1)} %bitcast.80), kind=kOutput, calls=%fused_computation.18 | convolution fusion | flops 67108864 | bytes 9699328 | tf_op jit(solution)/shard_map/gkl,gla->gka/dot_general | solution.py:174
  15.3 0.3 copy.86
  15.6 0.7 %convolution_convert_fusion = bf16[128,2048]{1,0:T(8,128)(2,1)S(1)} fusion(f32[128,2048]{1,0:T(8,128)S(1)} %bitcast.79, s32[128]{0:T(128)S(1)} %bitcast.206), kind=kOutput, calls=%fused_computation | convolution fusion | flops 402931712 | bytes 1573376 | tf_op jit(solution)/shard_map/dot_general | solution.py:181
  16.3 0.6 %reshape.27136 = bf16[128,2,1024]{2,1,0:T(2,128)(2,1)S(1)} reshape(bf16[128,2048]{1,0:T(8,128)(2,1)S(1)} %convolution_convert_fusion) | data formatting | bytes 1048576 | tf_op jit(solution)/shard_map/reshape | solution.py:185
  16.9 0.2 shard_map.141
  17.2 1.4 %pad_maximum_fusion = bf16[128,2,1280]{2,1,0:T(2,128)(2,1)} fusion(bf16[128,2,256]{2,1,0:T(2,128)(2,1)S(1)} %broadcast_in_dim.2, bf16[128,2,1024]{2,1,0:T(2,128)(2,1)S(1)} %reshape.27136), kind=kLoop, calls=%fused_computation.15 | loop fusion | flops 1310720 | bytes 1310720 | tf_op jit(solution)/shard_map/concatenate | solution.py:184
  18.6 11.5 %all-to-all-start = ((bf16[128,2,1280]{2,1,0:T(2,128)(2,1)}), bf16[128,2,1280]{2,1,0:T(2,128)(2,1)S(1)}, u32[]{:S(2)}, u32[]{:S(2)}) async-start(bf16[128,2,1280]{2,1,0:T(2,128)(2,1)} %pad_maximum_fusion), calls=%async_computation | async-start | bytes 1310720 | tf_op jit(solution)/shard_map/all_to_all | solution.py:187
  30.3 14.0 %all-to-all-done = bf16[128,2,1280]{2,1,0:T(2,128)(2,1)S(1)} async-done(((bf16[128,2,1280]{2,1,0:T(2,128)(2,1)}), bf16[128,2,1280]{2,1,0:T(2,128)(2,1)S(1)}, u32[]{:S(2)}, u32[]{:S(2)}) %all-to-all-start) | async-done | bytes 655392 | tf_op jit(solution)/shard_map/all_to_all | solution.py:187
  44.3 0.5 convert_reduce_fusion
  44.8 0.2 fusion.24
  45.0 0.2 constant_dynamic-update-slice_fusion.15
  45.8 0.1 constant_dynamic-update-slice_fusion.1
  46.1 0.7 %copy.65 = f32[8,16,256]{2,1,0:T(8,128)} copy(f32[8,16,256]{2,0,1:T(8,128)S(1)} %constant_dynamic-update-slice_fusion) | data formatting | bytes 262144
  46.9 0.2 convolution_convert_fusion.1
  47.2 5.6 %convolution_bitcast_fusion = f32[3,128,128]{2,0,1:T(4,128)S(1)} fusion(bf16[128,128,256]{2,1,0:T(8,128)(2,1)} %param.23, bf16[128,2,256]{2,1,0:T(2,128)(2,1)S(1)} %reshape.27138), kind=kOutput, calls=%fused_computation.10 | convolution fusion | flops 25165824 | bytes 8716288 | tf_op jit(solution)/shard_map/gla,gka->kgl/dot_general | solution.py:196
  52.8 0.2 fusion.41
  53.0 0.7 %pad_maximum_fusion.1 = f32[2,128,128]{2,1,0:T(8,128)} fusion(f32[1,128,128]{2,1,0:T(8,128)S(1)} %add_bitcast_fusion, f32[1,128,128]{2,1,0:T(8,128)S(1)} %div.1372), kind=kLoop, calls=%fused_computation.29 | loop fusion | flops 32768 | bytes 262144 | tf_op jit(solution)/shard_map/stack | solution.py:198
  (56 shorter events, 1.3 us)
Async XLA Ops:
  0.6 11.4 %copy-start = (f32[4,8,12]{2,1,0:T(8,128)S(1)}, f32[4,8,12]{2,1,0:T(8,128)}, u32[]{:S(2)}) copy-start(f32[4,8,12]{2,1,0:T(8,128)} %param.21) | copy-start | bytes 4612
  0.6 10.6 %copy-start.9 = (s32[128,128]{1,0:T(8,128)S(1)}, s32[128,128]{1,0:T(8,128)}, u32[]{:S(2)}) copy-start(s32[128,128]{1,0:T(8,128)} %param.17) | copy-start | bytes 196612
  0.7 10.6 %copy-start.5 = (f32[128,128]{1,0:T(8,128)S(1)}, f32[128,128]{1,0:T(8,128)}, u32[]{:S(2)}) copy-start(f32[128,128]{1,0:T(8,128)} %wind_ref.1) | copy-start | bytes 196612
  0.7 10.5 %copy-start.7 = (f32[128,128]{1,0:T(8,128)S(1)}, f32[128,128]{1,0:T(8,128)}, u32[]{:S(2)}) copy-start(f32[128,128]{1,0:T(8,128)} %param.16) | copy-start | bytes 196612
  0.7 10.5 %copy-start.12 = (f32[4,12]{1,0:T(4,128)S(1)}, f32[4,12]{1,0:T(4,128)}, u32[]{:S(2)}) copy-start(f32[4,12]{1,0:T(4,128)} %param.20) | copy-start | bytes 580
  2.7 0.8 %copy-start.3 = (s32[128,128]{1,0:T(8,128)S(1)}, s32[128,128]{1,0:T(8,128)}, u32[]{:S(2)}) copy-start(s32[128,128]{1,0:T(8,128)} %index_ref.1) | copy-start | bytes 196612
  3.6 0.8 %copy-start.4 = (f32[128,128]{1,0:T(8,128)S(1)}, f32[128,128]{1,0:T(8,128)}, u32[]{:S(2)}) copy-start(f32[128,128]{1,0:T(8,128)} %wind_ref.1) | copy-start | bytes 196612
  4.4 9.6 %copy-start.6 = (bf16[128,128,256]{2,1,0:T(8,128)(2,1)S(1)}, bf16[128,128,256]{2,1,0:T(8,128)(2,1)}, u32[]{:S(2)}) copy-start(bf16[128,128,256]{2,1,0:T(8,128)(2,1)} %param.23) | copy-start | bytes 25165828
  14.0 1.6 %copy-start.11 = (s32[128,1]{0,1:T(1,128)S(1)}, s32[128,1]{0,1:T(1,128)}, u32[]{:S(2)}) copy-start(s32[128,1]{0,1:T(1,128)} %param.22) | copy-start | bytes 1540
  14.0 2.9 %copy-start.1 = (f32[15,256]{1,0:T(8,128)S(1)}, f32[15,256]{1,0:T(8,128)}, u32[]{:S(2)}) copy-start(f32[15,256]{1,0:T(8,128)} %coupling_ref.1) | copy-start | bytes 46084
  14.0 2.9 %copy-start.2 = (f32[3,16,256]{2,1,0:T(8,128)S(1)}, f32[3,16,256]{2,1,0:T(8,128)}, u32[]{:S(2)}) copy-start(f32[3,16,256]{2,1,0:T(8,128)} %state_ref.1) | copy-start | bytes 147460
  14.1 16.2 %copy-start.8 = (f32[8,16,256]{2,1,0:T(8,128)S(1)}, f32[8,16,256]{2,1,0:T(8,128)}, u32[]{:S(2)}) copy-start(f32[8,16,256]{2,1,0:T(8,128)} %param.25) | copy-start | bytes 393220
  15.3 29.5 %copy-start.10 = (f32[8]{0:T(128)S(1)}, f32[8]{0:T(128)}, u32[]{:S(2)}) copy-start(f32[8]{0:T(128)} %param.27) | copy-start | bytes 100
  18.6 25.6 %all-to-all-start = ((bf16[128,2,1280]{2,1,0:T(2,128)(2,1)}), bf16[128,2,1280]{2,1,0:T(2,128)(2,1)S(1)}, u32[]{:S(2)}, u32[]{:S(2)}) async-start(bf16[128,2,1280]{2,1,0:T(2,128)(2,1)} %pad_maximum_fusion), calls=%async_computation | async-start | bytes 1310720 | tf_op jit(solution)/shard_map/all_to_all | solution.py:187

commit v16 on v15

--- a/solution.py
+++ b/solution.py
@@ -11,11 +11,10 @@
     return jnp.sqrt(0.0123 * (2160.0 * 9.81 * diameter + 0.0003 / (1.227 * diameter)))
 
 
-def emit(wind_rows, wind_square, moist_rows, texture_rows, erodible, mass_frac, blast_table, base_thresh):
+def emit(wind_rows, wind_square, moist_rows, onehot, erodible, mass_frac, blast_table, base_thresh):
     high = lax.Precision.HIGHEST
     thresh = base_thresh[:, None, None] * jnp.sqrt(1.0 + 12.1 * moist_rows)[None]
     classes = jnp.arange(mass_frac.shape[0])
-    onehot = (texture_rows[None] == classes[:, None, None]).astype(jnp.float32)
     fraction = jnp.einsum("tb,tnl->bnl", mass_frac, onehot, precision=high)
     speed = wind_rows[None]
     salt = (
@@ -30,7 +29,7 @@
     return jnp.transpose(emission, (1, 0, 2)).astype(jnp.bfloat16)
 
 
-def lookup_kernel(index_ref, parts_ref, wind_ref, out_ref, square_ref):
+def lookup_kernel(index_ref, parts_ref, wind_ref, texture_ref, out_ref, square_ref, classes_ref):
     rows_per_step, lanes = index_ref.shape
     segments = parts_ref.shape[1] // 3
     levels = lax.broadcasted_iota(jnp.int32, (segments, lanes), 0).astype(jnp.bfloat16)
@@ -38,6 +37,8 @@
     one = jnp.ones((segments, lanes), jnp.bfloat16)
     zero = jnp.zeros((segments, lanes), jnp.bfloat16)
     square_ref[...] = wind_ref[...] * wind_ref[...]
+    for t in range(classes_ref.shape[0]):
+        classes_ref[t] = jnp.where(texture_ref[...] == t, 1.0, 0.0)
     for r in range(rows_per_step):
         cell = index_ref[r : r + 1, :]
         high_part = (cell // 128).astype(jnp.bfloat16)
@@ -49,7 +50,7 @@
         out_ref[r : r + 1, :] = jnp.sum(jnp.where(pick_lane, row_values, 0.0), axis=0, keepdims=True)
 
 
-def lookup(table, index, wind):
+def lookup(table, index, wind, texture, classes):
     segments = table.shape[0] // 128
     grid = table.reshape(segments, 128)
     first_wide = lax.reduce_precision(grid, exponent_bits=8, mantissa_bits=7)
@@ -60,20 +61,23 @@
     step = 128
     return pl.pallas_call(
         lookup_kernel,
-        out_shape=(jax.ShapeDtypeStruct((rows, lanes), jnp.float32),) * 2,
+        out_shape=(jax.ShapeDtypeStruct((rows, lanes), jnp.float32),) * 2
+        + (jax.ShapeDtypeStruct((classes, rows, lanes), jnp.float32),),
         grid=(rows // step,),
         in_specs=[
             pl.BlockSpec((step, lanes), lambda i: (i, 0)),
             pl.BlockSpec((128, 3 * segments), lambda i: (0, 0)),
             pl.BlockSpec((step, lanes), lambda i: (i, 0)),
+            pl.BlockSpec((step, lanes), lambda i: (i, 0)),
         ],
-        out_specs=(pl.BlockSpec((step, lanes), lambda i: (i, 0)),) * 2,
+        out_specs=(pl.BlockSpec((step, lanes), lambda i: (i, 0)),) * 2
+        + (pl.BlockSpec((classes, step, lanes), lambda i: (0, i, 0)),),
         compiler_params=pltpu.CompilerParams(vmem_limit_bytes=8 * 1024 * 1024),
         cost_estimate=pl.CostEstimate(
             flops=2 * 384 * segments * rows * lanes, transcendentals=0,
             bytes_accessed=8 * rows * lanes + 768 * segments,
         ),
-    )(index, parts, wind)
+    )(index, parts, wind, texture)
 
 def solve(right_side, coupling, sinking):
     levels = right_side.shape[1]
@@ -169,8 +173,8 @@
     devices = lax.axis_size(("sec", "tile"))
     surface = surface_of(atm_state, mixing).astype(jnp.bfloat16).reshape(1, 2 * columns)
     base_thresh = threshold_table(mass_frac.shape[1])
-    erodible, wind_square = lookup(erod_map, land_index, land_wind)
-    emission = emit(land_wind, wind_square, land_moist, texture, erodible, mass_frac, blast_table, base_thresh)
+    erodible, wind_square, texture_onehot = lookup(erod_map, land_index, land_wind, texture, mass_frac.shape[0])
+    emission = emit(land_wind, wind_square, land_moist, texture_onehot, erodible, mass_frac, blast_table, base_thresh)
     partial_flux = jnp.einsum(
         "gkl,gla->gka", emission, regrid_w, preferred_element_type=jnp.float32
     )

time: 54 us -> 54.6 us (1.011)
  other arithmetic: 4.96 us -> 4.06 us
  local copies, waits for them, and re-layouts: 4.77 us -> 5.6 us
  matrix products: 10.5 us -> 11.1 us
    convert_element_type x1 -> x0, other arithmetic: 0.9 us -> none  [emit(): onehot = (texture_rows[None] == classes[:, None, None]).astype(jnp.float32)]
    unnamed x37, local copies, waits for them, and re-layouts: 2.86 us -> 3.69 us
where the time goes in v16:
time: 54.6 us; the launch traced here: 54.3 us
  waiting for transfers between devices  14 us (26%)
  starting transfers between devices  11.5 us (21%)
  matrix products  11.1 us (20%)
  Pallas kernels  6.94 us (13%)
  local copies, waits for them, and re-layouts  5.6 us (10%)
  other arithmetic  4.06 us (7%)
  between operations  1.1 us (2%)
    all_to_all x1, waiting for transfers between devices, on_device(): lax.all_to_all(payload, ('sec', 'tile'), split_axis=0, concat_axis=0, til...  14 us
    all_to_all x1, starting transfers between devices, on_device(): lax.all_to_all(payload, ('sec', 'tile'), split_axis=0, concat_axis=0, til...  11.5 us
    pallas_call x1, Pallas kernels, lookup(): pl.pallas_call(lookup_kernel, out_shape=(jax.ShapeDtypeStruct((rows, lane...  6.77 us
    dot_general x1, matrix products, on_device(): jnp.einsum('gla,gka->kgl', regrid_w, picked, preferred_element_type=jnp.f...  5.63 us
    unnamed x37, local copies, waits for them, and re-layouts  3.69 us
    dot_general x1, matrix products, emit(): blasted = jnp.einsum('tkb,bnl->tknl', blast_table, salt, precision=high)  1.88 us
    concatenate x1, other arithmetic, on_device(): jnp.concatenate([outgoing.astype(jnp.bfloat16).reshape(devices, 2, half),...  1.44 us
    dot_general x1, matrix products, emit(): fraction = jnp.einsum('tb,tnl->bnl', mass_frac, onehot, precision=high)  1.26 us
  transfers between devices with their start and end apart: 1, of which 1 were waited for; matrix products, arithmetic and copies ran while one was open for 0% of the time, Pallas kernels for 0%

profile of v16, /device:TPU:1, one launch (start us, length us, event | category | flops | bytes accessed | tf_op | source)
XLA Modules:
  0.0 54.3 jit_solution(1871310673633533082)
XLA Ops:
  0.7 1.0 %copy.42 = f32[256,128]{0,1:T(8,128)S(1)} copy(f32[256,128]{1,0:T(8,128)} %bitcast.86) | data formatting | bytes 262144 | tf_op jit(solution)/shard_map/reshape | solution.py:55
  1.8 0.8 %copy-done.3 = s32[128,128]{1,0:T(8,128)S(1)} copy-done((s32[128,128]{1,0:T(8,128)S(1)}, s32[128,128]{1,0:T(8,128)}, u32[]{:S(2)}) %copy-start.3) | copy-done | bytes 65560
  2.6 0.8 %copy-done.4 = s32[128,128]{1,0:T(8,128)S(1)} copy-done((s32[128,128]{1,0:T(8,128)S(1)}, s32[128,128]{1,0:T(8,128)}, u32[]{:S(2)}) %copy-start.4) | copy-done | bytes 65560
  3.5 0.8 %copy-done.5 = f32[128,128]{1,0:T(8,128)S(1)} copy-done((f32[128,128]{1,0:T(8,128)S(1)}, f32[128,128]{1,0:T(8,128)}, u32[]{:S(2)}) %copy-start.5) | copy-done | bytes 65560
  4.3 6.8 %shard_map.140 = (f32[128,128]{1,0:T(8,128)S(1)}, f32[128,128]{1,0:T(8,128)S(1)}, f32[4,128,128]{2,1,0:T(8,128)S(1)}) custom-call(s32[128,128]{1,0:T(8,128)S(1)} %copy-done.3, bf16[128,768]{1,0:T(8,128)(2,1)S(1)} %maximum_bitcast_fusion.parts_ref, f32[128,128]{1,0:T(8,128)S(1)} %copy-done.5, s32[128,128]{1,0:T(8,128)S(1)} %copy-done.4), custom_call_target="tpu_custom_call" | custom-call | flops 3221225472 | bytes 327680 | tf_op jit(solution)/shard_map/pallas_call | solution.py:62
  11.1 0.2 copy.44
  11.3 1.3 %fusion.4 = f32[12,128,128,1]{2,0,3,1:T(8,128)S(1)} fusion(f32[128,128]{1,0:T(8,128)S(1)} %get-tuple-element.19, f32[128,128]{1,0:T(8,128)S(1)} %get-tuple-element.92, f32[12]{0:T(128)S(1)} %multiply_sqrt_fusion, f32[128,128]{1,0:T(8,128)S(1)} %copy-done.6, f32[128,128]{1,0:T(8,128)S(1)} %get-tuple-element.93, f32[4,12]{1,0:T(4,128)S(1)} %copy-done.12, ...), kind=kOutput, calls=%fused_computation.9 | convolution fusion | flops 11010048 | bytes 1310960 | tf_op jit(solution)/shard_map/tb,tnl->bnl/dot_general | solution.py:18
  12.6 1.9 %fusion = bf16[8,128,128]{2,0,1:T(8,128)(2,1)S(1)} fusion(f32[12,128,128,1]{2,0,3,1:T(8,128)S(1)} %fusion.4, f32[4,128,128]{2,0,1:T(4,128)S(1)} %copy.44, f32[4,8,12]{2,1,0:T(8,128)S(1)} %copy-done), kind=kOutput, calls=%fused_computation.2 | convolution fusion | flops 76414976 | bytes 1312256 | tf_op jit(solution)/shard_map/tkb,bnl->tknl/dot_general | solution.py:27
  14.6 1.2 %fusion.8 = f32[128,8,256]{2,1,0:T(8,128)S(1)} fusion(bf16[128,128,256]{2,1,0:T(8,128)(2,1)S(1)} %copy-done.7, bf16[128,8,128]{2,0,1:T(8,128)(2,1)S(1)} %bitcast.80), kind=kOutput, calls=%fused_computation.18 | convolution fusion | flops 67108864 | bytes 9699328 | tf_op jit(solution)/shard_map/gkl,gla->gka/dot_general | solution.py:178
  15.8 0.3 copy.88
  16.2 0.9 %convolution_convert_fusion = bf16[128,2048]{1,0:T(8,128)(2,1)S(1)} fusion(f32[128,2048]{1,0:T(8,128)S(1)} %bitcast.79, s32[128]{0:T(128)S(1)} %bitcast.206), kind=kOutput, calls=%fused_computation | convolution fusion | flops 402931712 | bytes 1573376 | tf_op jit(solution)/shard_map/dot_general | solution.py:185
  17.1 0.4 reshape.27132
  17.5 0.2 shard_map.141
  17.8 1.4 %pad_maximum_fusion = bf16[128,2,1280]{2,1,0:T(2,128)(2,1)} fusion(bf16[128,2,256]{2,1,0:T(2,128)(2,1)S(1)} %broadcast_in_dim.2, bf16[128,2,1024]{2,1,0:T(2,128)(2,1)S(1)} %reshape.27132), kind=kLoop, calls=%fused_computation.15 | loop fusion | flops 1310720 | bytes 1310720 | tf_op jit(solution)/shard_map/concatenate | solution.py:188
  19.2 11.5 %all-to-all-start = ((bf16[128,2,1280]{2,1,0:T(2,128)(2,1)}), bf16[128,2,1280]{2,1,0:T(2,128)(2,1)S(1)}, u32[]{:S(2)}, u32[]{:S(2)}) async-start(bf16[128,2,1280]{2,1,0:T(2,128)(2,1)} %pad_maximum_fusion), calls=%async_computation | async-start | bytes 1310720 | tf_op jit(solution)/shard_map/all_to_all | solution.py:191
  30.9 14.0 %all-to-all-done = bf16[128,2,1280]{2,1,0:T(2,128)(2,1)S(1)} async-done(((bf16[128,2,1280]{2,1,0:T(2,128)(2,1)}), bf16[128,2,1280]{2,1,0:T(2,128)(2,1)S(1)}, u32[]{:S(2)}, u32[]{:S(2)}) %all-to-all-start) | async-done | bytes 655392 | tf_op jit(solution)/shard_map/all_to_all | solution.py:191
  44.9 0.5 convert_reduce_fusion
  45.4 0.2 fusion.22
  45.5 0.2 constant_dynamic-update-slice_fusion.15
  46.6 0.7 %copy.67 = f32[8,16,256]{2,1,0:T(8,128)} copy(f32[8,16,256]{2,0,1:T(8,128)S(1)} %constant_dynamic-update-slice_fusion) | data formatting | bytes 262144
  47.5 0.2 convolution_convert_fusion.1
  47.7 5.6 %convolution_bitcast_fusion = f32[3,128,128]{2,0,1:T(4,128)S(1)} fusion(bf16[128,128,256]{2,1,0:T(8,128)(2,1)} %param.23, bf16[128,2,256]{2,1,0:T(2,128)(2,1)S(1)} %reshape.27134), kind=kOutput, calls=%fused_computation.10 | convolution fusion | flops 25165824 | bytes 8716288 | tf_op jit(solution)/shard_map/gla,gka->kgl/dot_general | solution.py:200
  53.4 0.2 fusion.40
  53.6 0.7 %pad_maximum_fusion.1 = f32[2,128,128]{2,1,0:T(8,128)} fusion(f32[1,128,128]{2,1,0:T(8,128)S(1)} %add_bitcast_fusion, f32[1,128,128]{2,1,0:T(8,128)S(1)} %div.1372), kind=kLoop, calls=%fused_computation.27 | loop fusion | flops 32768 | bytes 262144 | tf_op jit(solution)/shard_map/stack | solution.py:202
  (56 shorter events, 1.4 us)
Async XLA Ops:
  0.6 12.0 %copy-start = (f32[4,8,12]{2,1,0:T(8,128)S(1)}, f32[4,8,12]{2,1,0:T(8,128)}, u32[]{:S(2)}) copy-start(f32[4,8,12]{2,1,0:T(8,128)} %param.21) | copy-start | bytes 4612
  0.6 10.7 %copy-start.6 = (f32[128,128]{1,0:T(8,128)S(1)}, f32[128,128]{1,0:T(8,128)}, u32[]{:S(2)}) copy-start(f32[128,128]{1,0:T(8,128)} %wind_ref.1) | copy-start | bytes 196612
  0.7 10.6 %copy-start.8 = (f32[128,128]{1,0:T(8,128)S(1)}, f32[128,128]{1,0:T(8,128)}, u32[]{:S(2)}) copy-start(f32[128,128]{1,0:T(8,128)} %param.16) | copy-start | bytes 196612
  0.7 10.7 %copy-start.12 = (f32[4,12]{1,0:T(4,128)S(1)}, f32[4,12]{1,0:T(4,128)}, u32[]{:S(2)}) copy-start(f32[4,12]{1,0:T(4,128)} %param.20) | copy-start | bytes 580
  1.8 0.8 %copy-start.3 = (s32[128,128]{1,0:T(8,128)S(1)}, s32[128,128]{1,0:T(8,128)}, u32[]{:S(2)}) copy-start(s32[128,128]{1,0:T(8,128)} %index_ref.1) | copy-start | bytes 196612
  2.6 0.8 %copy-start.4 = (s32[128,128]{1,0:T(8,128)S(1)}, s32[128,128]{1,0:T(8,128)}, u32[]{:S(2)}) copy-start(s32[128,128]{1,0:T(8,128)} %texture_ref.1) | copy-start | bytes 196612
  3.5 0.8 %copy-start.5 = (f32[128,128]{1,0:T(8,128)S(1)}, f32[128,128]{1,0:T(8,128)}, u32[]{:S(2)}) copy-start(f32[128,128]{1,0:T(8,128)} %wind_ref.1) | copy-start | bytes 196612
  4.3 10.2 %copy-start.7 = (bf16[128,128,256]{2,1,0:T(8,128)(2,1)S(1)}, bf16[128,128,256]{2,1,0:T(8,128)(2,1)}, u32[]{:S(2)}) copy-start(bf16[128,128,256]{2,1,0:T(8,128)(2,1)} %param.23) | copy-start | bytes 25165828
  14.6 1.6 %copy-start.11 = (s32[128,1]{0,1:T(1,128)S(1)}, s32[128,1]{0,1:T(1,128)}, u32[]{:S(2)}) copy-start(s32[128,1]{0,1:T(1,128)} %param.22) | copy-start | bytes 1540
  14.6 2.9 %copy-start.1 = (f32[15,256]{1,0:T(8,128)S(1)}, f32[15,256]{1,0:T(8,128)}, u32[]{:S(2)}) copy-start(f32[15,256]{1,0:T(8,128)} %coupling_ref.1) | copy-start | bytes 46084
  14.6 2.9 %copy-start.2 = (f32[3,16,256]{2,1,0:T(8,128)S(1)}, f32[3,16,256]{2,1,0:T(8,128)}, u32[]{:S(2)}) copy-start(f32[3,16,256]{2,1,0:T(8,128)} %state_ref.1) | copy-start | bytes 147460
  14.6 16.2 %copy-start.9 = (f32[8,16,256]{2,1,0:T(8,128)S(1)}, f32[8,16,256]{2,1,0:T(8,128)}, u32[]{:S(2)}) copy-start(f32[8,16,256]{2,1,0:T(8,128)} %param.25) | copy-start | bytes 393220
  15.8 29.5 %copy-start.10 = (f32[8]{0:T(128)S(1)}, f32[8]{0:T(128)}, u32[]{:S(2)}) copy-start(f32[8]{0:T(128)} %param.27) | copy-start | bytes 100
  19.2 25.6 %all-to-all-start = ((bf16[128,2,1280]{2,1,0:T(2,128)(2,1)}), bf16[128,2,1280]{2,1,0:T(2,128)(2,1)S(1)}, u32[]{:S(2)}, u32[]{:S(2)}) async-start(bf16[128,2,1280]{2,1,0:T(2,128)(2,1)} %pad_maximum_fusion), calls=%async_computation | async-start | bytes 1310720 | tf_op jit(solution)/shard_map/all_to_all | solution.py:191
